TPU v7x, 512 devices: a whole 4x8x8 slice. The times are simulated.
512 devices in a mesh: space: 64 (over z_lo, y, core), chan: 8 (over x, z_hi).
Axes of the slice: x: 4, y: 8, z: 8 (z_hi: 2, z_lo: 4; z = z_hi * 4 + z_lo), core: 2. Of those that a mesh axis runs over, the one named last changes fastest.
Arguments:
- features: bfloat16 [1, 128, 128, 2048], P(None, 'chan', 'space'), may hold values from -6 to 6
- top_map: int32 [64, 2048], P('space'), may hold values from 0 to 2048, as said below
- bottom_map: int32 [64, 2048], P('space'), may hold values from 0 to 2048, as said below
- first_weight: bfloat16 [128, 3, 3, 128], P('chan'), may hold values from -0.1875 to 0.1875
- first_bias: float32 [128], P('chan'), may hold values from -3 to 3
- second_weight: bfloat16 [256, 3, 3, 128], P('chan'), may hold values from -0.1875 to 0.1875
- second_bias: float32 [256], P('chan'), may hold values from -3 to 3
Outputs:
- hidden: bfloat16 [1, 128, 128, 2048], P(None, 'chan', 'space')
- coarse: bfloat16 [1, 256, 64, 1024], P(None, 'chan', 'space')
Inputs may be any that keep to these rules, and one draw needn't show every extreme that they name: `top_map`: each entry of row s, column k is k - 1, k or k + 1 taken modulo 2048, or 2048 for a missing neighbour at a face corner; exactly 4 entries of each row equal 2048. `bottom_map`: each entry of row s, column k is k - 1, k or k + 1 taken modulo 2048, or 2048 for a missing neighbour at a face corner; exactly 4 entries of each row equal 2048.
All inputs are finite; a program needn't handle non-finite values.
Results may differ from a plain program's by a relative error of at most 0.012.
Values may be sent and summed in bfloat16 or wider, within the bound.
No kernel may reach another device: no remote copies, remote signals or barrier semaphores. Data moves between devices by JAX's collectives and lax.ppermute only.
A program may use at most 64 MiB of HBM per device.

v0:
```python
import jax
import jax.numpy as jnp
from jax import lax
from jax.sharding import PartitionSpec as P


def with_halo(cells, sides, width):
    for axis, dim in sides:
        count = lax.axis_size(axis)
        ends = count - 1
        head = lax.slice_in_dim(cells, 0, width, axis=dim)
        tail = lax.slice_in_dim(cells, cells.shape[dim] - width, cells.shape[dim], axis=dim)
        cells = jnp.concatenate(
            [
                lax.ppermute(tail, axis, [(i, (i + 1) % count) for i in range(ends)]),
                cells,
                lax.ppermute(head, axis, [((i + 1) % count, i) for i in range(ends)]),
            ],
            axis=dim,
        )
    return cells


def shifted_2(array, axis, by):
    devices = lax.axis_size(axis)
    pairs = [(i, i + by) for i in range(devices) if 0 <= i + by < devices]
    return lax.ppermute(array, axis, pairs)


def remap_row(source_row, table):
    zero_col = jnp.zeros(source_row.shape[:-1] + (1,), source_row.dtype)
    return jnp.take(jnp.concatenate([source_row, zero_col], axis=-1), table, axis=-1)


def per_device(features, top_map, bottom_map, first_weight, first_bias, second_weight, second_bias):
    row_count = features.shape[2]
    cycle_width = features.shape[3]
    upper_map = top_map[0]
    lower_map = bottom_map[0]
    gathered = lax.all_gather(features, "chan", axis=1, tiled=True)
    framed = with_halo(gathered, (("space", 2),), 1)
    above_row = remap_row(framed[:, :, 0, :], upper_map)
    below_row = remap_row(framed[:, :, row_count + 1, :], lower_map)
    padded = jnp.concatenate([above_row[:, :, None], gathered, below_row[:, :, None]], 2)
    totals = jnp.zeros(
        (features.shape[0], first_weight.shape[0], row_count, cycle_width), jnp.float32
    )
    for row_step in range(3):
        for col_step in range(3):
            shifted = jnp.roll(
                padded[:, :, row_step : row_step + row_count, :], 1 - col_step, axis=3
            )
            totals = totals + jnp.einsum(
                "oc,bcrw->borw",
                first_weight[:, row_step, col_step, :],
                shifted,
                preferred_element_type=jnp.float32,
            )
    hidden = jax.nn.gelu(totals + first_bias[None, :, None, None]).astype(jnp.bfloat16)
    half_rows = row_count // 2
    gathered_hidden = lax.all_gather(hidden, "chan", axis=1, tiled=True)
    rim_row = shifted_2(gathered_hidden[:, :, row_count - 1, :], "space", 1)
    stacked = jnp.concatenate([remap_row(rim_row, upper_map)[:, :, None], gathered_hidden], 2)
    sums = jnp.zeros(
        (hidden.shape[0], second_weight.shape[0], half_rows, cycle_width // 2), jnp.float32
    )
    for row_step in range(3):
        for col_step in range(3):
            picked = jnp.roll(
                stacked[:, :, row_step : row_step + row_count : 2, :], 1 - col_step, axis=3
            )[..., ::2]
            sums = sums + jnp.einsum(
                "oc,bcrw->borw",
                second_weight[:, row_step, col_step, :],
                picked,
                preferred_element_type=jnp.float32,
            )
    coarse = jax.nn.gelu(sums + second_bias[None, :, None, None]).astype(jnp.bfloat16)
    return (hidden, coarse)


def solution(mesh):
    placed = (
        P(None, "chan", "space", None),
        P("space", None),
        P("space", None),
        P("chan", None, None, None),
        P("chan"),
        P("chan", None, None, None),
        P("chan"),
    )
    return jax.shard_map(
        per_device,
        mesh=mesh,
        in_specs=placed,
        out_specs=(P(None, "chan", "space", None), P(None, "chan", "space", None)),
        check_vma=False,
    )
```

profile of v0, /device:TPU:25, one launch (start us, length us, event | category | flops | bytes accessed | tf_op | source)
XLA Modules:
  0.0 264.1 jit_solution(7621877287431449558)
XLA Ops:
  7.2 1.6 copy.9
  10.3 72.2 %all-gather.3.cloned.1.call-done = bf16[1,128,2,2048]{3,1,2,0:T(8,128)(2,1)} async-done(((bf16[1,16,2,2048]{3,1,2,0:T(8,128)(2,1)}), bf16[1,128,2,2048]{3,1,2,0:T(8,128)(2,1)}) %all-gather.3.cloned.1.call-update) | async-done | bytes 1048592 | tf_op jit(solution)/shard_map/all_gather | solution.py:40
  82.5 2.2 fusion.128
  84.7 6.3 %collective-permute-start = (bf16[1,128,1,2048]{3,1,2,0:T(8,128)(2,1)S(1)}, bf16[1,128,1,2048]{3,1,2,0:T(8,128)(2,1)S(1)}, u32[]{:S(2)}, u32[]{:S(2)}) collective-permute-start(bf16[1,128,1,2048]{3,1,2,0:T(8,128)(2,1)S(1)} %get-tuple-element.25), channel_id=1, source_target_pairs={{0,8},{8,16},{16,24},{24,32},{32,40},{40,48},{48,56},{56,64},{64,7... | collective-permute-start | bytes 1572872 | tf_op jit(solution)/shard_map/ppermute | solution.py:15
  91.0 1.9 collective-permute-start.1
  93.0 4.0 %collective-permute-done = bf16[1,128,1,2048]{3,1,2,0:T(8,128)(2,1)S(1)} collective-permute-done((bf16[1,128,1,2048]{3,1,2,0:T(8,128)(2,1)S(1)}, bf16[1,128,1,2048]{3,1,2,0:T(8,128)(2,1)S(1)}, u32[]{:S(2)}, u32[]{:S(2)}) %collective-permute-start) | collective-permute-done | bytes 524320 | tf_op jit(solution)/shard_map/ppermute | solution.py:15
  97.4 6.2 %gather_fusion = bf16[2048,128]{1,0:T(8,128)(2,1)S(1)} fusion(bf16[128,2049]{0,1:T(8,128)(2,1)S(1)} %copy.10, s32[2048]{0:T(1024)S(1)} %fusion.97), kind=kCustom, calls=%fused_computation.clone | custom fusion | bytes 1056768 | tf_op jit(solution)/shard_map/jit(_take)/gather | solution.py:32
  104.2 6.2 %gather_fusion.1 = bf16[2048,128]{1,0:T(8,128)(2,1)S(1)} fusion(bf16[128,2049]{0,1:T(8,128)(2,1)S(1)} %copy.12, s32[2048]{0:T(1024)S(1)} %fusion.98), kind=kCustom, calls=%fused_computation.1.clone | custom fusion | bytes 1056768 | tf_op jit(solution)/shard_map/jit(_take)/gather | solution.py:32
  110.7 1.4 fusion.6
  115.4 0.9 fusion.54
  116.3 1.7 copy.15
  118.0 61.1 %all-gather.5.cloned.1.call-done = bf16[1,128,2,2048]{3,1,2,0:T(8,128)(2,1)} async-done(((bf16[1,16,2,2048]{3,1,2,0:T(8,128)(2,1)}), bf16[1,128,2,2048]{3,1,2,0:T(8,128)(2,1)}) %all-gather.5.cloned.1.call-update) | async-done | bytes 1048592 | tf_op jit(solution)/shard_map/all_gather | solution.py:61
  179.2 2.3 fusion.127
  181.4 6.3 %collective-permute-start.2 = (bf16[1,128,2048]{2,1,0:T(8,128)(2,1)}, bf16[1,128,2048]{2,1,0:T(8,128)(2,1)}, u32[]{:S(2)}, u32[]{:S(2)}) collective-permute-start(bf16[1,128,2048]{2,1,0:T(8,128)(2,1)} %get-tuple-element.18), channel_id=1, source_target_pairs={{0,8},{8,16},{16,24},{24,32},{32,40},{40,48},{48,56},{56,64},{64,7... | collective-permute-start | bytes 1572872 | tf_op jit(solution)/shard_map/ppermute | solution.py:27
  188.6 9.8 %slice.269 = bf16[1,128,1,1024]{3,1,2,0:T(8,128)(2,1)} slice(bf16[1,128,1,2048]{3,1,2,0:T(8,128)(2,1)S(1)} %pad_maximum_fusion.9), slice={[0:1:1], [0:128:1], [0:1:1], [0:2048:2]} | slice | bytes 524288 | tf_op jit(solution)/shard_map/slice | solution.py:69
  198.4 9.0 %slice.263 = bf16[1,128,1,1024]{3,1,2,0:T(8,128)(2,1)S(1)} slice(bf16[1,128,1,2048]{3,1,2,0:T(8,128)(2,1)S(1)} %pad_maximum_fusion.8), slice={[0:1:1], [0:128:1], [0:1:1], [0:2048:2]} | slice | bytes 524288 | tf_op jit(solution)/shard_map/slice | solution.py:69
  207.5 9.0 %slice.259 = bf16[1,128,1,1024]{3,1,2,0:T(8,128)(2,1)S(1)} slice(bf16[1,128,1,2048]{3,1,2,0:T(8,128)(2,1)S(1)} %pad_maximum_fusion.7), slice={[0:1:1], [0:128:1], [0:1:1], [0:2048:2]} | slice | bytes 524288 | tf_op jit(solution)/shard_map/slice | solution.py:69
  216.7 9.0 %slice.252 = bf16[1,128,1,1024]{3,1,2,0:T(8,128)(2,1)S(1)} slice(bf16[1,128,1,2048]{3,1,2,0:T(8,128)(2,1)S(1)} %pad_maximum_fusion.6), slice={[0:1:1], [0:128:1], [0:1:1], [0:2048:2]} | slice | bytes 524288 | tf_op jit(solution)/shard_map/slice | solution.py:69
  225.7 9.0 %slice.255 = bf16[1,128,1,1024]{3,1,2,0:T(8,128)(2,1)S(1)} slice(bf16[1,128,1,2048]{3,1,2,0:T(8,128)(2,1)S(1)} %get-tuple-element.19), slice={[0:1:1], [0:128:1], [0:1:1], [0:2048:2]} | slice | bytes 524288 | tf_op jit(solution)/shard_map/slice | solution.py:69
  234.7 9.2 %slice.265 = bf16[1,128,1,1024]{3,1,2,0:T(8,128)(2,1)S(1)} slice(bf16[1,128,1,2048]{3,1,2,0:T(8,128)(2,1)S(1)} %get-tuple-element.17), slice={[0:1:1], [0:128:1], [0:1:1], [0:2048:2]} | slice | bytes 524288 | tf_op jit(solution)/shard_map/slice | solution.py:69
  243.9 1.1 pad_bitcast_fusion
  245.3 6.2 %gather_fusion.2 = bf16[2048,128]{1,0:T(8,128)(2,1)S(1)} fusion(bf16[128,2049]{0,1:T(8,128)(2,1)S(1)} %copy.14, s32[2048]{0:T(1024)S(1)} %fusion.97), kind=kCustom, calls=%fused_computation.2.clone | custom fusion | bytes 1056768 | tf_op jit(solution)/shard_map/jit(_take)/gather | solution.py:32
  252.0 0.8 slice.244
  256.4 0.8 fusion.76
  (64 shorter events, 11.5 us)
Async XLA Ops:
  7.2 75.3 %all-gather.3.cloned.1.call-start = ((), (), s32[]{:S(2)}) async-start(), calls=%async_computation | async-start | bytes 1179648 | tf_op jit(solution)/shard_map/all_gather | solution.py:40
  8.8 170.3 %all-gather.5.cloned.1.call-start = ((), (), s32[]{:S(2)}) async-start(), calls=%async_computation.1 | async-start | bytes 1179648 | tf_op jit(solution)/shard_map/all_gather | solution.py:61
  10.3 80.7 %copy-start.4 = (s32[1,2048]{1,0:T(1,128)S(1)}, s32[1,2048]{1,0:T(1,128)}, u32[]{:S(2)}) copy-start(s32[1,2048]{1,0:T(1,128)} %param.11) | copy-start | bytes 24580
  82.5 10.4 %copy-start = (bf16[1,128,2,2048]{3,1,2,0:T(8,128)(2,1)S(1)}, bf16[1,128,2,2048]{3,1,2,0:T(8,128)(2,1)}, u32[]{:S(2)}) copy-start(bf16[1,128,2,2048]{3,1,2,0:T(8,128)(2,1)} %all-gather.3.cloned.1.call-done) | copy-start | bytes 3145732
  84.7 12.4 %collective-permute-start = (bf16[1,128,1,2048]{3,1,2,0:T(8,128)(2,1)S(1)}, bf16[1,128,1,2048]{3,1,2,0:T(8,128)(2,1)S(1)}, u32[]{:S(2)}, u32[]{:S(2)}) collective-permute-start(bf16[1,128,1,2048]{3,1,2,0:T(8,128)(2,1)S(1)} %get-tuple-element.25), channel_id=1, source_target_pairs={{0,8},{8,16},{16,24},{24,32},{32,40},{40,48},{48,56},{56,64},{64,7... | collective-permute-start | bytes 1572872 | tf_op jit(solution)/shard_map/ppermute | solution.py:15
  91.0 12.8 %collective-permute-start.1 = (bf16[1,128,1,2048]{3,1,2,0:T(8,128)(2,1)}, bf16[1,128,1,2048]{3,1,2,0:T(8,128)(2,1)S(1)}, u32[]{:S(2)}, u32[]{:S(2)}) collective-permute-start(bf16[1,128,1,2048]{3,1,2,0:T(8,128)(2,1)} %get-tuple-element.24), channel_id=1, source_target_pairs={{8,0},{16,8},{24,16},{32,24},{40,32},{48,40},{56,48},{64,56},{72,6... | collective-permute-start | bytes 1572872 | tf_op jit(solution)/shard_map/ppermute | solution.py:17
  110.7 1.4 copy-start.5
  114.7 0.7 copy-start.6
  179.1 8.6 %copy-start.1 = (bf16[1,128,2,2048]{3,1,2,0:T(8,128)(2,1)S(1)}, bf16[1,128,2,2048]{3,1,2,0:T(8,128)(2,1)}, u32[]{:S(2)}) copy-start(bf16[1,128,2,2048]{3,1,2,0:T(8,128)(2,1)} %all-gather.5.cloned.1.call-done) | copy-start | bytes 3145732
  181.4 62.4 %collective-permute-start.2 = (bf16[1,128,2048]{2,1,0:T(8,128)(2,1)}, bf16[1,128,2048]{2,1,0:T(8,128)(2,1)}, u32[]{:S(2)}, u32[]{:S(2)}) collective-permute-start(bf16[1,128,2048]{2,1,0:T(8,128)(2,1)} %get-tuple-element.18), channel_id=1, source_target_pairs={{0,8},{8,16},{16,24},{24,32},{32,40},{40,48},{48,56},{56,64},{64,7... | collective-permute-start | bytes 1572872 | tf_op jit(solution)/shard_map/ppermute | solution.py:27
  252.9 1.8 copy-start.3
  255.4 1.0 copy-start.2
  255.4 0.9 copy-start.7
Sparse Core Ops, SparseCore 0:
  11.8 70.6 all-gather.2
  116.5 62.6 all-gather.4
where the time goes:
time: 264 us
  waiting for transfers between devices  137 us (52%)
  local copies, waits for them, and re-layouts  87.6 us (33%)
  starting transfers between devices  14.6 us (6%)
  between operations  14.4 us (5%)
  matrix products  5.98 us (2%)
  other arithmetic  4.09 us (2%)
    all_gather x1, waiting for transfers between devices, per_device(): gathered = lax.all_gather(features, 'chan', axis=1, tiled=True)  72.2 us
    all_gather x1, waiting for transfers between devices, per_device(): gathered_hidden = lax.all_gather(hidden, 'chan', axis=1, tiled=True)  61.1 us
    slice x13, local copies, waits for them, and re-layouts, per_device(): jnp.roll(stacked[:, :, row_step:row_step + row_count:2, :], 1 - col_step,...  58.1 us
    gather x5, local copies, waits for them, and re-layouts, remap_row(): jnp.take(jnp.concatenate([source_row, zero_col], axis=-1), table, axis=-1)  19 us
    ppermute x1, starting transfers between devices, shifted_2(): return lax.ppermute(array, axis, pairs)  6.29 us
    ppermute x1, starting transfers between devices, with_halo(): lax.ppermute(tail, axis, [(i, (i + 1) % count) for i in range(ends)])  6.29 us
  transfers between devices with their start and end apart: 5, of which 3 were waited for; matrix products, arithmetic and copies ran while one was open for 25% of the time, Pallas kernels for 0%

commit v1 on v0

v1 whole, which is shorter than its diff:
```python
import jax
import jax.numpy as jnp
from jax import lax
from jax.sharding import PartitionSpec as P


def shifted(array, axis, by):
    devices = lax.axis_size(axis)
    pairs = [(i, i + by) for i in range(devices) if 0 <= i + by < devices]
    return lax.ppermute(array, axis, pairs)


def remap_window(source, table, first_col, width):
    cycle = table.shape[0]
    cols = (first_col + jnp.arange(width)) % cycle
    picked = lax.dynamic_slice_in_dim(
        jnp.concatenate([table, table], axis=0), first_col % cycle, width, axis=0
    )
    same = source[..., 1 : width + 1]
    prev = source[..., 0:width]
    nxt = source[..., 2 : width + 2]
    zero = jnp.zeros_like(same)
    out = jnp.where(picked == (cols + cycle - 1) % cycle, prev, zero)
    out = jnp.where(picked == (cols + 1) % cycle, nxt, out)
    out = jnp.where(picked == cols, same, out)
    return out


def remap_full(row, table):
    cycle = table.shape[0]
    wrapped = jnp.concatenate([row[..., -1:], row, row[..., :1]], axis=-1)
    return remap_window(wrapped, table, 0, cycle)


def conv(x, w, stride):
    return lax.conv_general_dilated(
        x,
        w,
        window_strides=stride,
        padding="VALID",
        dimension_numbers=("NCHW", "OHWI", "NCHW"),
        preferred_element_type=jnp.float32,
    )


def per_device(features, top_map, bottom_map, first_weight, first_bias, second_weight, second_bias):
    groups = lax.axis_size("chan")
    me = lax.axis_index("chan")
    x = features[0]
    rows = x.shape[1]
    cycle = x.shape[2]
    block = cycle // groups
    upper_map = top_map[0]
    lower_map = bottom_map[0]

    w1 = lax.all_gather(first_weight, "chan", axis=0, tiled=True)
    b1 = lax.all_gather(first_bias, "chan", axis=0, tiled=True)
    w2 = lax.all_gather(second_weight, "chan", axis=0, tiled=True)
    b2 = lax.all_gather(second_bias, "chan", axis=0, tiled=True)

    above_src = shifted(x[:, rows - 1, :], "space", 1)
    below_src = shifted(x[:, 0, :], "space", -1)
    above = remap_full(above_src, upper_map)
    below = remap_full(below_src, lower_map)
    padded = jnp.concatenate([above[:, None], x, below[:, None]], axis=1)

    halo = 3
    width = block + 2 * halo
    ext = jnp.concatenate([padded[..., cycle - halo :], padded, padded[..., :halo]], axis=-1)
    sends = jnp.stack([ext[..., j * block : j * block + width] for j in range(groups)], 0)
    got = lax.all_to_all(sends, "chan", 0, 0, tiled=True)
    window = got.reshape((-1,) + got.shape[2:])

    pre1 = conv(window[None], w1, (1, 1))
    hidden_win = jax.nn.gelu(pre1 + b1[None, :, None, None]).astype(jnp.bfloat16)[0]

    hidden_out = lax.all_to_all(
        hidden_win[:, :, halo - 1 : halo - 1 + block], "chan", 0, 2, tiled=True
    )

    rim_src = shifted(hidden_win[:, rows - 1, :], "space", 1)
    rim = remap_window(rim_src, upper_map, me * block - 1, block + 2)
    stacked = jnp.concatenate([rim[:, None], hidden_win[:, :, 1 : block + 3]], axis=1)
    pre2 = conv(stacked[None], w2, (1, 2))
    coarse_win = jax.nn.gelu(pre2 + b2[None, :, None, None]).astype(jnp.bfloat16)[0]
    coarse_out = lax.all_to_all(coarse_win, "chan", 0, 2, tiled=True)
    return hidden_out[None], coarse_out[None]


def solution(mesh):
    placed = (
        P(None, "chan", "space", None),
        P("space", None),
        P("space", None),
        P("chan", None, None, None),
        P("chan"),
        P("chan", None, None, None),
        P("chan"),
    )
    return jax.shard_map(
        per_device,
        mesh=mesh,
        in_specs=placed,
        out_specs=(P(None, "chan", "space", None), P(None, "chan", "space", None)),
        check_vma=False,
    )
```

time: 264 us -> 200 us (0.76)
  the two profiles are of different devices: /device:TPU:25 before, /device:TPU:64 now
where the time goes in v1:
time: 200 us; the launch traced here: 199 us
  blocking collectives  130 us (65%)
  waiting for transfers between devices  24.3 us (12%)
  starting transfers between devices  21.9 us (11%)
  local copies, waits for them, and re-layouts  16.6 us (8%)
  other arithmetic  2.91 us (1%)
  between operations  2.33 us (1%)
    all_gather x1, blocking collectives, per_device(): w1 = lax.all_gather(first_weight, 'chan', axis=0, tiled=True)  49.5 us
    all_gather x1, blocking collectives, per_device(): w2 = lax.all_gather(second_weight, 'chan', axis=0, tiled=True)  46.5 us
    unnamed x1, blocking collectives  34.2 us
    unnamed x38, local copies, waits for them, and re-layouts  11.9 us
    all_to_all x1, waiting for transfers between devices, per_device(): lax.all_to_all(hidden_win[:, :, halo - 1:halo - 1 + block], 'chan', 0, 2,...  9.74 us
    ppermute x3, starting transfers between devices, shifted(): return lax.ppermute(array, axis, pairs)  9.59 us
    all_to_all x1, waiting for transfers between devices, per_device(): coarse_out = lax.all_to_all(coarse_win, 'chan', 0, 2, tiled=True)  8.79 us
    ppermute x3, waiting for transfers between devices, shifted(): return lax.ppermute(array, axis, pairs)  5.76 us
  transfers between devices with their start and end apart: 6, of which 3 were waited for; matrix products, arithmetic and copies ran while one was open for 2% of the time, Pallas kernels for 0%

profile of v1, /device:TPU:64, one launch (start us, length us, event | category | flops | bytes accessed | tf_op | source)
XLA Modules:
  0.0 199.2 jit_solution(16435346475391124692)
XLA Ops:
  0.6 0.9 copy.98
  1.6 1.9 collective-permute-start
  3.5 5.8 %collective-permute-start.1 = (bf16[16,2048]{1,0:T(8,128)(2,1)S(1)}, bf16[16,2048]{1,0:T(8,128)(2,1)S(1)}, u32[]{:S(2)}, u32[]{:S(2)}) collective-permute-start(bf16[16,2048]{1,0:T(8,128)(2,1)S(1)} %get-tuple-element.15), channel_id=1, source_target_pairs={{8,0},{16,8},{24,16},{32,24},{40,32},{48,40},{56,48},{64,56},{72,6... | collective-permute-start | bytes 196616 | tf_op jit(solution)/shard_map/ppermute | solution.py:10
  10.0 1.3 dynamic-slice
  14.3 34.2 %all-reduce.2 = (f32[128]{0:T(128)S(1)}, f32[256]{0:T(256)S(1)}) all-reduce(f32[128]{0:T(128)S(1)} %dynamic-update-slice, f32[256]{0:T(256)S(1)} %dynamic-update-slice.1), channel_id=1, replica_groups=mesh['space'=64,'chan'=8] {'chan'}, use_global_device_ids=true, to_apply=%add | all-reduce | flops 384 | bytes 3072
  48.9 0.7 fusion.64
  50.3 0.7 fusion.60
  51.0 0.7 fusion.59
  51.7 0.7 fusion.58
  52.4 0.7 fusion.57
  53.1 0.7 fusion.56
  53.8 0.7 fusion.55
  54.6 3.6 %all-to-all-start = ((bf16[8,16,4,262]{3,1,2,0:T(8,128)(2,1)}), bf16[8,16,4,262]{3,1,2,0:T(8,128)(2,1)S(1)}, u32[]{:S(2)}, u32[]{:S(2)}) async-start(bf16[8,16,4,262]{3,1,2,0:T(8,128)(2,1)} %fusion.55), calls=%async_computation | async-start | bytes 786432 | tf_op jit(solution)/shard_map/all_to_all | solution.py:71
  58.2 49.5 %all_gather.12 = bf16[128,3,3,128]{3,0,2,1:T(8,128)(2,1)S(1)} all-gather(bf16[16,3,3,128]{3,0,2,1:T(8,128)(2,1)S(1)} %copy-done.2), channel_id=1, replica_groups=mesh['space'=64,'chan'=8] {'chan'}, dimensions={0}, use_global_device_ids=true | all-gather | bytes 331776 | tf_op jit(solution)/shard_map/all_gather | solution.py:56
  107.8 46.5 %all_gather.14 = bf16[256,3,3,128]{3,0,2,1:T(8,128)(2,1)S(1)} all-gather(bf16[32,3,3,128]{3,0,2,1:T(8,128)(2,1)S(1)} %copy-done.1), channel_id=1, replica_groups=mesh['space'=64,'chan'=8] {'chan'}, dimensions={0}, use_global_device_ids=true | all-gather | bytes 663552 | tf_op jit(solution)/shard_map/all_gather | solution.py:58
  156.4 1.9 collective-permute-start.2
  158.3 5.8 %collective-permute-done.2 = bf16[128,260]{0,1:T(8,128)(2,1)S(1)} collective-permute-done((bf16[128,260]{0,1:T(8,128)(2,1)S(1)}, bf16[128,260]{0,1:T(8,128)(2,1)S(1)}, u32[]{:S(2)}, u32[]{:S(2)}) %collective-permute-start.2) | collective-permute-done | bytes 66592 | tf_op jit(solution)/shard_map/ppermute | solution.py:10
  164.4 0.8 slice-done
  168.7 5.3 %all-to-all-start.2 = ((bf16[8,2,2048]{2,1,0:T(2,128)(2,1)}), bf16[8,2,2048]{2,1,0:T(2,128)(2,1)S(1)}, u32[]{:S(2)}, u32[]{:S(2)}) async-start(bf16[8,2,2048]{2,1,0:T(2,128)(2,1)} %reshape.47), calls=%async_computation.2 | async-start | bytes 131072 | tf_op jit(solution)/shard_map/all_to_all | solution.py:86
  174.1 0.9 slice-done.1
  175.0 0.8 copy.78
  175.8 8.8 %all-to-all-done.2 = bf16[8,2,2048]{2,1,0:T(2,128)(2,1)S(1)} async-done(((bf16[8,2,2048]{2,1,0:T(2,128)(2,1)}), bf16[8,2,2048]{2,1,0:T(2,128)(2,1)S(1)}, u32[]{:S(2)}, u32[]{:S(2)}) %all-to-all-start.2) | async-done | bytes 65568 | tf_op jit(solution)/shard_map/all_to_all | solution.py:86
  184.6 3.4 %all-to-all-start.1 = ((bf16[128,2,256]{2,1,0:T(2,128)(2,1)}), bf16[128,2,256]{2,1,0:T(2,128)(2,1)S(1)}, u32[]{:S(2)}, u32[]{:S(2)}) async-start(bf16[128,2,256]{2,1,0:T(2,128)(2,1)} %copy.78), calls=%async_computation.1 | async-start | bytes 262144 | tf_op jit(solution)/shard_map/all_to_all | solution.py:77
  188.7 9.7 %all-to-all-done.1 = bf16[128,2,256]{2,1,0:T(2,128)(2,1)S(1)} async-done(((bf16[128,2,256]{2,1,0:T(2,128)(2,1)}), bf16[128,2,256]{2,1,0:T(2,128)(2,1)S(1)}, u32[]{:S(2)}, u32[]{:S(2)}) %all-to-all-start.1) | async-done | bytes 131104 | tf_op jit(solution)/shard_map/all_to_all | solution.py:77
  (69 shorter events, 10.9 us)
Async XLA Ops:
  1.6 7.7 %copy-start.3 = (s32[1,2048]{1,0:T(1,128)S(1)}, s32[1,2048]{1,0:T(1,128)}, u32[]{:S(2)}) copy-start(s32[1,2048]{1,0:T(1,128)} %param.8) | copy-start | bytes 24580
  1.6 46.9 %collective-permute-start = (bf16[16,2048]{1,0:T(8,128)(2,1)S(1)}, bf16[16,2048]{1,0:T(8,128)(2,1)S(1)}, u32[]{:S(2)}, u32[]{:S(2)}) collective-permute-start(bf16[16,2048]{1,0:T(8,128)(2,1)S(1)} %get-tuple-element.14), channel_id=1, source_target_pairs={{0,8},{8,16},{16,24},{24,32},{32,40},{40,48},{48,56},{56,64},{64,7... | collective-permute-start | bytes 196616 | tf_op jit(solution)/shard_map/ppermute | solution.py:10
  3.5 45.0 %collective-permute-start.1 = (bf16[16,2048]{1,0:T(8,128)(2,1)S(1)}, bf16[16,2048]{1,0:T(8,128)(2,1)S(1)}, u32[]{:S(2)}, u32[]{:S(2)}) collective-permute-start(bf16[16,2048]{1,0:T(8,128)(2,1)S(1)} %get-tuple-element.15), channel_id=1, source_target_pairs={{8,0},{16,8},{24,16},{32,24},{40,32},{48,40},{56,48},{64,56},{72,6... | collective-permute-start | bytes 196616 | tf_op jit(solution)/shard_map/ppermute | solution.py:10
  9.3 0.7 copy-start.4
  12.6 0.7 copy-start.5
  13.5 0.7 copy-start.6
  54.5 3.7 %copy-start.2 = (bf16[16,3,3,128]{3,0,2,1:T(8,128)(2,1)S(1)}, bf16[16,3,3,128]{3,0,2,1:T(8,128)(2,1)}, u32[]{:S(2)}) copy-start(bf16[16,3,3,128]{3,0,2,1:T(8,128)(2,1)} %param.10) | copy-start | bytes 110596
  54.6 99.7 %all-to-all-start = ((bf16[8,16,4,262]{3,1,2,0:T(8,128)(2,1)}), bf16[8,16,4,262]{3,1,2,0:T(8,128)(2,1)S(1)}, u32[]{:S(2)}, u32[]{:S(2)}) async-start(bf16[8,16,4,262]{3,1,2,0:T(8,128)(2,1)} %fusion.55), calls=%async_computation | async-start | bytes 786432 | tf_op jit(solution)/shard_map/all_to_all | solution.py:71
  58.2 49.5 %copy-start.1 = (bf16[32,3,3,128]{3,0,2,1:T(8,128)(2,1)S(1)}, bf16[32,3,3,128]{3,0,2,1:T(8,128)(2,1)}, u32[]{:S(2)}) copy-start(bf16[32,3,3,128]{3,0,2,1:T(8,128)(2,1)} %param.12) | copy-start | bytes 221188
  154.7 0.7 copy-start.7
  156.2 2.1 %copy-start = (bf16[128,2,260]{0,1,2:T(2,128)(2,1)}, bf16[128,2,260]{0,1,2:T(2,128)(2,1)S(1)}, u32[]{:S(2)}) copy-start(bf16[128,2,260]{0,1,2:T(2,128)(2,1)S(1)} %slice_bitcast_fusion) | copy-start | bytes 399364
  156.4 7.7 %collective-permute-start.2 = (bf16[128,260]{0,1:T(8,128)(2,1)S(1)}, bf16[128,260]{0,1:T(8,128)(2,1)S(1)}, u32[]{:S(2)}, u32[]{:S(2)}) collective-permute-start(bf16[128,260]{0,1:T(8,128)(2,1)S(1)} %bitcast.104), channel_id=1, source_target_pairs={{0,8},{8,16},{16,24},{24,32},{32,40},{40,48},{48,56},{56,64},{64,7... | collective-permute-start | bytes 199688 | tf_op jit(solution)/shard_map/ppermute | solution.py:10
  164.3 0.9 slice-start
  165.6 0.7 copy-start.8
  168.7 15.8 %all-to-all-start.2 = ((bf16[8,2,2048]{2,1,0:T(2,128)(2,1)}), bf16[8,2,2048]{2,1,0:T(2,128)(2,1)S(1)}, u32[]{:S(2)}, u32[]{:S(2)}) async-start(bf16[8,2,2048]{2,1,0:T(2,128)(2,1)} %reshape.47), calls=%async_computation.2 | async-start | bytes 131072 | tf_op jit(solution)/shard_map/all_to_all | solution.py:86
  174.1 0.9 slice-start.1
  184.6 13.9 %all-to-all-start.1 = ((bf16[128,2,256]{2,1,0:T(2,128)(2,1)}), bf16[128,2,256]{2,1,0:T(2,128)(2,1)S(1)}, u32[]{:S(2)}, u32[]{:S(2)}) async-start(bf16[128,2,256]{2,1,0:T(2,128)(2,1)} %copy.78), calls=%async_computation.1 | async-start | bytes 262144 | tf_op jit(solution)/shard_map/all_to_all | solution.py:77

commit v2 on v1

--- a/solution.py
+++ b/solution.py
@@ -32,6 +32,32 @@
     return remap_window(wrapped, table, 0, cycle)
 
 
+def gather_chan(x):
+    groups = lax.axis_size("chan")
+    me = lax.axis_index("chan")
+    got = [x]
+    for k in range(1, groups):
+        pairs = [(i, (i + k) % groups) for i in range(groups)]
+        got.append(lax.ppermute(x, "chan", pairs))
+    ahead = jnp.stack([got[0]] + got[:0:-1], 0)
+    both = jnp.concatenate([ahead, ahead], 0)
+    ordered = lax.dynamic_slice_in_dim(both, (groups - me) % groups, groups, axis=0)
+    return ordered.reshape((-1,) + x.shape[1:])
+
+
+def split3(v):
+    hi = v.astype(jnp.bfloat16)
+    rest = v - hi.astype(jnp.float32)
+    mid = rest.astype(jnp.bfloat16)
+    lo = (rest - mid.astype(jnp.float32)).astype(jnp.bfloat16)
+    return jnp.stack([hi, mid, lo], -1)
+
+
+def join3(parts):
+    parts = parts.astype(jnp.float32)
+    return (parts[..., 0] + parts[..., 1]) + parts[..., 2]
+
+
 def conv(x, w, stride):
     return lax.conv_general_dilated(
         x,
@@ -53,10 +79,20 @@
     upper_map = top_map[0]
     lower_map = bottom_map[0]
 
-    w1 = lax.all_gather(first_weight, "chan", axis=0, tiled=True)
-    b1 = lax.all_gather(first_bias, "chan", axis=0, tiled=True)
-    w2 = lax.all_gather(second_weight, "chan", axis=0, tiled=True)
-    b2 = lax.all_gather(second_bias, "chan", axis=0, tiled=True)
+    n1 = first_weight.shape[0]
+    n2 = second_weight.shape[0]
+    flat = jnp.concatenate(
+        [first_weight.reshape(n1, -1), second_weight.reshape(n2, -1)], axis=0
+    )
+    packed = jnp.concatenate(
+        [flat, split3(jnp.concatenate([first_bias, second_bias]))], axis=1
+    )
+    every = gather_chan(packed[None]).reshape((groups, n1 + n2, -1))
+    taps = flat.shape[1]
+    w1 = every[:, :n1, :taps].reshape((-1,) + first_weight.shape[1:])
+    w2 = every[:, n1:, :taps].reshape((-1,) + second_weight.shape[1:])
+    b1 = join3(every[:, :n1, taps:]).reshape(-1)
+    b2 = join3(every[:, n1:, taps:]).reshape(-1)
 
     above_src = shifted(x[:, rows - 1, :], "space", 1)
     below_src = shifted(x[:, 0, :], "space", -1)

time: 200 us -> 130 us (0.65)
  blocking collectives: 130 us -> 0 us
  starting transfers between devices: 21.9 us -> 60.4 us
  waiting for transfers between devices: 24.3 us -> 36.1 us
  local copies, waits for them, and re-layouts: 16.6 us -> 24.8 us
  other arithmetic: 2.91 us -> 6.17 us
    all_gather x2 -> x0, blocking collectives: 96 us -> none  [the longest x1 49.5 us: per_device(): w1 = lax.all_gather(first_weight, 'chan', axis=0, tiled=True)]
    ppermute x0 -> x7, starting transfers between devices: none -> 38.7 us  [gather_chan(): got.append(lax.ppermute(x, 'chan', pairs))]
    unnamed x1 -> x0, blocking collectives: 34.2 us -> none
    unnamed x38 -> x36, local copies, waits for them, and re-layouts: 11.9 us -> 18.6 us
    ppermute x0 -> x7, waiting for transfers between devices: none -> 6.41 us  [gather_chan(): got.append(lax.ppermute(x, 'chan', pairs))]
    ppermute x3, waiting for transfers between devices: 5.76 us -> 10 us  [shifted(): return lax.ppermute(array, axis, pairs)]
    ppermute x3, starting transfers between devices: 9.59 us -> 6.76 us  [shifted(): return lax.ppermute(array, axis, pairs)]
    all_to_all x1, starting transfers between devices: 3.58 us -> 5.74 us  [per_device(): got = lax.all_to_all(sends, 'chan', 0, 0, tiled=True)]
  transfers between devices with their start and end apart: 6 -> 13, of which waited for: 3 -> 6; matrix products, arithmetic and copies ran while one was open for 2% -> 18% of each run, Pallas kernels for 0% -> 0%
where the time goes in v2:
time: 130 us
  starting transfers between devices  60.4 us (46%)
  waiting for transfers between devices  36.1 us (28%)
  local copies, waits for them, and re-layouts  24.8 us (19%)
  other arithmetic  6.17 us (5%)
    ppermute x7, starting transfers between devices, gather_chan(): got.append(lax.ppermute(x, 'chan', pairs))  38.7 us
    unnamed x36, local copies, waits for them, and re-layouts  18.6 us
    all_to_all x1, waiting for transfers between devices, per_device(): lax.all_to_all(hidden_win[:, :, halo - 1:halo - 1 + block], 'chan', 0, 2,...  10.1 us
    ppermute x3, waiting for transfers between devices, shifted(): return lax.ppermute(array, axis, pairs)  10 us
    all_to_all x1, waiting for transfers between devices, per_device(): coarse_out = lax.all_to_all(coarse_win, 'chan', 0, 2, tiled=True)  9.57 us
    ppermute x3, starting transfers between devices, shifted(): return lax.ppermute(array, axis, pairs)  6.76 us
    ppermute x7, waiting for transfers between devices, gather_chan(): got.append(lax.ppermute(x, 'chan', pairs))  6.41 us
    all_to_all x1, starting transfers between devices, per_device(): coarse_out = lax.all_to_all(coarse_win, 'chan', 0, 2, tiled=True)  5.82 us
  transfers between devices with their start and end apart: 13, of which 6 were waited for; matrix products, arithmetic and copies ran while one was open for 18% of the time, Pallas kernels for 0%

profile of v2, /device:TPU:64, one launch (start us, length us, event | category | flops | bytes accessed | tf_op | source)
XLA Modules:
  0.0 129.5 jit_solution(12854763176655193830)
XLA Ops:
  1.7 0.9 copy.141
  2.7 0.8 copy.140
  3.7 12.2 %collective-permute-start.2 = (bf16[1,48,1155]{2,1,0:T(8,128)(2,1)S(1)}, bf16[1,48,1155]{2,1,0:T(8,128)(2,1)S(1)}, u32[]{:S(2)}, u32[]{:S(2)}) collective-permute-start(bf16[1,48,1155]{2,1,0:T(8,128)(2,1)S(1)} %bitcast.125), channel_id=1, source_target_pairs={{0,7},{1,0},{2,1},{3,2},{4,3},{5,4},{6,5},{7,6},{8,15},{9,8},{10,9... | collective-permute-start | bytes 332648 | tf_op jit(solution)/shard_map/ppermute | solution.py:41
  15.9 2.7 %collective-permute-start.3 = (bf16[1,48,1155]{2,1,0:T(8,128)(2,1)S(1)}, bf16[1,48,1155]{2,1,0:T(8,128)(2,1)S(1)}, u32[]{:S(2)}, u32[]{:S(2)}) collective-permute-start(bf16[1,48,1155]{2,1,0:T(8,128)(2,1)S(1)} %bitcast.126), channel_id=1, source_target_pairs={{0,6},{1,7},{2,0},{3,1},{4,2},{5,3},{6,4},{7,5},{8,14},{9,15},{10,... | collective-permute-start | bytes 332648 | tf_op jit(solution)/shard_map/ppermute | solution.py:41
  18.6 1.9 %collective-permute-start.4 = (bf16[1,48,1155]{2,1,0:T(8,128)(2,1)S(1)}, bf16[1,48,1155]{2,1,0:T(8,128)(2,1)S(1)}, u32[]{:S(2)}, u32[]{:S(2)}) collective-permute-start(bf16[1,48,1155]{2,1,0:T(8,128)(2,1)S(1)} %bitcast.127), channel_id=1, source_target_pairs={{0,5},{1,6},{2,7},{3,0},{4,1},{5,2},{6,3},{7,4},{8,13},{9,14},{10,... | collective-permute-start | bytes 332648 | tf_op jit(solution)/shard_map/ppermute | solution.py:41
  20.6 4.6 %collective-permute-start.5 = (bf16[1,48,1155]{2,1,0:T(8,128)(2,1)S(1)}, bf16[1,48,1155]{2,1,0:T(8,128)(2,1)S(1)}, u32[]{:S(2)}, u32[]{:S(2)}) collective-permute-start(bf16[1,48,1155]{2,1,0:T(8,128)(2,1)S(1)} %bitcast.128), channel_id=1, source_target_pairs={{0,4},{1,5},{2,6},{3,7},{4,0},{5,1},{6,2},{7,3},{8,12},{9,13},{10,... | collective-permute-start | bytes 332648 | tf_op jit(solution)/shard_map/ppermute | solution.py:41
  25.2 0.9 copy.180
  26.2 1.9 %collective-permute-start = (bf16[16,2048]{1,0:T(8,128)(2,1)S(1)}, bf16[16,2048]{1,0:T(8,128)(2,1)S(1)}, u32[]{:S(2)}, u32[]{:S(2)}) collective-permute-start(bf16[16,2048]{1,0:T(8,128)(2,1)S(1)} %get-tuple-element.16), channel_id=1, source_target_pairs={{0,8},{8,16},{16,24},{24,32},{32,40},{40,48},{48,56},{56,64},{64,7... | collective-permute-start | bytes 196616 | tf_op jit(solution)/shard_map/ppermute | solution.py:10
  31.0 2.8 %collective-permute-done = bf16[16,2048]{1,0:T(8,128)(2,1)S(1)} collective-permute-done((bf16[16,2048]{1,0:T(8,128)(2,1)S(1)}, bf16[16,2048]{1,0:T(8,128)(2,1)S(1)}, u32[]{:S(2)}, u32[]{:S(2)}) %collective-permute-start) | collective-permute-done | bytes 65568 | tf_op jit(solution)/shard_map/ppermute | solution.py:10
  33.9 2.9 %collective-permute-start.1 = (bf16[16,2048]{1,0:T(8,128)(2,1)S(1)}, bf16[16,2048]{1,0:T(8,128)(2,1)S(1)}, u32[]{:S(2)}, u32[]{:S(2)}) collective-permute-start(bf16[16,2048]{1,0:T(8,128)(2,1)S(1)} %get-tuple-element.17), channel_id=1, source_target_pairs={{8,0},{16,8},{24,16},{32,24},{40,32},{48,40},{56,48},{64,56},{72,6... | collective-permute-start | bytes 196616 | tf_op jit(solution)/shard_map/ppermute | solution.py:10
  36.9 1.8 %collective-permute-done.1 = bf16[16,2048]{1,0:T(8,128)(2,1)S(1)} collective-permute-done((bf16[16,2048]{1,0:T(8,128)(2,1)S(1)}, bf16[16,2048]{1,0:T(8,128)(2,1)S(1)}, u32[]{:S(2)}, u32[]{:S(2)}) %collective-permute-start.1) | collective-permute-done | bytes 65568 | tf_op jit(solution)/shard_map/ppermute | solution.py:10
  38.7 6.0 %collective-permute-start.6 = (bf16[1,48,1155]{2,1,0:T(8,128)(2,1)S(1)}, bf16[1,48,1155]{2,1,0:T(8,128)(2,1)S(1)}, u32[]{:S(2)}, u32[]{:S(2)}) collective-permute-start(bf16[1,48,1155]{2,1,0:T(8,128)(2,1)S(1)} %bitcast.129), channel_id=1, source_target_pairs={{0,3},{1,4},{2,5},{3,6},{4,7},{5,0},{6,1},{7,2},{8,11},{9,12},{10,... | collective-permute-start | bytes 332648 | tf_op jit(solution)/shard_map/ppermute | solution.py:41
  50.7 5.7 %all-to-all-start = ((bf16[8,16,4,262]{3,1,2,0:T(8,128)(2,1)}), bf16[8,16,4,262]{3,1,2,0:T(8,128)(2,1)S(1)}, u32[]{:S(2)}, u32[]{:S(2)}) async-start(bf16[8,16,4,262]{3,1,2,0:T(8,128)(2,1)} %constant_dynamic-update-slice_fusion), calls=%async_computation | async-start | bytes 786432 | tf_op jit(solution)/shard_map/all_to_all | solution.py:107
  56.4 3.9 %collective-permute-start.7 = (bf16[1,48,1155]{2,1,0:T(8,128)(2,1)S(1)}, bf16[1,48,1155]{2,1,0:T(8,128)(2,1)S(1)}, u32[]{:S(2)}, u32[]{:S(2)}) collective-permute-start(bf16[1,48,1155]{2,1,0:T(8,128)(2,1)S(1)} %bitcast.130), channel_id=1, source_target_pairs={{0,2},{1,3},{2,4},{3,5},{4,6},{5,7},{6,0},{7,1},{8,10},{9,11},{10,... | collective-permute-start | bytes 332648 | tf_op jit(solution)/shard_map/ppermute | solution.py:41
  61.0 7.3 %collective-permute-start.8 = (bf16[1,48,1155]{2,1,0:T(8,128)(2,1)S(1)}, bf16[1,48,1155]{2,1,0:T(8,128)(2,1)S(1)}, u32[]{:S(2)}, u32[]{:S(2)}) collective-permute-start(bf16[1,48,1155]{2,1,0:T(8,128)(2,1)S(1)} %bitcast.131), channel_id=1, source_target_pairs={{0,1},{1,2},{2,3},{3,4},{4,5},{5,6},{6,7},{7,0},{8,9},{9,10},{10,1... | collective-permute-start | bytes 332648 | tf_op jit(solution)/shard_map/ppermute | solution.py:41
  71.6 6.4 %collective-permute-done.8 = bf16[1,48,1155]{2,1,0:T(8,128)(2,1)S(1)} collective-permute-done((bf16[1,48,1155]{2,1,0:T(8,128)(2,1)S(1)}, bf16[1,48,1155]{2,1,0:T(8,128)(2,1)S(1)}, u32[]{:S(2)}, u32[]{:S(2)}) %collective-permute-start.8) | collective-permute-done | bytes 110912 | tf_op jit(solution)/shard_map/ppermute | solution.py:41
  83.9 1.3 dynamic-slice_bitcast_fusion
  87.3 1.9 %collective-permute-start.9 = (bf16[128,260]{0,1:T(8,128)(2,1)S(1)}, bf16[128,260]{0,1:T(8,128)(2,1)S(1)}, u32[]{:S(2)}, u32[]{:S(2)}) collective-permute-start(bf16[128,260]{0,1:T(8,128)(2,1)S(1)} %bitcast.136), channel_id=1, source_target_pairs={{0,8},{8,16},{16,24},{24,32},{32,40},{40,48},{48,56},{56,64},{64,7... | collective-permute-start | bytes 199688 | tf_op jit(solution)/shard_map/ppermute | solution.py:10
  89.6 5.4 %collective-permute-done.9 = bf16[128,260]{0,1:T(8,128)(2,1)S(1)} collective-permute-done((bf16[128,260]{0,1:T(8,128)(2,1)S(1)}, bf16[128,260]{0,1:T(8,128)(2,1)S(1)}, u32[]{:S(2)}, u32[]{:S(2)}) %collective-permute-start.9) | collective-permute-done | bytes 66592 | tf_op jit(solution)/shard_map/ppermute | solution.py:10
  98.2 5.8 %all-to-all-start.2 = ((bf16[8,2,2048]{2,1,0:T(2,128)(2,1)}), bf16[8,2,2048]{2,1,0:T(2,128)(2,1)S(1)}, u32[]{:S(2)}, u32[]{:S(2)}) async-start(bf16[8,2,2048]{2,1,0:T(2,128)(2,1)} %reshape.182), calls=%async_computation.2 | async-start | bytes 131072 | tf_op jit(solution)/shard_map/all_to_all | solution.py:122
  104.1 0.8 copy.147
  104.9 9.6 %all-to-all-done.2 = bf16[8,2,2048]{2,1,0:T(2,128)(2,1)S(1)} async-done(((bf16[8,2,2048]{2,1,0:T(2,128)(2,1)}), bf16[8,2,2048]{2,1,0:T(2,128)(2,1)S(1)}, u32[]{:S(2)}, u32[]{:S(2)}) %all-to-all-start.2) | async-done | bytes 65568 | tf_op jit(solution)/shard_map/all_to_all | solution.py:122
  114.5 3.4 %all-to-all-start.1 = ((bf16[128,2,256]{2,1,0:T(2,128)(2,1)}), bf16[128,2,256]{2,1,0:T(2,128)(2,1)S(1)}, u32[]{:S(2)}, u32[]{:S(2)}) async-start(bf16[128,2,256]{2,1,0:T(2,128)(2,1)} %copy.147), calls=%async_computation.1 | async-start | bytes 262144 | tf_op jit(solution)/shard_map/all_to_all | solution.py:113
  118.7 10.1 %all-to-all-done.1 = bf16[128,2,256]{2,1,0:T(2,128)(2,1)S(1)} async-done(((bf16[128,2,256]{2,1,0:T(2,128)(2,1)}), bf16[128,2,256]{2,1,0:T(2,128)(2,1)S(1)}, u32[]{:S(2)}, u32[]{:S(2)}) %all-to-all-start.1) | async-done | bytes 131104 | tf_op jit(solution)/shard_map/all_to_all | solution.py:113
  (97 shorter events, 27.2 us)
Async XLA Ops:
  3.7 52.7 %collective-permute-start.2 = (bf16[1,48,1155]{2,1,0:T(8,128)(2,1)S(1)}, bf16[1,48,1155]{2,1,0:T(8,128)(2,1)S(1)}, u32[]{:S(2)}, u32[]{:S(2)}) collective-permute-start(bf16[1,48,1155]{2,1,0:T(8,128)(2,1)S(1)} %bitcast.125), channel_id=1, source_target_pairs={{0,7},{1,0},{2,1},{3,2},{4,3},{5,4},{6,5},{7,6},{8,15},{9,8},{10,9... | collective-permute-start | bytes 332648 | tf_op jit(solution)/shard_map/ppermute | solution.py:41
  15.9 45.1 %collective-permute-start.3 = (bf16[1,48,1155]{2,1,0:T(8,128)(2,1)S(1)}, bf16[1,48,1155]{2,1,0:T(8,128)(2,1)S(1)}, u32[]{:S(2)}, u32[]{:S(2)}) collective-permute-start(bf16[1,48,1155]{2,1,0:T(8,128)(2,1)S(1)} %bitcast.126), channel_id=1, source_target_pairs={{0,6},{1,7},{2,0},{3,1},{4,2},{5,3},{6,4},{7,5},{8,14},{9,15},{10,... | collective-permute-start | bytes 332648 | tf_op jit(solution)/shard_map/ppermute | solution.py:41
  18.6 50.3 %collective-permute-start.4 = (bf16[1,48,1155]{2,1,0:T(8,128)(2,1)S(1)}, bf16[1,48,1155]{2,1,0:T(8,128)(2,1)S(1)}, u32[]{:S(2)}, u32[]{:S(2)}) collective-permute-start(bf16[1,48,1155]{2,1,0:T(8,128)(2,1)S(1)} %bitcast.127), channel_id=1, source_target_pairs={{0,5},{1,6},{2,7},{3,0},{4,1},{5,2},{6,3},{7,4},{8,13},{9,14},{10,... | collective-permute-start | bytes 332648 | tf_op jit(solution)/shard_map/ppermute | solution.py:41
  20.6 49.0 %collective-permute-start.5 = (bf16[1,48,1155]{2,1,0:T(8,128)(2,1)S(1)}, bf16[1,48,1155]{2,1,0:T(8,128)(2,1)S(1)}, u32[]{:S(2)}, u32[]{:S(2)}) collective-permute-start(bf16[1,48,1155]{2,1,0:T(8,128)(2,1)S(1)} %bitcast.128), channel_id=1, source_target_pairs={{0,4},{1,5},{2,6},{3,7},{4,0},{5,1},{6,2},{7,3},{8,12},{9,13},{10,... | collective-permute-start | bytes 332648 | tf_op jit(solution)/shard_map/ppermute | solution.py:41
  26.2 7.7 %collective-permute-start = (bf16[16,2048]{1,0:T(8,128)(2,1)S(1)}, bf16[16,2048]{1,0:T(8,128)(2,1)S(1)}, u32[]{:S(2)}, u32[]{:S(2)}) collective-permute-start(bf16[16,2048]{1,0:T(8,128)(2,1)S(1)} %get-tuple-element.16), channel_id=1, source_target_pairs={{0,8},{8,16},{16,24},{24,32},{32,40},{40,48},{48,56},{56,64},{64,7... | collective-permute-start | bytes 196616 | tf_op jit(solution)/shard_map/ppermute | solution.py:10
  33.9 4.8 %collective-permute-start.1 = (bf16[16,2048]{1,0:T(8,128)(2,1)S(1)}, bf16[16,2048]{1,0:T(8,128)(2,1)S(1)}, u32[]{:S(2)}, u32[]{:S(2)}) collective-permute-start(bf16[16,2048]{1,0:T(8,128)(2,1)S(1)} %get-tuple-element.17), channel_id=1, source_target_pairs={{8,0},{16,8},{24,16},{32,24},{40,32},{48,40},{56,48},{64,56},{72,6... | collective-permute-start | bytes 196616 | tf_op jit(solution)/shard_map/ppermute | solution.py:10
  38.7 31.6 %collective-permute-start.6 = (bf16[1,48,1155]{2,1,0:T(8,128)(2,1)S(1)}, bf16[1,48,1155]{2,1,0:T(8,128)(2,1)S(1)}, u32[]{:S(2)}, u32[]{:S(2)}) collective-permute-start(bf16[1,48,1155]{2,1,0:T(8,128)(2,1)S(1)} %bitcast.129), channel_id=1, source_target_pairs={{0,3},{1,4},{2,5},{3,6},{4,7},{5,0},{6,1},{7,2},{8,11},{9,12},{10,... | collective-permute-start | bytes 332648 | tf_op jit(solution)/shard_map/ppermute | solution.py:41
  50.7 35.2 %all-to-all-start = ((bf16[8,16,4,262]{3,1,2,0:T(8,128)(2,1)}), bf16[8,16,4,262]{3,1,2,0:T(8,128)(2,1)S(1)}, u32[]{:S(2)}, u32[]{:S(2)}) async-start(bf16[8,16,4,262]{3,1,2,0:T(8,128)(2,1)} %constant_dynamic-update-slice_fusion), calls=%async_computation | async-start | bytes 786432 | tf_op jit(solution)/shard_map/all_to_all | solution.py:107
  56.4 14.5 %collective-permute-start.7 = (bf16[1,48,1155]{2,1,0:T(8,128)(2,1)S(1)}, bf16[1,48,1155]{2,1,0:T(8,128)(2,1)S(1)}, u32[]{:S(2)}, u32[]{:S(2)}) collective-permute-start(bf16[1,48,1155]{2,1,0:T(8,128)(2,1)S(1)} %bitcast.130), channel_id=1, source_target_pairs={{0,2},{1,3},{2,4},{3,5},{4,6},{5,7},{6,0},{7,1},{8,10},{9,11},{10,... | collective-permute-start | bytes 332648 | tf_op jit(solution)/shard_map/ppermute | solution.py:41
  61.0 17.0 %collective-permute-start.8 = (bf16[1,48,1155]{2,1,0:T(8,128)(2,1)S(1)}, bf16[1,48,1155]{2,1,0:T(8,128)(2,1)S(1)}, u32[]{:S(2)}, u32[]{:S(2)}) collective-permute-start(bf16[1,48,1155]{2,1,0:T(8,128)(2,1)S(1)} %bitcast.131), channel_id=1, source_target_pairs={{0,1},{1,2},{2,3},{3,4},{4,5},{5,6},{6,7},{7,0},{8,9},{9,10},{10,1... | collective-permute-start | bytes 332648 | tf_op jit(solution)/shard_map/ppermute | solution.py:41
  85.6 0.7 copy-start
  86.9 8.9 %copy-start.1 = (pred[8,17]{0,1:T(8,128)(4,1)S(1)}, pred[8,17]{0,1:T(8,128)(4,1)}, u32[]{:S(2)}) copy-start(pred[8,17]{0,1:T(8,128)(4,1)} %constant.119) | copy-start | bytes 412
  87.3 7.7 %collective-permute-start.9 = (bf16[128,260]{0,1:T(8,128)(2,1)S(1)}, bf16[128,260]{0,1:T(8,128)(2,1)S(1)}, u32[]{:S(2)}, u32[]{:S(2)}) collective-permute-start(bf16[128,260]{0,1:T(8,128)(2,1)S(1)} %bitcast.136), channel_id=1, source_target_pairs={{0,8},{8,16},{16,24},{24,32},{32,40},{40,48},{48,56},{56,64},{64,7... | collective-permute-start | bytes 199688 | tf_op jit(solution)/shard_map/ppermute | solution.py:10
  98.2 16.3 %all-to-all-start.2 = ((bf16[8,2,2048]{2,1,0:T(2,128)(2,1)}), bf16[8,2,2048]{2,1,0:T(2,128)(2,1)S(1)}, u32[]{:S(2)}, u32[]{:S(2)}) async-start(bf16[8,2,2048]{2,1,0:T(2,128)(2,1)} %reshape.182), calls=%async_computation.2 | async-start | bytes 131072 | tf_op jit(solution)/shard_map/all_to_all | solution.py:122
  114.5 14.3 %all-to-all-start.1 = ((bf16[128,2,256]{2,1,0:T(2,128)(2,1)}), bf16[128,2,256]{2,1,0:T(2,128)(2,1)S(1)}, u32[]{:S(2)}, u32[]{:S(2)}) async-start(bf16[128,2,256]{2,1,0:T(2,128)(2,1)} %copy.147), calls=%async_computation.1 | async-start | bytes 262144 | tf_op jit(solution)/shard_map/all_to_all | solution.py:113

commit v3 on v1

--- a/solution.py
+++ b/solution.py
@@ -32,6 +32,19 @@
     return remap_window(wrapped, table, 0, cycle)
 
 
+def split3(v):
+    hi = lax.reduce_precision(v, exponent_bits=8, mantissa_bits=7)
+    rest = v - hi
+    mid = lax.reduce_precision(rest, exponent_bits=8, mantissa_bits=7)
+    lo = rest - mid
+    return jnp.stack([hi, mid, lo], -1).astype(jnp.bfloat16)
+
+
+def join3(parts):
+    parts = parts.astype(jnp.float32)
+    return (parts[..., 0] + parts[..., 1]) + parts[..., 2]
+
+
 def conv(x, w, stride):
     return lax.conv_general_dilated(
         x,
@@ -43,20 +56,34 @@
     )
 
 
+def column_windows(padded, groups, halo):
+    cycle = padded.shape[-1]
+    block = cycle // groups
+    lead = padded.shape[:-1]
+    left = jnp.roll(padded, halo, axis=-1).reshape(lead + (groups, block))[..., :halo]
+    mid = padded.reshape(lead + (groups, block))
+    right = jnp.roll(padded, -halo, axis=-1).reshape(lead + (groups, block))[..., block - halo :]
+    wins = jnp.concatenate([left, mid, right], axis=-1)
+    return jnp.moveaxis(wins, -2, 0)
+
+
+def pad_to(flat, multiple):
+    extra = (-flat.shape[-1]) % multiple
+    return jnp.pad(flat, [(0, 0)] * (flat.ndim - 1) + [(0, extra)])
+
+
 def per_device(features, top_map, bottom_map, first_weight, first_bias, second_weight, second_bias):
     groups = lax.axis_size("chan")
     me = lax.axis_index("chan")
     x = features[0]
+    chans = x.shape[0]
     rows = x.shape[1]
     cycle = x.shape[2]
     block = cycle // groups
     upper_map = top_map[0]
     lower_map = bottom_map[0]
-
-    w1 = lax.all_gather(first_weight, "chan", axis=0, tiled=True)
-    b1 = lax.all_gather(first_bias, "chan", axis=0, tiled=True)
-    w2 = lax.all_gather(second_weight, "chan", axis=0, tiled=True)
-    b2 = lax.all_gather(second_bias, "chan", axis=0, tiled=True)
+    n1 = first_weight.shape[0]
+    n2 = second_weight.shape[0]
 
     above_src = shifted(x[:, rows - 1, :], "space", 1)
     below_src = shifted(x[:, 0, :], "space", -1)
@@ -66,24 +93,50 @@
 
     halo = 3
     width = block + 2 * halo
-    ext = jnp.concatenate([padded[..., cycle - halo :], padded, padded[..., :halo]], axis=-1)
-    sends = jnp.stack([ext[..., j * block : j * block + width] for j in range(groups)], 0)
-    got = lax.all_to_all(sends, "chan", 0, 0, tiled=True)
-    window = got.reshape((-1,) + got.shape[2:])
+    wins = column_windows(padded, groups, halo).reshape(groups, -1)
+    feat_len = wins.shape[1]
+
+    flat_w = jnp.concatenate(
+        [first_weight.reshape(n1, -1), second_weight.reshape(n2, -1)], axis=0
+    )
+    taps = flat_w.shape[1]
+    packed_w = jnp.concatenate(
+        [flat_w, split3(jnp.concatenate([first_bias, second_bias]))], axis=1
+    ).reshape(1, -1)
+    sends = jnp.concatenate([wins, jnp.broadcast_to(packed_w, (groups,) + packed_w.shape[1:])], 1)
+    got = lax.all_to_all(pad_to(sends, 1024), "chan", 0, 0, tiled=True)
+
+    window = got[:, :feat_len].reshape(groups * chans, rows + 2, width)
+    every = got[:, feat_len : feat_len + packed_w.shape[1]].reshape(groups, n1 + n2, taps + 3)
+    w1 = every[:, :n1, :taps].reshape((-1,) + first_weight.shape[1:])
+    w2 = every[:, n1:, :taps].reshape((-1,) + second_weight.shape[1:])
+    b1 = join3(every[:, :n1, taps:]).reshape(-1)
+    b2 = join3(every[:, n1:, taps:]).reshape(-1)
 
     pre1 = conv(window[None], w1, (1, 1))
     hidden_win = jax.nn.gelu(pre1 + b1[None, :, None, None]).astype(jnp.bfloat16)[0]
-
-    hidden_out = lax.all_to_all(
-        hidden_win[:, :, halo - 1 : halo - 1 + block], "chan", 0, 2, tiled=True
-    )
 
     rim_src = shifted(hidden_win[:, rows - 1, :], "space", 1)
     rim = remap_window(rim_src, upper_map, me * block - 1, block + 2)
     stacked = jnp.concatenate([rim[:, None], hidden_win[:, :, 1 : block + 3]], axis=1)
     pre2 = conv(stacked[None], w2, (1, 2))
     coarse_win = jax.nn.gelu(pre2 + b2[None, :, None, None]).astype(jnp.bfloat16)[0]
-    coarse_out = lax.all_to_all(coarse_win, "chan", 0, 2, tiled=True)
+
+    hidden_part = hidden_win[:, :, halo - 1 : halo - 1 + block].reshape(groups, -1)
+    coarse_part = coarse_win.reshape(groups, -1)
+    back = lax.all_to_all(
+        jnp.concatenate([hidden_part, coarse_part], 1), "chan", 0, 0, tiled=True
+    )
+    h_len = hidden_part.shape[1]
+    hidden_out = back[:, :h_len].reshape((groups, chans, rows, block))
+    hidden_out = jnp.moveaxis(hidden_out, 0, 2).reshape(chans, rows, cycle)
+    coarse_shape = coarse_win.shape
+    coarse_out = back[:, h_len:].reshape(
+        (groups, coarse_shape[0] // groups) + coarse_shape[1:]
+    )
+    coarse_out = jnp.moveaxis(coarse_out, 0, 2).reshape(
+        (coarse_shape[0] // groups, coarse_shape[1], groups * coarse_shape[2])
+    )
     return hidden_out[None], coarse_out[None]
 
 

time: 200 us -> 97.9 us (0.49)
  the two profiles are of different devices: /device:TPU:64 before, /device:TPU:81 now
where the time goes in v3:
time: 97.9 us; the launch traced here: 97.4 us
  waiting for transfers between devices  32.8 us (34%)
  starting transfers between devices  23.8 us (24%)
  local copies, waits for them, and re-layouts  16.2 us (17%)
  blocking collectives  14.9 us (15%)
  other arithmetic  7.54 us (8%)
  between operations  1.25 us (1%)
    all_to_all x1, waiting for transfers between devices, per_device(): got = lax.all_to_all(pad_to(sends, 1024), 'chan', 0, 0, tiled=True)  32.3 us
    all_to_all x1, blocking collectives, per_device(): lax.all_to_all(jnp.concatenate([hidden_part, coarse_part], 1), 'chan', 0,...  14.9 us
    ppermute x3, starting transfers between devices, shifted(): return lax.ppermute(array, axis, pairs)  12.1 us
    all_to_all x1, starting transfers between devices, per_device(): got = lax.all_to_all(pad_to(sends, 1024), 'chan', 0, 0, tiled=True)  11.7 us
    unnamed x27, local copies, waits for them, and re-layouts  7.67 us
    reshape x1, local copies, waits for them, and re-layouts, per_device(): got[:, feat_len:feat_len + packed_w.shape[1]]  1.98 us
  transfers between devices with their start and end apart: 4, of which 2 were waited for; matrix products, arithmetic and copies ran while one was open for 6% of the time, Pallas kernels for 0%

profile of v3, /device:TPU:81, one launch (start us, length us, event | category | flops | bytes accessed | tf_op | source)
XLA Modules:
  0.0 97.4 jit_solution(11430495276533701856)
XLA Ops:
  0.6 1.0 %copy.191 = bf16[1,16,2,2048]{3,1,2,0:T(8,128)(2,1)S(1)} copy(bf16[1,16,2,2048]{3,2,1,0:T(2,128)(2,1)} %param.7) | data formatting | bytes 262144 | tf_op args[0]
  1.7 3.8 %collective-permute-start = (bf16[16,2048]{1,0:T(8,128)(2,1)S(1)}, bf16[16,2048]{1,0:T(8,128)(2,1)S(1)}, u32[]{:S(2)}, u32[]{:S(2)}) collective-permute-start(bf16[16,2048]{1,0:T(8,128)(2,1)S(1)} %get-tuple-element.10), channel_id=1, source_target_pairs={{0,8},{8,16},{16,24},{24,32},{32,40},{40,48},{48,56},{56,64},{64,7... | collective-permute-start | bytes 196616 | tf_op jit(solution)/shard_map/ppermute | solution.py:10
  5.4 1.9 %collective-permute-start.1 = (bf16[16,2048]{1,0:T(8,128)(2,1)S(1)}, bf16[16,2048]{1,0:T(8,128)(2,1)S(1)}, u32[]{:S(2)}, u32[]{:S(2)}) collective-permute-start(bf16[16,2048]{1,0:T(8,128)(2,1)S(1)} %get-tuple-element.11), channel_id=1, source_target_pairs={{8,0},{16,8},{24,16},{32,24},{40,32},{48,40},{56,48},{64,56},{72,6... | collective-permute-start | bytes 196616 | tf_op jit(solution)/shard_map/ppermute | solution.py:10
  7.4 0.7 fusion.70
  8.1 0.7 fusion.69
  8.8 0.9 copy.142
  9.8 0.8 copy.141
  10.6 0.8 fusion.83
  14.1 1.3 %maximum_bitcast_fusion = bf16[8,16,4,262]{3,2,1,0:T(4,128)(2,1)S(1)} fusion(bf16[16,4,8,3]{3,1,0,2:T(4,128)(2,1)S(1)} %copy.167, bf16[16,1,8,256]{3,1,0,2:T(2,128)(2,1)S(1)} %copy.139, bf16[16,2,8,256]{3,1,0,2:T(2,128)(2,1)S(1)} %copy.138, bf16[16,1,8,256]{3,1,0,2:T(2,128)(2,1)S(1)} %copy.137, bf16[16,4,8,3]{3,1,0,2:T(4,128)(2,1)S(1)} %copy.166), kind=kLoop, calls=%fused_computation.13 | loop fusion | flops 1341440 | bytes 536576 | tf_op jit(solution)/shard_map/transpose | solution.py:67
  15.4 0.5 reshape.172
  16.1 0.5 broadcast.130
  16.6 1.5 %reduce.4 = bf16[8,72704]{1,0:T(8,128)(2,1)S(1)} reduce(bf16[8,1,72704]{2,0,1:T(8,128)(2,1)S(1)} %pad_bitcast_fusion, bf16[]{:T(256)} %broadcast.130), dimensions={1}, to_apply=%copy.146.reduce_sub_computation | reduce | bytes 2326530 | tf_op jit(solution)/shard_map/all_to_all | solution.py:107
  18.2 2.0 %reshape.208 = bf16[8,2,36352]{2,1,0:T(2,128)(2,1)} reshape(bf16[8,72704]{1,0:T(8,128)(2,1)S(1)} %reduce.4) | data formatting | bytes 2326528
  20.2 11.7 %all-to-all-start = ((bf16[8,2,36352]{2,1,0:T(2,128)(2,1)}), bf16[8,2,36352]{2,1,0:T(2,128)(2,1)S(1)}, u32[]{:S(2)}, u32[]{:S(2)}) async-start(bf16[8,2,36352]{2,1,0:T(2,128)(2,1)} %reshape.208), calls=%async_computation | async-start | bytes 2326528 | tf_op jit(solution)/shard_map/all_to_all | solution.py:107
  32.0 32.3 %all-to-all-done = bf16[8,2,36352]{2,1,0:T(2,128)(2,1)S(1)} async-done(((bf16[8,2,36352]{2,1,0:T(2,128)(2,1)}), bf16[8,2,36352]{2,1,0:T(2,128)(2,1)S(1)}, u32[]{:S(2)}, u32[]{:S(2)}) %all-to-all-start) | async-done | bytes 1163296 | tf_op jit(solution)/shard_map/all_to_all | solution.py:107
  64.3 0.9 reshape.209
  65.7 2.0 %reshape.175 = bf16[8,48,1155]{2,1,0:T(8,128)(2,1)S(1)} reshape(bf16[8,55440]{1,0:T(8,128)(2,1)S(1)} %slice.168) | data formatting | bytes 1774080 | tf_op jit(solution)/shard_map/reshape | solution.py:110
  68.2 0.7 reshape.195
  69.4 0.6 fusion.23
  70.8 6.4 %collective-permute-start.2 = (bf16[128,260]{0,1:T(8,128)(2,1)S(1)}, bf16[128,260]{0,1:T(8,128)(2,1)S(1)}, u32[]{:S(2)}, u32[]{:S(2)}) collective-permute-start(bf16[128,260]{0,1:T(8,128)(2,1)S(1)} %bitcast.113), channel_id=1, source_target_pairs={{0,8},{8,16},{16,24},{24,32},{32,40},{40,48},{48,56},{56,64},{64,7... | collective-permute-start | bytes 199688 | tf_op jit(solution)/shard_map/ppermute | solution.py:10
  79.8 0.8 reduce.5
  80.7 14.9 %all_to_all.24 = bf16[8,2,6144]{2,1,0:T(2,128)(2,1)S(1)} all-to-all(bf16[8,2,6144]{2,1,0:T(2,128)(2,1)S(1)} %reshape.210), channel_id=1, replica_groups=mesh['space'=64,'chan'=8] {'chan'}, dimensions={0} | all-to-all | bytes 393216 | tf_op jit(solution)/shard_map/all_to_all | solution.py:127
  96.0 0.7 broadcast_in_dim_reshape.12
  96.7 0.7 broadcast_in_dim_reshape.13
  (94 shorter events, 8.1 us)
Async XLA Ops:
  0.6 10.8 %copy-start.1 = (bf16[1,16,2,2048]{3,2,1,0:T(2,128)(2,1)S(1)}, bf16[1,16,2,2048]{3,2,1,0:T(2,128)(2,1)}, u32[]{:S(2)}) copy-start(bf16[1,16,2,2048]{3,2,1,0:T(2,128)(2,1)} %param.7) | copy-start | bytes 393220
  1.7 10.7 %collective-permute-start = (bf16[16,2048]{1,0:T(8,128)(2,1)S(1)}, bf16[16,2048]{1,0:T(8,128)(2,1)S(1)}, u32[]{:S(2)}, u32[]{:S(2)}) collective-permute-start(bf16[16,2048]{1,0:T(8,128)(2,1)S(1)} %get-tuple-element.10), channel_id=1, source_target_pairs={{0,8},{8,16},{16,24},{24,32},{32,40},{40,48},{48,56},{56,64},{64,7... | collective-permute-start | bytes 196616 | tf_op jit(solution)/shard_map/ppermute | solution.py:10
  5.4 7.0 %collective-permute-start.1 = (bf16[16,2048]{1,0:T(8,128)(2,1)S(1)}, bf16[16,2048]{1,0:T(8,128)(2,1)S(1)}, u32[]{:S(2)}, u32[]{:S(2)}) collective-permute-start(bf16[16,2048]{1,0:T(8,128)(2,1)S(1)} %get-tuple-element.11), channel_id=1, source_target_pairs={{8,0},{16,8},{24,16},{32,24},{40,32},{48,40},{56,48},{64,56},{72,6... | collective-permute-start | bytes 196616 | tf_op jit(solution)/shard_map/ppermute | solution.py:10
  20.2 11.7 %copy-start.2 = (s32[1,2048]{1,0:T(1,128)S(1)}, s32[1,2048]{1,0:T(1,128)}, u32[]{:S(2)}) copy-start(s32[1,2048]{1,0:T(1,128)} %param.8) | copy-start | bytes 24580
  20.2 44.2 %all-to-all-start = ((bf16[8,2,36352]{2,1,0:T(2,128)(2,1)}), bf16[8,2,36352]{2,1,0:T(2,128)(2,1)S(1)}, u32[]{:S(2)}, u32[]{:S(2)}) async-start(bf16[8,2,36352]{2,1,0:T(2,128)(2,1)} %reshape.208), calls=%async_computation | async-start | bytes 2326528 | tf_op jit(solution)/shard_map/all_to_all | solution.py:107
  68.2 1.2 %copy-start.3 = (pred[8,33]{0,1:T(8,128)(4,1)S(1)}, pred[8,33]{0,1:T(8,128)(4,1)}, u32[]{:S(2)}) copy-start(pred[8,33]{0,1:T(8,128)(4,1)} %constant.109) | copy-start | bytes 796
  70.2 0.7 copy-start
  70.8 6.9 %slice-start.1 = ((bf16[128,2,260]{0,1,2:T(2,128)(2,1)}), bf16[128,2,256]{0,1,2:T(2,128)(2,1)S(1)}, s32[]{:S(2)}) async-start(bf16[128,2,260]{0,1,2:T(2,128)(2,1)} %copy-done), calls=%async_computation.3 | async-start | bytes 262144 | tf_op jit(solution)/shard_map/slice | solution.py:125
  70.8 7.8 %slice-start = ((bf16[128,2,260]{0,1,2:T(2,128)(2,1)}), bf16[128,2,258]{0,1,2:T(2,128)(2,1)S(1)}, s32[]{:S(2)}) async-start(bf16[128,2,260]{0,1,2:T(2,128)(2,1)} %copy-done), calls=%async_computation.2 | async-start | bytes 264192 | tf_op jit(solution)/shard_map/slice | solution.py:121
  70.8 7.5 %collective-permute-start.2 = (bf16[128,260]{0,1:T(8,128)(2,1)S(1)}, bf16[128,260]{0,1:T(8,128)(2,1)S(1)}, u32[]{:S(2)}, u32[]{:S(2)}) collective-permute-start(bf16[128,260]{0,1:T(8,128)(2,1)S(1)} %bitcast.113), channel_id=1, source_target_pairs={{0,8},{8,16},{16,24},{24,32},{32,40},{40,48},{48,56},{56,64},{64,7... | collective-permute-start | bytes 199688 | tf_op jit(solution)/shard_map/ppermute | solution.py:10
  77.9 1.3 %copy-start.4 = (pred[8,17]{0,1:T(8,128)(4,1)S(1)}, pred[8,17]{0,1:T(8,128)(4,1)}, u32[]{:S(2)}) copy-start(pred[8,17]{0,1:T(8,128)(4,1)} %constant.110) | copy-start | bytes 412

commit v4 on v3

--- a/solution.py
+++ b/solution.py
@@ -85,15 +85,9 @@
     n1 = first_weight.shape[0]
     n2 = second_weight.shape[0]
 
-    above_src = shifted(x[:, rows - 1, :], "space", 1)
-    below_src = shifted(x[:, 0, :], "space", -1)
-    above = remap_full(above_src, upper_map)
-    below = remap_full(below_src, lower_map)
-    padded = jnp.concatenate([above[:, None], x, below[:, None]], axis=1)
-
     halo = 3
     width = block + 2 * halo
-    wins = column_windows(padded, groups, halo).reshape(groups, -1)
+    wins = column_windows(x, groups, halo + 1).reshape(groups, -1)
     feat_len = wins.shape[1]
 
     flat_w = jnp.concatenate(
@@ -106,12 +100,18 @@
     sends = jnp.concatenate([wins, jnp.broadcast_to(packed_w, (groups,) + packed_w.shape[1:])], 1)
     got = lax.all_to_all(pad_to(sends, 1024), "chan", 0, 0, tiled=True)
 
-    window = got[:, :feat_len].reshape(groups * chans, rows + 2, width)
+    tile = got[:, :feat_len].reshape(groups * chans, rows, width + 2)
     every = got[:, feat_len : feat_len + packed_w.shape[1]].reshape(groups, n1 + n2, taps + 3)
     w1 = every[:, :n1, :taps].reshape((-1,) + first_weight.shape[1:])
     w2 = every[:, n1:, :taps].reshape((-1,) + second_weight.shape[1:])
     b1 = join3(every[:, :n1, taps:]).reshape(-1)
     b2 = join3(every[:, n1:, taps:]).reshape(-1)
+
+    above_src = shifted(tile[:, rows - 1, :], "space", 1)
+    below_src = shifted(tile[:, 0, :], "space", -1)
+    above = remap_window(above_src, upper_map, me * block - halo, width)
+    below = remap_window(below_src, lower_map, me * block - halo, width)
+    window = jnp.concatenate([above[:, None], tile[:, :, 1 : width + 1], below[:, None]], axis=1)
 
     pre1 = conv(window[None], w1, (1, 1))
     hidden_win = jax.nn.gelu(pre1 + b1[None, :, None, None]).astype(jnp.bfloat16)[0]

time: 97.9 us -> 95.8 us (0.979)
  the two profiles are of different devices: /device:TPU:81 before, /device:TPU:64 now
where the time goes in v4:
time: 95.8 us; the launch traced here: 95.4 us
  waiting for transfers between devices  36 us (38%)
  starting transfers between devices  21.6 us (23%)
  local copies, waits for them, and re-layouts  16.8 us (18%)
  blocking collectives  13.3 us (14%)
  other arithmetic  5.45 us (6%)
  between operations  1.31 us (1%)
    all_to_all x1, waiting for transfers between devices, per_device(): got = lax.all_to_all(pad_to(sends, 1024), 'chan', 0, 0, tiled=True)  30.1 us
    all_to_all x1, blocking collectives, per_device(): lax.all_to_all(jnp.concatenate([hidden_part, coarse_part], 1), 'chan', 0,...  13.3 us
    all_to_all x1, starting transfers between devices, per_device(): got = lax.all_to_all(pad_to(sends, 1024), 'chan', 0, 0, tiled=True)  11.8 us
    ppermute x3, starting transfers between devices, shifted(): return lax.ppermute(array, axis, pairs)  9.77 us
    ppermute x3, waiting for transfers between devices, shifted(): return lax.ppermute(array, axis, pairs)  5.89 us
    unnamed x30, local copies, waits for them, and re-layouts  4.11 us
    slice x3, local copies, waits for them, and re-layouts, column_windows(): jnp.roll(padded, halo, axis=-1).reshape(lead + (groups, block))[..., :halo]  2.07 us
    reshape x1, local copies, waits for them, and re-layouts, per_device(): got[:, feat_len:feat_len + packed_w.shape[1]]  1.98 us
  transfers between devices with their start and end apart: 4, of which 3 were waited for; matrix products, arithmetic and copies ran while one was open for 2% of the time, Pallas kernels for 0%

profile of v4, /device:TPU:64, one launch (start us, length us, event | category | flops | bytes accessed | tf_op | source)
XLA Modules:
  0.0 95.4 jit_solution(7141124271016563487)
XLA Ops:
  0.7 1.3 %fusion.93 = (bf16[16,2,2044]{2,1,0:T(2,128)(2,1)S(1)}, bf16[16,2,2044]{2,1,0:T(2,128)(2,1)S(1)}) fusion(bf16[16,2,2048]{2,1,0:T(2,128)(2,1)} %bitcast.74), kind=kLoop, calls=%fused_computation.131 | loop fusion | bytes 523264 | tf_op jit(solution)/shard_map/jit(_roll_static)/slice | solution.py:63
  1.9 0.8 fusion.92
  2.7 1.0 %reshape_squeeze.6 = bf16[16,2,8,256]{3,2,1,0:T(8,128)(2,1)S(1)} reshape(bf16[1,16,2,2048]{3,2,1,0:T(2,128)(2,1)} %param.7) | data formatting | bytes 262144 | tf_op jit(solution)/shard_map/reshape;squeeze | solution.py:64
  4.6 0.5 maximum_bitcast_fusion.2
  6.6 0.5 broadcast.148
  7.1 1.4 %reduce.4 = bf16[8,64512]{1,0:T(8,128)(2,1)S(1)} reduce(bf16[8,1,64512]{2,0,1:T(8,128)(2,1)S(1)} %pad_bitcast_fusion, bf16[]{:T(256)} %broadcast.148), dimensions={1}, to_apply=%copy.193.reduce_sub_computation | reduce | bytes 2064386 | tf_op jit(solution)/shard_map/all_to_all | solution.py:101
  8.5 1.8 %reshape.205 = bf16[8,2,32256]{2,1,0:T(2,128)(2,1)} reshape(bf16[8,64512]{1,0:T(8,128)(2,1)S(1)} %reduce.4) | data formatting | bytes 2064384
  10.4 11.8 %all-to-all-start = ((bf16[8,2,32256]{2,1,0:T(2,128)(2,1)}), bf16[8,2,32256]{2,1,0:T(2,128)(2,1)S(1)}, u32[]{:S(2)}, u32[]{:S(2)}) async-start(bf16[8,2,32256]{2,1,0:T(2,128)(2,1)} %reshape.205), calls=%async_computation | async-start | bytes 2064384 | tf_op jit(solution)/shard_map/all_to_all | solution.py:101
  22.6 30.1 %all-to-all-done = bf16[8,2,32256]{2,1,0:T(2,128)(2,1)S(1)} async-done(((bf16[8,2,32256]{2,1,0:T(2,128)(2,1)}), bf16[8,2,32256]{2,1,0:T(2,128)(2,1)S(1)}, u32[]{:S(2)}, u32[]{:S(2)}) %all-to-all-start) | async-done | bytes 1032224 | tf_op jit(solution)/shard_map/all_to_all | solution.py:101
  52.7 0.9 reshape.206
  53.9 0.4 reshape.171
  54.6 1.0 %slice.159 = bf16[128,2,262]{2,1,0:T(2,128)(2,1)} slice(bf16[128,2,264]{2,1,0:T(2,128)(2,1)S(1)} %reshape.171), slice={[0:128], [0:2], [1:263]} | slice | bytes 268288 | tf_op jit(solution)/shard_map/slice | solution.py:114
  55.7 2.0 %reshape.172 = bf16[8,48,1155]{2,1,0:T(8,128)(2,1)S(1)} reshape(bf16[8,55440]{1,0:T(8,128)(2,1)S(1)} %slice.165) | data formatting | bytes 1774080 | tf_op jit(solution)/shard_map/reshape | solution.py:104
  58.0 1.9 %collective-permute-start = (bf16[128,264]{0,1:T(8,128)(2,1)S(1)}, bf16[128,264]{0,1:T(8,128)(2,1)S(1)}, u32[]{:S(2)}, u32[]{:S(2)}) collective-permute-start(bf16[128,264]{0,1:T(8,128)(2,1)S(1)} %bitcast.84), channel_id=1, source_target_pairs={{0,8},{8,16},{16,24},{24,32},{32,40},{40,48},{48,56},{56,64},{64,7... | collective-permute-start | bytes 202760 | tf_op jit(solution)/shard_map/ppermute | solution.py:10
  60.0 5.8 %collective-permute-start.1 = (bf16[128,264]{0,1:T(8,128)(2,1)S(1)}, bf16[128,264]{0,1:T(8,128)(2,1)S(1)}, u32[]{:S(2)}, u32[]{:S(2)}) collective-permute-start(bf16[128,264]{0,1:T(8,128)(2,1)S(1)} %bitcast.83), channel_id=1, source_target_pairs={{8,0},{16,8},{24,16},{32,24},{40,32},{48,40},{56,48},{64,56},{72,6... | collective-permute-start | bytes 202760 | tf_op jit(solution)/shard_map/ppermute | solution.py:10
  66.8 0.9 collective-permute-done.1
  68.1 0.7 maximum_bitcast_fusion
  69.3 0.6 fusion.23
  70.3 2.1 %collective-permute-start.2 = (bf16[128,260]{0,1:T(8,128)(2,1)S(1)}, bf16[128,260]{0,1:T(8,128)(2,1)S(1)}, u32[]{:S(2)}, u32[]{:S(2)}) collective-permute-start(bf16[128,260]{0,1:T(8,128)(2,1)S(1)} %bitcast.82), channel_id=1, source_target_pairs={{0,8},{8,16},{16,24},{24,32},{32,40},{40,48},{48,56},{56,64},{64,7... | collective-permute-start | bytes 199688 | tf_op jit(solution)/shard_map/ppermute | solution.py:10
  73.1 4.9 %collective-permute-done.2 = bf16[128,260]{0,1:T(8,128)(2,1)S(1)} collective-permute-done((bf16[128,260]{0,1:T(8,128)(2,1)S(1)}, bf16[128,260]{0,1:T(8,128)(2,1)S(1)}, u32[]{:S(2)}, u32[]{:S(2)}) %collective-permute-start.2) | collective-permute-done | bytes 66592 | tf_op jit(solution)/shard_map/ppermute | solution.py:10
  79.5 0.8 reduce.5
  80.4 13.3 %all_to_all.24 = bf16[8,2,6144]{2,1,0:T(2,128)(2,1)S(1)} all-to-all(bf16[8,2,6144]{2,1,0:T(2,128)(2,1)S(1)} %reshape.207), channel_id=1, replica_groups=mesh['space'=64,'chan'=8] {'chan'}, dimensions={0} | all-to-all | bytes 393216 | tf_op jit(solution)/shard_map/all_to_all | solution.py:127
  94.1 0.7 broadcast_in_dim_reshape.8
  94.8 0.7 broadcast_in_dim_reshape.9
  (99 shorter events, 8.3 us)
Async XLA Ops:
  0.6 4.7 %copy-start.6 = (f32[16]{0:T(128)S(1)}, f32[16]{0:T(128)}, u32[]{:S(2)}) copy-start(f32[16]{0:T(128)} %param.11) | copy-start | bytes 196
  0.6 4.7 %copy-start.5 = (f32[32]{0:T(128)S(1)}, f32[32]{0:T(128)}, u32[]{:S(2)}) copy-start(f32[32]{0:T(128)} %param.13) | copy-start | bytes 388
  0.7 5.1 %copy-start.1 = (bf16[32,3,3,128]{3,0,2,1:T(8,128)(2,1)S(1)}, bf16[32,3,3,128]{3,0,2,1:T(8,128)(2,1)}, u32[]{:S(2)}) copy-start(bf16[32,3,3,128]{3,0,2,1:T(8,128)(2,1)} %param.12) | copy-start | bytes 221188
  0.7 5.2 %copy-start.2 = (bf16[16,3,3,128]{3,0,2,1:T(8,128)(2,1)S(1)}, bf16[16,3,3,128]{3,0,2,1:T(8,128)(2,1)}, u32[]{:S(2)}) copy-start(bf16[16,3,3,128]{3,0,2,1:T(8,128)(2,1)} %param.10) | copy-start | bytes 110596
  8.5 13.7 %copy-start.3 = (s32[1,2048]{1,0:T(1,128)S(1)}, s32[1,2048]{1,0:T(1,128)}, u32[]{:S(2)}) copy-start(s32[1,2048]{1,0:T(1,128)} %param.8) | copy-start | bytes 24580
  8.5 13.8 %copy-start.4 = (s32[1,2048]{1,0:T(1,128)S(1)}, s32[1,2048]{1,0:T(1,128)}, u32[]{:S(2)}) copy-start(s32[1,2048]{1,0:T(1,128)} %param.9) | copy-start | bytes 24580
  10.4 42.3 %all-to-all-start = ((bf16[8,2,32256]{2,1,0:T(2,128)(2,1)}), bf16[8,2,32256]{2,1,0:T(2,128)(2,1)S(1)}, u32[]{:S(2)}, u32[]{:S(2)}) async-start(bf16[8,2,32256]{2,1,0:T(2,128)(2,1)} %reshape.205), calls=%async_computation | async-start | bytes 2064384 | tf_op jit(solution)/shard_map/all_to_all | solution.py:101
  57.8 10.3 %copy-start = (bf16[128,2,262]{2,1,0:T(2,128)(2,1)S(1)}, bf16[128,2,262]{2,1,0:T(2,128)(2,1)}, u32[]{:S(2)}) copy-start(bf16[128,2,262]{2,1,0:T(2,128)(2,1)} %slice.159) | copy-start | bytes 402436
  58.0 8.4 %collective-permute-start = (bf16[128,264]{0,1:T(8,128)(2,1)S(1)}, bf16[128,264]{0,1:T(8,128)(2,1)S(1)}, u32[]{:S(2)}, u32[]{:S(2)}) collective-permute-start(bf16[128,264]{0,1:T(8,128)(2,1)S(1)} %bitcast.84), channel_id=1, source_target_pairs={{0,8},{8,16},{16,24},{24,32},{32,40},{40,48},{48,56},{56,64},{64,7... | collective-permute-start | bytes 202760 | tf_op jit(solution)/shard_map/ppermute | solution.py:10
  60.0 7.7 %collective-permute-start.1 = (bf16[128,264]{0,1:T(8,128)(2,1)S(1)}, bf16[128,264]{0,1:T(8,128)(2,1)S(1)}, u32[]{:S(2)}, u32[]{:S(2)}) collective-permute-start(bf16[128,264]{0,1:T(8,128)(2,1)S(1)} %bitcast.83), channel_id=1, source_target_pairs={{8,0},{16,8},{24,16},{32,24},{40,32},{48,40},{56,48},{64,56},{72,6... | collective-permute-start | bytes 202760 | tf_op jit(solution)/shard_map/ppermute | solution.py:10
  66.4 3.0 %copy-start.7 = (pred[8,33]{0,1:T(8,128)(4,1)S(1)}, pred[8,33]{0,1:T(8,128)(4,1)}, u32[]{:S(2)}) copy-start(pred[8,33]{0,1:T(8,128)(4,1)} %constant.117) | copy-start | bytes 796
  70.1 8.7 %copy-start.8 = (pred[8,17]{0,1:T(8,128)(4,1)S(1)}, pred[8,17]{0,1:T(8,128)(4,1)}, u32[]{:S(2)}) copy-start(pred[8,17]{0,1:T(8,128)(4,1)} %constant.118) | copy-start | bytes 412
  70.3 7.8 %collective-permute-start.2 = (bf16[128,260]{0,1:T(8,128)(2,1)S(1)}, bf16[128,260]{0,1:T(8,128)(2,1)S(1)}, u32[]{:S(2)}, u32[]{:S(2)}) collective-permute-start(bf16[128,260]{0,1:T(8,128)(2,1)S(1)} %bitcast.82), channel_id=1, source_target_pairs={{0,8},{8,16},{16,24},{24,32},{32,40},{40,48},{48,56},{56,64},{64,7... | collective-permute-start | bytes 199688 | tf_op jit(solution)/shard_map/ppermute | solution.py:10

commit v5 on v4

--- a/solution.py
+++ b/solution.py
@@ -107,16 +107,28 @@
     b1 = join3(every[:, :n1, taps:]).reshape(-1)
     b2 = join3(every[:, n1:, taps:]).reshape(-1)
 
-    above_src = shifted(tile[:, rows - 1, :], "space", 1)
+    prior_lower_map = shifted(lower_map, "space", 1)
+    prior = shifted(tile, "space", 1)
     below_src = shifted(tile[:, 0, :], "space", -1)
-    above = remap_window(above_src, upper_map, me * block - halo, width)
-    below = remap_window(below_src, lower_map, me * block - halo, width)
-    window = jnp.concatenate([above[:, None], tile[:, :, 1 : width + 1], below[:, None]], axis=1)
+    start = me * block - halo
+    above = remap_window(prior[:, rows - 1, :], upper_map, start, width)
+    below = remap_window(below_src, lower_map, start, width)
+    prior_below = remap_window(tile[:, 0, :], prior_lower_map, start, width)
+    inner = tile[:, :, 1 : width + 1]
+    prior_inner = prior[:, :, 1 : width + 1]
+    window = jnp.stack(
+        [
+            jnp.concatenate([above[:, None], inner, below[:, None]], axis=1),
+            jnp.concatenate([prior_inner, prior_below[:, None], prior_below[:, None]], axis=1),
+        ],
+        0,
+    )
 
-    pre1 = conv(window[None], w1, (1, 1))
-    hidden_win = jax.nn.gelu(pre1 + b1[None, :, None, None]).astype(jnp.bfloat16)[0]
-
-    rim_src = shifted(hidden_win[:, rows - 1, :], "space", 1)
+    pre1 = conv(window, w1, (1, 1))
+    both = jax.nn.gelu(pre1 + b1[None, :, None, None]).astype(jnp.bfloat16)
+    hidden_win = both[0]
+    has_prior = lax.axis_index("space") > 0
+    rim_src = jnp.where(has_prior, both[1, :, 0, :], jnp.zeros_like(both[1, :, 0, :]))
     rim = remap_window(rim_src, upper_map, me * block - 1, block + 2)
     stacked = jnp.concatenate([rim[:, None], hidden_win[:, :, 1 : block + 3]], axis=1)
     pre2 = conv(stacked[None], w2, (1, 2))

time: 95.8 us -> 93.9 us (0.980)
  the two profiles are of different devices: /device:TPU:64 before, /device:TPU:89 now
where the time goes in v5:
time: 93.9 us; the launch traced here: 93.5 us
  waiting for transfers between devices  26.3 us (28%)
  starting transfers between devices  25.5 us (27%)
  local copies, waits for them, and re-layouts  19.2 us (20%)
  blocking collectives  12.1 us (13%)
  other arithmetic  7.66 us (8%)
  between operations  1.42 us (2%)
  matrix products  1.32 us (1%)
    all_to_all x1, waiting for transfers between devices, per_device(): got = lax.all_to_all(pad_to(sends, 1024), 'chan', 0, 0, tiled=True)  23.1 us
    ppermute x3, starting transfers between devices, shifted(): return lax.ppermute(array, axis, pairs)  13.8 us
    all_to_all x1, blocking collectives, per_device(): lax.all_to_all(jnp.concatenate([hidden_part, coarse_part], 1), 'chan', 0,...  12.1 us
    all_to_all x1, starting transfers between devices, per_device(): got = lax.all_to_all(pad_to(sends, 1024), 'chan', 0, 0, tiled=True)  11.7 us
    unnamed x34, local copies, waits for them, and re-layouts  4.82 us
    ppermute x3, waiting for transfers between devices, shifted(): return lax.ppermute(array, axis, pairs)  3.12 us
    slice x3, local copies, waits for them, and re-layouts, column_windows(): jnp.roll(padded, halo, axis=-1).reshape(lead + (groups, block))[..., :halo]  2.04 us
    another operation x3, other arithmetic, per_device(): jnp.stack([jnp.concatenate([above[:, None], inner, below[:, None]], axis=...  2.04 us
  transfers between devices with their start and end apart: 4, of which 3 were waited for; matrix products, arithmetic and copies ran while one was open for 6% of the time, Pallas kernels for 0%

profile of v5, /device:TPU:89, one launch (start us, length us, event | category | flops | bytes accessed | tf_op | source)
XLA Modules:
  0.0 93.5 jit_solution(106549272644144354)
XLA Ops:
  0.6 1.2 %fusion.88 = (bf16[16,2,2044]{2,1,0:T(2,128)(2,1)S(1)}, bf16[16,2,2044]{2,1,0:T(2,128)(2,1)S(1)}) fusion(bf16[16,2,2048]{2,1,0:T(2,128)(2,1)} %bitcast.84), kind=kLoop, calls=%fused_computation.137 | loop fusion | bytes 523264 | tf_op jit(solution)/shard_map/jit(_roll_static)/slice | solution.py:63
  1.9 0.8 fusion.87
  2.7 1.0 %reshape_squeeze.6 = bf16[16,2,8,256]{3,2,1,0:T(8,128)(2,1)S(1)} reshape(bf16[1,16,2,2048]{3,2,1,0:T(2,128)(2,1)} %param.7) | data formatting | bytes 262144 | tf_op jit(solution)/shard_map/reshape;squeeze | solution.py:64
  7.1 1.4 %reduce.4 = bf16[8,64512]{1,0:T(8,128)(2,1)S(1)} reduce(bf16[8,1,64512]{2,0,1:T(8,128)(2,1)S(1)} %pad_bitcast_fusion, bf16[]{:T(256)} %broadcast.153), dimensions={1}, to_apply=%copy.240.reduce_sub_computation | reduce | bytes 2064386 | tf_op jit(solution)/shard_map/all_to_all | solution.py:101
  8.5 1.8 %reshape.204 = bf16[8,2,32256]{2,1,0:T(2,128)(2,1)} reshape(bf16[8,64512]{1,0:T(8,128)(2,1)S(1)} %reduce.4) | data formatting | bytes 2064384
  10.3 11.7 %all-to-all-start = ((bf16[8,2,32256]{2,1,0:T(2,128)(2,1)}), bf16[8,2,32256]{2,1,0:T(2,128)(2,1)S(1)}, u32[]{:S(2)}, u32[]{:S(2)}) async-start(bf16[8,2,32256]{2,1,0:T(2,128)(2,1)} %reshape.204), calls=%async_computation | async-start | bytes 2064384 | tf_op jit(solution)/shard_map/all_to_all | solution.py:101
  22.0 5.3 %collective-permute-start.2 = (s32[2048]{0:T(1024)S(1)}, s32[2048]{0:T(1024)S(1)}, u32[]{:S(2)}, u32[]{:S(2)}) collective-permute-start(s32[2048]{0:T(1024)S(1)} %bitcast.97), channel_id=1, source_target_pairs={{0,8},{8,16},{16,24},{24,32},{32,40},{40,48},{48,56},{56,64},{64,7... | collective-permute-start | bytes 24584 | tf_op jit(solution)/shard_map/ppermute | solution.py:10
  28.2 23.1 %all-to-all-done = bf16[8,2,32256]{2,1,0:T(2,128)(2,1)S(1)} async-done(((bf16[8,2,32256]{2,1,0:T(2,128)(2,1)}), bf16[8,2,32256]{2,1,0:T(2,128)(2,1)S(1)}, u32[]{:S(2)}, u32[]{:S(2)}) %all-to-all-start) | async-done | bytes 1032224 | tf_op jit(solution)/shard_map/all_to_all | solution.py:101
  51.3 0.9 reshape.205
  53.0 6.5 %collective-permute-start = (bf16[128,2,264]{2,1,0:T(2,128)(2,1)S(1)}, bf16[128,2,264]{2,1,0:T(2,128)(2,1)S(1)}, u32[]{:S(2)}, u32[]{:S(2)}) collective-permute-start(bf16[128,2,264]{2,1,0:T(2,128)(2,1)S(1)} %reshape.172), channel_id=1, source_target_pairs={{0,8},{8,16},{16,24},{24,32},{32,40},{40,48},{48,56},{56,64},{64,7... | collective-permute-start | bytes 405512 | tf_op jit(solution)/shard_map/ppermute | solution.py:10
  59.4 1.0 %slice.180 = bf16[128,2,262]{2,1,0:T(2,128)(2,1)} slice(bf16[128,2,264]{2,1,0:T(2,128)(2,1)S(1)} %reshape.172), slice={[0:128], [0:2], [1:263]} | slice | bytes 268288 | tf_op jit(solution)/shard_map/slice | solution.py:117
  60.4 2.0 %reshape.173 = bf16[8,48,1155]{2,1,0:T(8,128)(2,1)S(1)} reshape(bf16[8,55440]{1,0:T(8,128)(2,1)S(1)} %slice.190) | data formatting | bytes 1774080 | tf_op jit(solution)/shard_map/reshape | solution.py:104
  62.7 2.1 %collective-permute-start.1 = (bf16[128,264]{0,1:T(8,128)(2,1)S(1)}, bf16[128,264]{0,1:T(8,128)(2,1)S(1)}, u32[]{:S(2)}, u32[]{:S(2)}) collective-permute-start(bf16[128,264]{0,1:T(8,128)(2,1)S(1)} %bitcast.88), channel_id=1, source_target_pairs={{8,0},{16,8},{24,16},{32,24},{40,32},{48,40},{56,48},{64,56},{72,6... | collective-permute-start | bytes 202760 | tf_op jit(solution)/shard_map/ppermute | solution.py:10
  65.2 0.8 reshape.174
  66.8 2.7 %collective-permute-done.1 = bf16[128,264]{0,1:T(8,128)(2,1)S(1)} collective-permute-done((bf16[128,264]{0,1:T(8,128)(2,1)S(1)}, bf16[128,264]{0,1:T(8,128)(2,1)S(1)}, u32[]{:S(2)}, u32[]{:S(2)}) %collective-permute-start.1) | collective-permute-done | bytes 67616 | tf_op jit(solution)/shard_map/ppermute | solution.py:10
  71.0 0.7 maximum_bitcast_fusion.2
  71.7 0.7 maximum_bitcast_fusion.1
  72.5 0.6 maximum_bitcast_fusion
  73.1 1.0 %copy.267 = bf16[128,4,2,262]{0,2,3,1:T(2,128)(2,1)S(1)} copy(bf16[128,4,2,262]{3,1,0,2:T(4,128)(2,1)S(1)} %maximum_bitcast_fusion) | data formatting | bytes 1073152
  75.1 0.9 fusion.15
  78.7 0.8 reduce.5
  79.6 12.1 %all_to_all.24 = bf16[8,2,6144]{2,1,0:T(2,128)(2,1)S(1)} all-to-all(bf16[8,2,6144]{2,1,0:T(2,128)(2,1)S(1)} %reshape.206), channel_id=1, replica_groups=mesh['space'=64,'chan'=8] {'chan'}, dimensions={0} | all-to-all | bytes 393216 | tf_op jit(solution)/shard_map/all_to_all | solution.py:139
  92.2 0.7 broadcast_in_dim_reshape.8
  92.8 0.7 broadcast_in_dim_reshape.9
  (112 shorter events, 11.6 us)
Async XLA Ops:
  4.0 1.3 %copy-start.7 = (f32[32]{0:T(128)S(1)}, f32[32]{0:T(128)}, u32[]{:S(2)}) copy-start(f32[32]{0:T(128)} %param.13) | copy-start | bytes 388
  4.0 1.3 %copy-start.8 = (f32[16]{0:T(128)S(1)}, f32[16]{0:T(128)}, u32[]{:S(2)}) copy-start(f32[16]{0:T(128)} %param.11) | copy-start | bytes 196
  4.0 1.7 %copy-start.3 = (bf16[32,3,3,128]{3,0,2,1:T(8,128)(2,1)S(1)}, bf16[32,3,3,128]{3,0,2,1:T(8,128)(2,1)}, u32[]{:S(2)}) copy-start(bf16[32,3,3,128]{3,0,2,1:T(8,128)(2,1)} %param.12) | copy-start | bytes 221188
  4.1 1.7 %copy-start.4 = (bf16[16,3,3,128]{3,0,2,1:T(8,128)(2,1)S(1)}, bf16[16,3,3,128]{3,0,2,1:T(8,128)(2,1)}, u32[]{:S(2)}) copy-start(bf16[16,3,3,128]{3,0,2,1:T(8,128)(2,1)} %param.10) | copy-start | bytes 110596
  10.3 11.7 %copy-start.6 = (s32[1,2048]{1,0:T(1,128)S(1)}, s32[1,2048]{1,0:T(1,128)}, u32[]{:S(2)}) copy-start(s32[1,2048]{1,0:T(1,128)} %param.9) | copy-start | bytes 24580
  10.3 17.1 %copy-start.5 = (s32[1,2048]{1,0:T(1,128)S(1)}, s32[1,2048]{1,0:T(1,128)}, u32[]{:S(2)}) copy-start(s32[1,2048]{1,0:T(1,128)} %param.8) | copy-start | bytes 24580
  10.3 41.0 %all-to-all-start = ((bf16[8,2,32256]{2,1,0:T(2,128)(2,1)}), bf16[8,2,32256]{2,1,0:T(2,128)(2,1)S(1)}, u32[]{:S(2)}, u32[]{:S(2)}) async-start(bf16[8,2,32256]{2,1,0:T(2,128)(2,1)} %reshape.204), calls=%async_computation | async-start | bytes 2064384 | tf_op jit(solution)/shard_map/all_to_all | solution.py:101
  22.0 6.0 %collective-permute-start.2 = (s32[2048]{0:T(1024)S(1)}, s32[2048]{0:T(1024)S(1)}, u32[]{:S(2)}, u32[]{:S(2)}) collective-permute-start(s32[2048]{0:T(1024)S(1)} %bitcast.97), channel_id=1, source_target_pairs={{0,8},{8,16},{16,24},{24,32},{32,40},{40,48},{48,56},{56,64},{64,7... | collective-permute-start | bytes 24584 | tf_op jit(solution)/shard_map/ppermute | solution.py:10
  53.0 17.0 %collective-permute-start = (bf16[128,2,264]{2,1,0:T(2,128)(2,1)S(1)}, bf16[128,2,264]{2,1,0:T(2,128)(2,1)S(1)}, u32[]{:S(2)}, u32[]{:S(2)}) collective-permute-start(bf16[128,2,264]{2,1,0:T(2,128)(2,1)S(1)} %reshape.172), channel_id=1, source_target_pairs={{0,8},{8,16},{16,24},{24,32},{32,40},{40,48},{48,56},{56,64},{64,7... | collective-permute-start | bytes 405512 | tf_op jit(solution)/shard_map/ppermute | solution.py:10
  62.7 6.8 %collective-permute-start.1 = (bf16[128,264]{0,1:T(8,128)(2,1)S(1)}, bf16[128,264]{0,1:T(8,128)(2,1)S(1)}, u32[]{:S(2)}, u32[]{:S(2)}) collective-permute-start(bf16[128,264]{0,1:T(8,128)(2,1)S(1)} %bitcast.88), channel_id=1, source_target_pairs={{8,0},{16,8},{24,16},{32,24},{40,32},{48,40},{56,48},{64,56},{72,6... | collective-permute-start | bytes 202760 | tf_op jit(solution)/shard_map/ppermute | solution.py:10
  69.9 1.8 %copy-start.1 = (bf16[128,2,262]{2,1,0:T(2,128)(2,1)S(1)}, bf16[128,2,262]{2,1,0:T(2,128)(2,1)}, u32[]{:S(2)}) copy-start(bf16[128,2,262]{2,1,0:T(2,128)(2,1)} %slice.180) | copy-start | bytes 402436
  74.1 1.0 %copy-start.2 = (bf16[128,3,3,128]{3,2,1,0:T(4,128)(2,1)S(1)}, bf16[128,3,3,128]{3,2,1,0:T(4,128)(2,1)}, u32[]{:S(2)}) copy-start(bf16[128,3,3,128]{3,2,1,0:T(4,128)(2,1)} %reshape.174) | copy-start | bytes 884740
  74.1 1.0 %copy-start.9 = (pred[16,33]{0,1:T(8,128)(4,1)S(1)}, pred[16,33]{0,1:T(8,128)(4,1)}, u32[]{:S(2)}) copy-start(pred[16,33]{0,1:T(8,128)(4,1)} %constant.134) | copy-start | bytes 1588
  76.5 1.0 %copy-start = (bf16[128,2,260]{0,1,2:T(2,128)(2,1)}, bf16[128,2,260]{0,1,2:T(2,128)(2,1)S(1)}, u32[]{:S(2)}) copy-start(bf16[128,2,260]{0,1,2:T(2,128)(2,1)S(1)} %slice_bitcast_fusion.1) | copy-start | bytes 399364
  76.7 0.8 copy-start.10
  77.5 0.9 slice-start

commit v6 on v5

--- a/solution.py
+++ b/solution.py
@@ -67,6 +67,20 @@
     return jnp.moveaxis(wins, -2, 0)
 
 
+def gather_space(part):
+    count = lax.axis_size("space")
+    me = lax.axis_index("space")
+    acc = part[None]
+    bit = count // 2
+    while bit >= 1:
+        recv = lax.ppermute(acc, "space", [(i, i ^ bit) for i in range(count)])
+        low = (me & bit) == 0
+        pair = jnp.where(low, jnp.stack([acc, recv], 1), jnp.stack([recv, acc], 1))
+        acc = pair.reshape((-1,) + part.shape)
+        bit //= 2
+    return acc
+
+
 def pad_to(flat, multiple):
     extra = (-flat.shape[-1]) % multiple
     return jnp.pad(flat, [(0, 0)] * (flat.ndim - 1) + [(0, extra)])
@@ -96,12 +110,18 @@
     taps = flat_w.shape[1]
     packed_w = jnp.concatenate(
         [flat_w, split3(jnp.concatenate([first_bias, second_bias]))], axis=1
-    ).reshape(1, -1)
-    sends = jnp.concatenate([wins, jnp.broadcast_to(packed_w, (groups,) + packed_w.shape[1:])], 1)
+    ).reshape(-1)
+    tiles = lax.axis_size("space")
+    piece = -(-packed_w.shape[0] // (tiles * 128)) * 128
+    packed_w = jnp.pad(packed_w, (0, piece * tiles - packed_w.shape[0]))
+    my_piece = lax.dynamic_slice_in_dim(packed_w, lax.axis_index("space") * piece, piece)
+    sends = jnp.concatenate([wins, jnp.broadcast_to(my_piece[None], (groups, piece))], 1)
     got = lax.all_to_all(pad_to(sends, 1024), "chan", 0, 0, tiled=True)
 
     tile = got[:, :feat_len].reshape(groups * chans, rows, width + 2)
-    every = got[:, feat_len : feat_len + packed_w.shape[1]].reshape(groups, n1 + n2, taps + 3)
+    pieces = gather_space(got[:, feat_len : feat_len + piece])
+    every = jnp.moveaxis(pieces, 0, 1).reshape(groups, -1)
+    every = every[:, : (n1 + n2) * (taps + 3)].reshape(groups, n1 + n2, taps + 3)
     w1 = every[:, :n1, :taps].reshape((-1,) + first_weight.shape[1:])
     w2 = every[:, n1:, :taps].reshape((-1,) + second_weight.shape[1:])
     b1 = join3(every[:, :n1, taps:]).reshape(-1)

time: 93.9 us -> 114 us (1.21)
  the two profiles are of different devices: /device:TPU:89 before, /device:TPU:1 now
where the time goes in v6:
time: 114 us; the launch traced here: 113 us
  starting transfers between devices  46.6 us (41%)
  waiting for transfers between devices  25.9 us (23%)
  local copies, waits for them, and re-layouts  17.2 us (15%)
  blocking collectives  13.1 us (11%)
  other arithmetic  7.9 us (7%)
  between operations  1.47 us (1%)
  matrix products  1.31 us (1%)
    ppermute x6, starting transfers between devices, gather_space(): recv = lax.ppermute(acc, 'space', [(i, i ^ bit) for i in range(count)])  22.6 us
    ppermute x6, waiting for transfers between devices, gather_space(): recv = lax.ppermute(acc, 'space', [(i, i ^ bit) for i in range(count)])  16.3 us
    all_to_all x1, blocking collectives, per_device(): lax.all_to_all(jnp.concatenate([hidden_part, coarse_part], 1), 'chan', 0,...  13.1 us
    all_to_all x1, starting transfers between devices, per_device(): got = lax.all_to_all(pad_to(sends, 1024), 'chan', 0, 0, tiled=True)  12.5 us
    ppermute x3, starting transfers between devices, shifted(): return lax.ppermute(array, axis, pairs)  11.6 us
    all_to_all x1, waiting for transfers between devices, per_device(): got = lax.all_to_all(pad_to(sends, 1024), 'chan', 0, 0, tiled=True)  9.59 us
    unnamed x22, local copies, waits for them, and re-layouts  4.18 us
  transfers between devices with their start and end apart: 10, of which 5 were waited for; matrix products, arithmetic and copies ran while one was open for 14% of the time, Pallas kernels for 0%

profile of v6, /device:TPU:1, one launch (start us, length us, event | category | flops | bytes accessed | tf_op | source)
XLA Modules:
  0.0 113.5 jit_solution(2595798471843111249)
XLA Ops:
  0.6 4.7 %collective-permute-start.2 = (s32[2048]{0:T(1024)}, s32[2048]{0:T(1024)S(1)}, u32[]{:S(2)}, u32[]{:S(2)}) collective-permute-start(s32[2048]{0:T(1024)} %bitcast.135), channel_id=1, source_target_pairs={{0,8},{8,16},{16,24},{24,32},{32,40},{40,48},{48,56},{56,64},{64,7... | collective-permute-start | bytes 24584 | tf_op jit(solution)/shard_map/ppermute | solution.py:10
  5.4 1.0 reshape_squeeze.6
  6.4 0.8 fusion.87
  7.2 1.2 %fusion.88 = (bf16[16,2,2044]{2,1,0:T(2,128)(2,1)S(1)}, bf16[16,2,2044]{2,1,0:T(2,128)(2,1)S(1)}) fusion(bf16[16,2,2048]{2,1,0:T(2,128)(2,1)} %bitcast.109), kind=kLoop, calls=%fused_computation.147 | loop fusion | bytes 523264 | tf_op jit(solution)/shard_map/jit(_roll_static)/slice | solution.py:63
  9.5 0.8 copy.290
  13.8 0.8 reshape.393
  14.6 12.5 %all-to-all-start = ((bf16[8,2,5120]{2,1,0:T(2,128)(2,1)}), bf16[8,2,5120]{2,1,0:T(2,128)(2,1)S(1)}, u32[]{:S(2)}, u32[]{:S(2)}) async-start(bf16[8,2,5120]{2,1,0:T(2,128)(2,1)} %reshape.393), calls=%async_computation | async-start | bytes 327680 | tf_op jit(solution)/shard_map/all_to_all | solution.py:119
  27.4 9.6 %all-to-all-done = bf16[8,2,5120]{2,1,0:T(2,128)(2,1)S(1)} async-done(((bf16[8,2,5120]{2,1,0:T(2,128)(2,1)}), bf16[8,2,5120]{2,1,0:T(2,128)(2,1)S(1)}, u32[]{:S(2)}, u32[]{:S(2)}) %all-to-all-start) | async-done | bytes 163872 | tf_op jit(solution)/shard_map/all_to_all | solution.py:119
  37.3 5.8 %collective-permute-start.3 = (bf16[1,8,896]{2,1,0:T(8,128)(2,1)S(1)}, bf16[1,8,896]{2,1,0:T(8,128)(2,1)S(1)}, u32[]{:S(2)}, u32[]{:S(2)}) collective-permute-start(bf16[1,8,896]{2,1,0:T(8,128)(2,1)S(1)} %get-tuple-element.13), channel_id=1, source_target_pairs={{0,256},{8,264},{16,272},{24,280},{32,288},{40,296},{48,304},{56,3... | collective-permute-start | bytes 43016 | tf_op jit(solution)/shard_map/ppermute | solution.py:76
  43.2 1.0 collective-permute-done.3
  44.2 1.9 %collective-permute-start.4 = (bf16[2,8,896]{2,1,0:T(8,128)(2,1)S(1)}, bf16[2,8,896]{2,1,0:T(8,128)(2,1)S(1)}, u32[]{:S(2)}, u32[]{:S(2)}) collective-permute-start(bf16[2,8,896]{2,1,0:T(8,128)(2,1)S(1)} %maximum_select_fusion.6), channel_id=1, source_target_pairs={{0,128},{8,136},{16,144},{24,152},{32,160},{40,168},{48,176},{56,1... | collective-permute-start | bytes 86024 | tf_op jit(solution)/shard_map/ppermute | solution.py:76
  46.2 2.7 %collective-permute-done.4 = bf16[2,8,896]{2,1,0:T(8,128)(2,1)S(1)} collective-permute-done((bf16[2,8,896]{2,1,0:T(8,128)(2,1)S(1)}, bf16[2,8,896]{2,1,0:T(8,128)(2,1)S(1)}, u32[]{:S(2)}, u32[]{:S(2)}) %collective-permute-start.4) | collective-permute-done | bytes 28704 | tf_op jit(solution)/shard_map/ppermute | solution.py:76
  48.9 7.2 %collective-permute-start.5 = (bf16[4,8,896]{2,1,0:T(8,128)(2,1)S(1)}, bf16[4,8,896]{2,1,0:T(8,128)(2,1)S(1)}, u32[]{:S(2)}, u32[]{:S(2)}) collective-permute-start(bf16[4,8,896]{2,1,0:T(8,128)(2,1)S(1)} %bitcast.126), channel_id=1, source_target_pairs={{0,64},{8,72},{16,80},{24,88},{32,96},{40,104},{48,112},{56,120},{... | collective-permute-start | bytes 172040 | tf_op jit(solution)/shard_map/ppermute | solution.py:76
  56.8 4.9 %collective-permute-start = (bf16[128,2,264]{2,1,0:T(2,128)(2,1)S(1)}, bf16[128,2,264]{2,1,0:T(2,128)(2,1)S(1)}, u32[]{:S(2)}, u32[]{:S(2)}) collective-permute-start(bf16[128,2,264]{2,1,0:T(2,128)(2,1)S(1)} %reshape.360), channel_id=1, source_target_pairs={{0,8},{8,16},{16,24},{24,32},{32,40},{40,48},{48,56},{56,64},{64,7... | collective-permute-start | bytes 405512 | tf_op jit(solution)/shard_map/ppermute | solution.py:10
  61.9 1.9 %collective-permute-start.1 = (bf16[128,264]{0,1:T(8,128)(2,1)S(1)}, bf16[128,264]{0,1:T(8,128)(2,1)S(1)}, u32[]{:S(2)}, u32[]{:S(2)}) collective-permute-start(bf16[128,264]{0,1:T(8,128)(2,1)S(1)} %bitcast.112), channel_id=1, source_target_pairs={{8,0},{16,8},{24,16},{32,24},{40,32},{48,40},{56,48},{64,56},{72,6... | collective-permute-start | bytes 202760 | tf_op jit(solution)/shard_map/ppermute | solution.py:10
  63.9 2.4 %collective-permute-start.6 = (bf16[8,8,896]{2,1,0:T(8,128)(2,1)S(1)}, bf16[8,8,896]{2,1,0:T(8,128)(2,1)S(1)}, u32[]{:S(2)}, u32[]{:S(2)}) collective-permute-start(bf16[8,8,896]{2,1,0:T(8,128)(2,1)S(1)} %bitcast.123), channel_id=1, source_target_pairs={{0,32},{8,40},{16,48},{24,56},{32,0},{40,8},{48,16},{56,24},{64,96... | collective-permute-start | bytes 344072 | tf_op jit(solution)/shard_map/ppermute | solution.py:76
  66.7 7.2 %collective-permute-done.6 = bf16[8,8,896]{2,1,0:T(8,128)(2,1)S(1)} collective-permute-done((bf16[8,8,896]{2,1,0:T(8,128)(2,1)S(1)}, bf16[8,8,896]{2,1,0:T(8,128)(2,1)S(1)}, u32[]{:S(2)}, u32[]{:S(2)}) %collective-permute-start.6) | collective-permute-done | bytes 114720 | tf_op jit(solution)/shard_map/ppermute | solution.py:76
  73.9 1.9 %collective-permute-start.7 = (bf16[16,8,896]{2,1,0:T(8,128)(2,1)S(1)}, bf16[16,8,896]{2,1,0:T(8,128)(2,1)S(1)}, u32[]{:S(2)}, u32[]{:S(2)}) collective-permute-start(bf16[16,8,896]{2,1,0:T(8,128)(2,1)S(1)} %bitcast.116), channel_id=1, source_target_pairs={{0,16},{8,24},{16,0},{24,8},{32,48},{40,56},{48,32},{56,40},{64,80... | collective-permute-start | bytes 688136 | tf_op jit(solution)/shard_map/ppermute | solution.py:76
  77.1 5.5 %collective-permute-done.7 = bf16[16,8,896]{2,1,0:T(8,128)(2,1)S(1)} collective-permute-done((bf16[16,8,896]{2,1,0:T(8,128)(2,1)S(1)}, bf16[16,8,896]{2,1,0:T(8,128)(2,1)S(1)}, u32[]{:S(2)}, u32[]{:S(2)}) %collective-permute-start.7) | collective-permute-done | bytes 229408 | tf_op jit(solution)/shard_map/ppermute | solution.py:76
  82.8 3.3 %collective-permute-start.8 = (bf16[32,8,896]{2,1,0:T(8,128)(2,1)S(1)}, bf16[32,8,896]{2,1,0:T(8,128)(2,1)S(1)}, u32[]{:S(2)}, u32[]{:S(2)}) collective-permute-start(bf16[32,8,896]{2,1,0:T(8,128)(2,1)S(1)} %bitcast.105), channel_id=1, source_target_pairs={{0,8},{8,0},{16,24},{24,16},{32,40},{40,32},{48,56},{56,48},{64,72... | collective-permute-start | bytes 1376264 | tf_op jit(solution)/shard_map/ppermute | solution.py:76
  88.3 1.0 copy.331
  90.6 2.0 %reshape.362 = bf16[8,48,1155]{2,1,0:T(8,128)(2,1)S(1)} reshape(bf16[8,55440]{1,0:T(8,128)(2,1)S(1)} %slice.195) | data formatting | bytes 1774080 | tf_op jit(solution)/shard_map/reshape | solution.py:124
  93.4 0.9 fusion.15
  98.6 13.1 %all_to_all.24 = bf16[8,2,6144]{2,1,0:T(2,128)(2,1)S(1)} all-to-all(bf16[8,2,6144]{2,1,0:T(2,128)(2,1)S(1)} %reshape.395), channel_id=1, replica_groups=mesh['space'=64,'chan'=8] {'chan'}, dimensions={0} | all-to-all | bytes 393216 | tf_op jit(solution)/shard_map/all_to_all | solution.py:159
  (125 shorter events, 18.0 us)
Async XLA Ops:
  0.6 9.7 %copy-start = (bf16[32,3,3,128]{3,0,2,1:T(8,128)(2,1)S(1)}, bf16[32,3,3,128]{3,0,2,1:T(8,128)(2,1)}, u32[]{:S(2)}) copy-start(bf16[32,3,3,128]{3,0,2,1:T(8,128)(2,1)} %param.12) | copy-start | bytes 221188
  0.6 42.5 %collective-permute-start.2 = (s32[2048]{0:T(1024)}, s32[2048]{0:T(1024)S(1)}, u32[]{:S(2)}, u32[]{:S(2)}) collective-permute-start(s32[2048]{0:T(1024)} %bitcast.135), channel_id=1, source_target_pairs={{0,8},{8,16},{16,24},{24,32},{32,40},{40,48},{48,56},{56,64},{64,7... | collective-permute-start | bytes 24584 | tf_op jit(solution)/shard_map/ppermute | solution.py:10
  12.4 14.7 %copy-start.1 = (s32[1,2048]{1,0:T(1,128)S(1)}, s32[1,2048]{1,0:T(1,128)}, u32[]{:S(2)}) copy-start(s32[1,2048]{1,0:T(1,128)} %param.8) | copy-start | bytes 24580
  12.4 14.9 %copy-start.2 = (s32[1,2048]{1,0:T(1,128)S(1)}, s32[1,2048]{1,0:T(1,128)}, u32[]{:S(2)}) copy-start(s32[1,2048]{1,0:T(1,128)} %param.9) | copy-start | bytes 24580
  14.6 22.4 %all-to-all-start = ((bf16[8,2,5120]{2,1,0:T(2,128)(2,1)}), bf16[8,2,5120]{2,1,0:T(2,128)(2,1)S(1)}, u32[]{:S(2)}, u32[]{:S(2)}) async-start(bf16[8,2,5120]{2,1,0:T(2,128)(2,1)} %reshape.393), calls=%async_computation | async-start | bytes 327680 | tf_op jit(solution)/shard_map/all_to_all | solution.py:119
  37.3 6.9 %collective-permute-start.3 = (bf16[1,8,896]{2,1,0:T(8,128)(2,1)S(1)}, bf16[1,8,896]{2,1,0:T(8,128)(2,1)S(1)}, u32[]{:S(2)}, u32[]{:S(2)}) collective-permute-start(bf16[1,8,896]{2,1,0:T(8,128)(2,1)S(1)} %get-tuple-element.13), channel_id=1, source_target_pairs={{0,256},{8,264},{16,272},{24,280},{32,288},{40,296},{48,304},{56,3... | collective-permute-start | bytes 43016 | tf_op jit(solution)/shard_map/ppermute | solution.py:76
  44.2 4.6 %collective-permute-start.4 = (bf16[2,8,896]{2,1,0:T(8,128)(2,1)S(1)}, bf16[2,8,896]{2,1,0:T(8,128)(2,1)S(1)}, u32[]{:S(2)}, u32[]{:S(2)}) collective-permute-start(bf16[2,8,896]{2,1,0:T(8,128)(2,1)S(1)} %maximum_select_fusion.6), channel_id=1, source_target_pairs={{0,128},{8,136},{16,144},{24,152},{32,160},{40,168},{48,176},{56,1... | collective-permute-start | bytes 86024 | tf_op jit(solution)/shard_map/ppermute | solution.py:76
  48.9 15.0 %collective-permute-start.5 = (bf16[4,8,896]{2,1,0:T(8,128)(2,1)S(1)}, bf16[4,8,896]{2,1,0:T(8,128)(2,1)S(1)}, u32[]{:S(2)}, u32[]{:S(2)}) collective-permute-start(bf16[4,8,896]{2,1,0:T(8,128)(2,1)S(1)} %bitcast.126), channel_id=1, source_target_pairs={{0,64},{8,72},{16,80},{24,88},{32,96},{40,104},{48,112},{56,120},{... | collective-permute-start | bytes 172040 | tf_op jit(solution)/shard_map/ppermute | solution.py:76
  56.8 19.5 %collective-permute-start = (bf16[128,2,264]{2,1,0:T(2,128)(2,1)S(1)}, bf16[128,2,264]{2,1,0:T(2,128)(2,1)S(1)}, u32[]{:S(2)}, u32[]{:S(2)}) collective-permute-start(bf16[128,2,264]{2,1,0:T(2,128)(2,1)S(1)} %reshape.360), channel_id=1, source_target_pairs={{0,8},{8,16},{16,24},{24,32},{32,40},{40,48},{48,56},{56,64},{64,7... | collective-permute-start | bytes 405512 | tf_op jit(solution)/shard_map/ppermute | solution.py:10
  61.9 14.0 %collective-permute-start.1 = (bf16[128,264]{0,1:T(8,128)(2,1)S(1)}, bf16[128,264]{0,1:T(8,128)(2,1)S(1)}, u32[]{:S(2)}, u32[]{:S(2)}) collective-permute-start(bf16[128,264]{0,1:T(8,128)(2,1)S(1)} %bitcast.112), channel_id=1, source_target_pairs={{8,0},{16,8},{24,16},{32,24},{40,32},{48,40},{56,48},{64,56},{72,6... | collective-permute-start | bytes 202760 | tf_op jit(solution)/shard_map/ppermute | solution.py:10
  63.9 10.0 %collective-permute-start.6 = (bf16[8,8,896]{2,1,0:T(8,128)(2,1)S(1)}, bf16[8,8,896]{2,1,0:T(8,128)(2,1)S(1)}, u32[]{:S(2)}, u32[]{:S(2)}) collective-permute-start(bf16[8,8,896]{2,1,0:T(8,128)(2,1)S(1)} %bitcast.123), channel_id=1, source_target_pairs={{0,32},{8,40},{16,48},{24,56},{32,0},{40,8},{48,16},{56,24},{64,96... | collective-permute-start | bytes 344072 | tf_op jit(solution)/shard_map/ppermute | solution.py:76
  73.9 8.7 %collective-permute-start.7 = (bf16[16,8,896]{2,1,0:T(8,128)(2,1)S(1)}, bf16[16,8,896]{2,1,0:T(8,128)(2,1)S(1)}, u32[]{:S(2)}, u32[]{:S(2)}) collective-permute-start(bf16[16,8,896]{2,1,0:T(8,128)(2,1)S(1)} %bitcast.116), channel_id=1, source_target_pairs={{0,16},{8,24},{16,0},{24,8},{32,48},{40,56},{48,32},{56,40},{64,80... | collective-permute-start | bytes 688136 | tf_op jit(solution)/shard_map/ppermute | solution.py:76
  82.8 7.5 %collective-permute-start.8 = (bf16[32,8,896]{2,1,0:T(8,128)(2,1)S(1)}, bf16[32,8,896]{2,1,0:T(8,128)(2,1)S(1)}, u32[]{:S(2)}, u32[]{:S(2)}) collective-permute-start(bf16[32,8,896]{2,1,0:T(8,128)(2,1)S(1)} %bitcast.105), channel_id=1, source_target_pairs={{0,8},{8,0},{16,24},{24,16},{32,40},{40,32},{48,56},{56,48},{64,72... | collective-permute-start | bytes 1376264 | tf_op jit(solution)/shard_map/ppermute | solution.py:76
  92.7 0.7 copy-start.3
  96.4 0.7 copy-start.4

commit v7 on v5

--- a/solution.py
+++ b/solution.py
@@ -97,11 +97,14 @@
     packed_w = jnp.concatenate(
         [flat_w, split3(jnp.concatenate([first_bias, second_bias]))], axis=1
     ).reshape(1, -1)
-    sends = jnp.concatenate([wins, jnp.broadcast_to(packed_w, (groups,) + packed_w.shape[1:])], 1)
-    got = lax.all_to_all(pad_to(sends, 1024), "chan", 0, 0, tiled=True)
+    w_got = lax.all_to_all(
+        pad_to(jnp.broadcast_to(packed_w, (groups,) + packed_w.shape[1:]), 1024),
+        "chan", 0, 0, tiled=True,
+    )
+    got = lax.all_to_all(pad_to(wins, 1024), "chan", 0, 0, tiled=True)
 
     tile = got[:, :feat_len].reshape(groups * chans, rows, width + 2)
-    every = got[:, feat_len : feat_len + packed_w.shape[1]].reshape(groups, n1 + n2, taps + 3)
+    every = w_got[:, : packed_w.shape[1]].reshape(groups, n1 + n2, taps + 3)
     w1 = every[:, :n1, :taps].reshape((-1,) + first_weight.shape[1:])
     w2 = every[:, n1:, :taps].reshape((-1,) + second_weight.shape[1:])
     b1 = join3(every[:, :n1, taps:]).reshape(-1)

time: 93.9 us -> 96.2 us (1.024)
  the two profiles are of different devices: /device:TPU:89 before, /device:TPU:81 now
where the time goes in v7:
time: 96.2 us; the launch traced here: 95.6 us
  starting transfers between devices  29.4 us (31%)
  local copies, waits for them, and re-layouts  19.6 us (20%)
  waiting for transfers between devices  15.9 us (17%)
  blocking collectives  15 us (16%)
  other arithmetic  12.9 us (13%)
  between operations  1.44 us (1%)
  matrix products  1.31 us (1%)
    all_to_all x1, blocking collectives, per_device(): lax.all_to_all(jnp.concatenate([hidden_part, coarse_part], 1), 'chan', 0,...  15 us
    all_to_all x1, waiting for transfers between devices, per_device(): lax.all_to_all(pad_to(jnp.broadcast_to(packed_w, (groups,) + packed_w.sha...  12.1 us
    all_to_all x1, starting transfers between devices, per_device(): got = lax.all_to_all(pad_to(wins, 1024), 'chan', 0, 0, tiled=True)  11.6 us
    all_to_all x1, starting transfers between devices, per_device(): lax.all_to_all(pad_to(jnp.broadcast_to(packed_w, (groups,) + packed_w.sha...  9.33 us
    ppermute x3, starting transfers between devices, shifted(): return lax.ppermute(array, axis, pairs)  8.55 us
    pad x1, other arithmetic, pad_to(): return jnp.pad(flat, [(0, 0)] * (flat.ndim - 1) + [(0, extra)])  6.12 us
    unnamed x33, local copies, waits for them, and re-layouts  5.77 us
    ppermute x3, waiting for transfers between devices, shifted(): return lax.ppermute(array, axis, pairs)  3.79 us
  transfers between devices with their start and end apart: 5, of which 2 were waited for; matrix products, arithmetic and copies ran while one was open for 18% of the time, Pallas kernels for 0%

profile of v7, /device:TPU:81, one launch (start us, length us, event | category | flops | bytes accessed | tf_op | source)
XLA Modules:
  0.0 95.6 jit_solution(9184072259191806989)
XLA Ops:
  0.6 1.2 %fusion.88 = (bf16[16,2,2044]{2,1,0:T(2,128)(2,1)S(1)}, bf16[16,2,2044]{2,1,0:T(2,128)(2,1)S(1)}) fusion(bf16[16,2,2048]{2,1,0:T(2,128)(2,1)} %bitcast.86), kind=kLoop, calls=%fused_computation.137 | loop fusion | bytes 523264 | tf_op jit(solution)/shard_map/jit(_roll_static)/slice | solution.py:63
  1.9 0.8 fusion.87
  2.7 1.0 %reshape_squeeze.6 = bf16[16,2,8,256]{3,2,1,0:T(8,128)(2,1)S(1)} reshape(bf16[1,16,2,2048]{3,2,1,0:T(2,128)(2,1)} %param.7) | data formatting | bytes 262144 | tf_op jit(solution)/shard_map/reshape;squeeze | solution.py:64
  5.9 0.7 reduce.5
  6.5 0.8 reshape.209
  7.3 11.6 %all-to-all-start = ((bf16[8,2,4608]{2,1,0:T(2,128)(2,1)}), bf16[8,2,4608]{2,1,0:T(2,128)(2,1)S(1)}, u32[]{:S(2)}, u32[]{:S(2)}) async-start(bf16[8,2,4608]{2,1,0:T(2,128)(2,1)} %reshape.209), calls=%async_computation | async-start | bytes 294912 | tf_op jit(solution)/shard_map/all_to_all | solution.py:104
  18.9 4.0 %collective-permute-start.2 = (s32[2048]{0:T(1024)S(1)}, s32[2048]{0:T(1024)S(1)}, u32[]{:S(2)}, u32[]{:S(2)}) collective-permute-start(s32[2048]{0:T(1024)S(1)} %bitcast.100), channel_id=1, source_target_pairs={{0,8},{8,16},{16,24},{24,32},{32,40},{40,48},{48,56},{56,64},{64,7... | collective-permute-start | bytes 24584 | tf_op jit(solution)/shard_map/ppermute | solution.py:10
  24.3 0.9 pad.12
  25.2 6.1 %reduce.4 = bf16[8,56320]{1,0:T(8,128)(2,1)S(1)} reduce(bf16[8,1,56320]{2,1,0:T(2,128)(2,1)S(1)} %pad.12, bf16[]{:T(256)} %broadcast.157), dimensions={1}, to_apply=%pad.12.reduce_sub_computation | reduce | bytes 1802242 | tf_op jit(solution)/shard_map/jit(_pad)/pad | solution.py:72
  31.4 1.7 %reshape.207 = bf16[8,2,28160]{2,1,0:T(2,128)(2,1)} reshape(bf16[8,56320]{1,0:T(8,128)(2,1)S(1)} %reduce.4) | data formatting | bytes 1802240
  33.0 9.3 %all-to-all-start.1 = ((bf16[8,2,28160]{2,1,0:T(2,128)(2,1)}), bf16[8,2,28160]{2,1,0:T(2,128)(2,1)S(1)}, u32[]{:S(2)}, u32[]{:S(2)}) async-start(bf16[8,2,28160]{2,1,0:T(2,128)(2,1)} %reshape.207), calls=%async_computation.1 | async-start | bytes 1802240 | tf_op jit(solution)/shard_map/all_to_all | solution.py:100
  43.1 2.2 %collective-permute-start = (bf16[128,2,264]{2,1,0:T(2,128)(2,1)S(1)}, bf16[128,2,264]{2,1,0:T(2,128)(2,1)S(1)}, u32[]{:S(2)}, u32[]{:S(2)}) collective-permute-start(bf16[128,2,264]{2,1,0:T(2,128)(2,1)S(1)} %reshape.174), channel_id=1, source_target_pairs={{0,8},{8,16},{16,24},{24,32},{32,40},{40,48},{48,56},{56,64},{64,7... | collective-permute-start | bytes 405512 | tf_op jit(solution)/shard_map/ppermute | solution.py:10
  45.5 2.3 %collective-permute-start.1 = (bf16[128,264]{0,1:T(8,128)(2,1)S(1)}, bf16[128,264]{0,1:T(8,128)(2,1)S(1)}, u32[]{:S(2)}, u32[]{:S(2)}) collective-permute-start(bf16[128,264]{0,1:T(8,128)(2,1)S(1)} %bitcast.90), channel_id=1, source_target_pairs={{8,0},{16,8},{24,16},{32,24},{40,32},{48,40},{56,48},{64,56},{72,6... | collective-permute-start | bytes 202760 | tf_op jit(solution)/shard_map/ppermute | solution.py:10
  48.5 3.8 %collective-permute-done.1 = bf16[128,264]{0,1:T(8,128)(2,1)S(1)} collective-permute-done((bf16[128,264]{0,1:T(8,128)(2,1)S(1)}, bf16[128,264]{0,1:T(8,128)(2,1)S(1)}, u32[]{:S(2)}, u32[]{:S(2)}) %collective-permute-start.1) | collective-permute-done | bytes 67616 | tf_op jit(solution)/shard_map/ppermute | solution.py:10
  53.7 0.7 maximum_bitcast_fusion.2
  54.5 0.7 maximum_bitcast_fusion.1
  55.8 1.0 %copy.269 = bf16[128,4,2,262]{0,2,3,1:T(2,128)(2,1)S(1)} copy(bf16[128,4,2,262]{3,1,0,2:T(4,128)(2,1)S(1)} %maximum_bitcast_fusion) | data formatting | bytes 1073152
  57.7 12.1 %all-to-all-done.1 = bf16[8,2,28160]{2,1,0:T(2,128)(2,1)S(1)} async-done(((bf16[8,2,28160]{2,1,0:T(2,128)(2,1)}), bf16[8,2,28160]{2,1,0:T(2,128)(2,1)S(1)}, u32[]{:S(2)}, u32[]{:S(2)}) %all-to-all-start.1) | async-done | bytes 901152 | tf_op jit(solution)/shard_map/all_to_all | solution.py:100
  69.8 0.8 reshape.208
  71.0 2.0 %reshape.177 = bf16[8,48,1155]{2,1,0:T(8,128)(2,1)S(1)} reshape(bf16[8,55440]{1,0:T(8,128)(2,1)S(1)} %slice.190) | data formatting | bytes 1774080 | tf_op jit(solution)/shard_map/reshape | solution.py:107
  73.7 0.9 fusion.15
  77.9 0.8 reduce.6
  78.8 15.0 %all_to_all.33 = bf16[8,2,6144]{2,1,0:T(2,128)(2,1)S(1)} all-to-all(bf16[8,2,6144]{2,1,0:T(2,128)(2,1)S(1)} %reshape.211), channel_id=1, replica_groups=mesh['space'=64,'chan'=8] {'chan'}, dimensions={0} | all-to-all | bytes 393216 | tf_op jit(solution)/shard_map/all_to_all | solution.py:142
  94.3 0.7 broadcast_in_dim_reshape.8
  (114 shorter events, 13.2 us)
Async XLA Ops:
  4.4 14.5 %copy-start.4 = (s32[1,2048]{1,0:T(1,128)S(1)}, s32[1,2048]{1,0:T(1,128)}, u32[]{:S(2)}) copy-start(s32[1,2048]{1,0:T(1,128)} %param.9) | copy-start | bytes 24580
  4.4 18.6 %copy-start.3 = (s32[1,2048]{1,0:T(1,128)S(1)}, s32[1,2048]{1,0:T(1,128)}, u32[]{:S(2)}) copy-start(s32[1,2048]{1,0:T(1,128)} %param.8) | copy-start | bytes 24580
  4.4 18.7 %copy-start.5 = (f32[32]{0:T(128)S(1)}, f32[32]{0:T(128)}, u32[]{:S(2)}) copy-start(f32[32]{0:T(128)} %param.13) | copy-start | bytes 388
  4.4 18.7 %copy-start.6 = (f32[16]{0:T(128)S(1)}, f32[16]{0:T(128)}, u32[]{:S(2)}) copy-start(f32[16]{0:T(128)} %param.11) | copy-start | bytes 196
  4.5 18.8 %copy-start.1 = (bf16[32,3,3,128]{3,0,2,1:T(8,128)(2,1)S(1)}, bf16[32,3,3,128]{3,0,2,1:T(8,128)(2,1)}, u32[]{:S(2)}) copy-start(bf16[32,3,3,128]{3,0,2,1:T(8,128)(2,1)} %param.12) | copy-start | bytes 221188
  4.6 18.8 %copy-start.2 = (bf16[16,3,3,128]{3,0,2,1:T(8,128)(2,1)S(1)}, bf16[16,3,3,128]{3,0,2,1:T(8,128)(2,1)}, u32[]{:S(2)}) copy-start(bf16[16,3,3,128]{3,0,2,1:T(8,128)(2,1)} %param.10) | copy-start | bytes 110596
  7.3 25.7 %all-to-all-start = ((bf16[8,2,4608]{2,1,0:T(2,128)(2,1)}), bf16[8,2,4608]{2,1,0:T(2,128)(2,1)S(1)}, u32[]{:S(2)}, u32[]{:S(2)}) async-start(bf16[8,2,4608]{2,1,0:T(2,128)(2,1)} %reshape.209), calls=%async_computation | async-start | bytes 294912 | tf_op jit(solution)/shard_map/all_to_all | solution.py:104
  18.9 23.5 %collective-permute-start.2 = (s32[2048]{0:T(1024)S(1)}, s32[2048]{0:T(1024)S(1)}, u32[]{:S(2)}, u32[]{:S(2)}) collective-permute-start(s32[2048]{0:T(1024)S(1)} %bitcast.100), channel_id=1, source_target_pairs={{0,8},{8,16},{16,24},{24,32},{32,40},{40,48},{48,56},{56,64},{64,7... | collective-permute-start | bytes 24584 | tf_op jit(solution)/shard_map/ppermute | solution.py:10
  33.0 36.8 %all-to-all-start.1 = ((bf16[8,2,28160]{2,1,0:T(2,128)(2,1)}), bf16[8,2,28160]{2,1,0:T(2,128)(2,1)S(1)}, u32[]{:S(2)}, u32[]{:S(2)}) async-start(bf16[8,2,28160]{2,1,0:T(2,128)(2,1)} %reshape.207), calls=%async_computation.1 | async-start | bytes 1802240 | tf_op jit(solution)/shard_map/all_to_all | solution.py:100
  43.1 9.5 %collective-permute-start = (bf16[128,2,264]{2,1,0:T(2,128)(2,1)S(1)}, bf16[128,2,264]{2,1,0:T(2,128)(2,1)S(1)}, u32[]{:S(2)}, u32[]{:S(2)}) collective-permute-start(bf16[128,2,264]{2,1,0:T(2,128)(2,1)S(1)} %reshape.174), channel_id=1, source_target_pairs={{0,8},{8,16},{16,24},{24,32},{32,40},{40,48},{48,56},{56,64},{64,7... | collective-permute-start | bytes 405512 | tf_op jit(solution)/shard_map/ppermute | solution.py:10
  45.5 6.8 %collective-permute-start.1 = (bf16[128,264]{0,1:T(8,128)(2,1)S(1)}, bf16[128,264]{0,1:T(8,128)(2,1)S(1)}, u32[]{:S(2)}, u32[]{:S(2)}) collective-permute-start(bf16[128,264]{0,1:T(8,128)(2,1)S(1)} %bitcast.90), channel_id=1, source_target_pairs={{8,0},{16,8},{24,16},{32,24},{40,32},{48,40},{56,48},{64,56},{72,6... | collective-permute-start | bytes 202760 | tf_op jit(solution)/shard_map/ppermute | solution.py:10
  73.0 0.7 copy-start.7
  75.1 0.9 copy-start
  76.1 0.7 copy-start.8
  76.8 0.9 slice-start

commit v8 on v5

--- a/solution.py
+++ b/solution.py
@@ -96,12 +96,25 @@
     taps = flat_w.shape[1]
     packed_w = jnp.concatenate(
         [flat_w, split3(jnp.concatenate([first_bias, second_bias]))], axis=1
-    ).reshape(1, -1)
-    sends = jnp.concatenate([wins, jnp.broadcast_to(packed_w, (groups,) + packed_w.shape[1:])], 1)
+    ).reshape(-1)
+    w_len = packed_w.shape[0]
+    half = -(-w_len // 256) * 128
+    packed_w = jnp.pad(packed_w, (0, 2 * half - w_len))
+    second = (lax.axis_index("space") % 2) == 1
+    mine = lax.dynamic_slice_in_dim(packed_w, jnp.where(second, half, 0), half)
+    sends = jnp.concatenate([wins, jnp.broadcast_to(mine[None], (groups, half))], 1)
     got = lax.all_to_all(pad_to(sends, 1024), "chan", 0, 0, tiled=True)
 
     tile = got[:, :feat_len].reshape(groups * chans, rows, width + 2)
-    every = got[:, feat_len : feat_len + packed_w.shape[1]].reshape(groups, n1 + n2, taps + 3)
+    own_half = got[:, feat_len : feat_len + half]
+    spaces = lax.axis_size("space")
+    other_half = lax.ppermute(own_half, "space", [(i, i ^ 1) for i in range(spaces)])
+    every = jnp.where(
+        second,
+        jnp.concatenate([other_half, own_half], 1),
+        jnp.concatenate([own_half, other_half], 1),
+    )
+    every = every[:, :w_len].reshape(groups, n1 + n2, taps + 3)
     w1 = every[:, :n1, :taps].reshape((-1,) + first_weight.shape[1:])
     w2 = every[:, n1:, :taps].reshape((-1,) + second_weight.shape[1:])
     b1 = join3(every[:, :n1, taps:]).reshape(-1)

time: 93.9 us -> 91.7 us (0.977)
  the two profiles are of different devices: /device:TPU:89 before, /device:TPU:64 now
where the time goes in v8:
time: 91.7 us; the launch traced here: 91.2 us
  starting transfers between devices  23.5 us (26%)
  waiting for transfers between devices  21.5 us (23%)
  local copies, waits for them, and re-layouts  19.3 us (21%)
  blocking collectives  15.9 us (17%)
  other arithmetic  8.18 us (9%)
  between operations  1.34 us (1%)
  matrix products  1.31 us (1%)
    all_to_all x1, waiting for transfers between devices, per_device(): got = lax.all_to_all(pad_to(sends, 1024), 'chan', 0, 0, tiled=True)  21.5 us
    all_to_all x1, blocking collectives, per_device(): lax.all_to_all(jnp.concatenate([hidden_part, coarse_part], 1), 'chan', 0,...  15.9 us
    all_to_all x1, starting transfers between devices, per_device(): got = lax.all_to_all(pad_to(sends, 1024), 'chan', 0, 0, tiled=True)  11.8 us
    ppermute x3, starting transfers between devices, shifted(): return lax.ppermute(array, axis, pairs)  9.59 us
    unnamed x20, local copies, waits for them, and re-layouts  6.43 us
    ppermute x1, starting transfers between devices, per_device(): lax.ppermute(own_half, 'space', [(i, i ^ 1) for i in range(spaces)])  2.1 us
    slice x3, local copies, waits for them, and re-layouts, column_windows(): jnp.roll(padded, halo, axis=-1).reshape(lead + (groups, block))[..., :halo]  2.04 us
    another operation x3, other arithmetic, per_device(): jnp.stack([jnp.concatenate([above[:, None], inner, below[:, None]], axis=...  2.04 us
  transfers between devices with their start and end apart: 5, of which 1 were waited for; matrix products, arithmetic and copies ran while one was open for 19% of the time, Pallas kernels for 0%

profile of v8, /device:TPU:64, one launch (start us, length us, event | category | flops | bytes accessed | tf_op | source)
XLA Modules:
  0.0 91.2 jit_solution(2618326515431308483)
XLA Ops:
  0.6 1.9 %collective-permute-start.2 = (s32[2048]{0:T(1024)}, s32[2048]{0:T(1024)S(1)}, u32[]{:S(2)}, u32[]{:S(2)}) collective-permute-start(s32[2048]{0:T(1024)} %bitcast.97), channel_id=1, source_target_pairs={{0,8},{8,16},{16,24},{24,32},{32,40},{40,48},{48,56},{56,64},{64,7... | collective-permute-start | bytes 24584 | tf_op jit(solution)/shard_map/ppermute | solution.py:10
  2.6 1.0 %reshape_squeeze.6 = bf16[16,2,8,256]{3,2,1,0:T(8,128)(2,1)S(1)} reshape(bf16[1,16,2,2048]{3,2,1,0:T(2,128)(2,1)} %param.7) | data formatting | bytes 262144 | tf_op jit(solution)/shard_map/reshape;squeeze | solution.py:64
  3.6 0.8 fusion.88
  4.4 1.2 %fusion.89 = (bf16[16,2,2044]{2,1,0:T(2,128)(2,1)S(1)}, bf16[16,2,2044]{2,1,0:T(2,128)(2,1)S(1)}) fusion(bf16[16,2,2048]{2,1,0:T(2,128)(2,1)} %bitcast.85), kind=kLoop, calls=%fused_computation.141 | loop fusion | bytes 523264 | tf_op jit(solution)/shard_map/jit(_roll_static)/slice | solution.py:63
  5.6 0.8 fusion.80
  6.7 0.8 copy.235
  7.5 0.9 %copy.236 = bf16[32,3,3,128]{3,2,1,0:T(4,128)(2,1)S(1)} copy(bf16[32,3,3,128]{3,0,2,1:T(8,128)(2,1)} %param.12) | data formatting | bytes 147456 | tf_op args[5]
  11.3 1.1 %reduce.4 = bf16[8,36864]{1,0:T(8,128)(2,1)S(1)} reduce(bf16[8,1,36864]{2,0,1:T(8,128)(2,1)S(1)} %pad_bitcast_fusion, bf16[]{:T(256)} %broadcast.157), dimensions={1}, to_apply=%copy.240.reduce_sub_computation | reduce | bytes 1179650 | tf_op jit(solution)/shard_map/all_to_all | solution.py:106
  12.4 1.2 %reshape.207 = bf16[8,2,18432]{2,1,0:T(2,128)(2,1)} reshape(bf16[8,36864]{1,0:T(8,128)(2,1)S(1)} %reduce.4) | data formatting | bytes 1179648
  13.6 11.8 %all-to-all-start = ((bf16[8,2,18432]{2,1,0:T(2,128)(2,1)}), bf16[8,2,18432]{2,1,0:T(2,128)(2,1)S(1)}, u32[]{:S(2)}, u32[]{:S(2)}) async-start(bf16[8,2,18432]{2,1,0:T(2,128)(2,1)} %reshape.207), calls=%async_computation | async-start | bytes 1179648 | tf_op jit(solution)/shard_map/all_to_all | solution.py:106
  26.0 21.5 %all-to-all-done = bf16[8,2,18432]{2,1,0:T(2,128)(2,1)S(1)} async-done(((bf16[8,2,18432]{2,1,0:T(2,128)(2,1)}), bf16[8,2,18432]{2,1,0:T(2,128)(2,1)S(1)}, u32[]{:S(2)}, u32[]{:S(2)}) %all-to-all-start) | async-done | bytes 589856 | tf_op jit(solution)/shard_map/all_to_all | solution.py:106
  48.1 0.7 copy.287
  49.5 2.1 %collective-permute-start = (bf16[128,2,264]{2,1,0:T(2,128)(2,1)S(1)}, bf16[128,2,264]{2,1,0:T(2,128)(2,1)S(1)}, u32[]{:S(2)}, u32[]{:S(2)}) collective-permute-start(bf16[128,2,264]{2,1,0:T(2,128)(2,1)S(1)} %reshape.175), channel_id=1, source_target_pairs={{0,8},{8,16},{16,24},{24,32},{32,40},{40,48},{48,56},{56,64},{64,7... | collective-permute-start | bytes 405512 | tf_op jit(solution)/shard_map/ppermute | solution.py:10
  51.8 5.5 %collective-permute-start.1 = (bf16[128,264]{0,1:T(8,128)(2,1)S(1)}, bf16[128,264]{0,1:T(8,128)(2,1)S(1)}, u32[]{:S(2)}, u32[]{:S(2)}) collective-permute-start(bf16[128,264]{0,1:T(8,128)(2,1)S(1)} %bitcast.88), channel_id=1, source_target_pairs={{8,0},{16,8},{24,16},{32,24},{40,32},{48,40},{56,48},{64,56},{72,6... | collective-permute-start | bytes 202760 | tf_op jit(solution)/shard_map/ppermute | solution.py:10
  57.7 2.1 %collective-permute-start.3 = (bf16[8,27776]{1,0:T(8,128)(2,1)S(1)}, bf16[8,27776]{1,0:T(8,128)(2,1)S(1)}, u32[]{:S(2)}, u32[]{:S(2)}) collective-permute-start(bf16[8,27776]{1,0:T(8,128)(2,1)S(1)} %slice.194), channel_id=1, source_target_pairs={{0,8},{8,0},{16,24},{24,16},{32,40},{40,32},{48,56},{56,48},{64,72... | collective-permute-start | bytes 1333256 | tf_op jit(solution)/shard_map/ppermute | solution.py:111
  61.1 0.7 maximum_bitcast_fusion.2
  62.0 0.7 maximum_bitcast_fusion.1
  63.4 1.0 %copy.267 = bf16[128,4,2,262]{0,2,3,1:T(2,128)(2,1)S(1)} copy(bf16[128,4,2,262]{3,1,0,2:T(4,128)(2,1)S(1)} %maximum_bitcast_fusion) | data formatting | bytes 1073152
  65.6 2.0 %reshape.176 = bf16[8,48,1155]{2,1,0:T(8,128)(2,1)S(1)} reshape(bf16[8,55440]{1,0:T(8,128)(2,1)S(1)} %fusion.2) | data formatting | bytes 1774080 | tf_op jit(solution)/shard_map/reshape | solution.py:117
  68.3 0.9 %fusion.16 = bf16[2,16,33,128]{3,1,2,0:T(8,128)(2,1)S(1)} fusion(bf16[128,4,2,8,35]{0,2,4,3,1:T(2,128)(2,1)S(1)} %fusion.4, bf16[128,3,3,128]{3,2,1,0:T(4,128)(2,1)S(1)} %reshape.177, f32[128]{0:T(128)S(1)} %add.183, pred[16,33]{0,1:T(8,128)(4,1)S(1)} %copy-done.2), kind=kOutput, calls=%fused_computation.24 | convolution fusion | flops 312913920 | bytes 1139728 | tf_op jit(solution)/shard_map/conv_general_dilated | solution.py:49
  72.5 0.8 reduce.5
  73.4 15.9 %all_to_all.24 = bf16[8,2,6144]{2,1,0:T(2,128)(2,1)S(1)} all-to-all(bf16[8,2,6144]{2,1,0:T(2,128)(2,1)S(1)} %reshape.209), channel_id=1, replica_groups=mesh['space'=64,'chan'=8] {'chan'}, dimensions={0} | all-to-all | bytes 393216 | tf_op jit(solution)/shard_map/all_to_all | solution.py:152
  89.8 0.7 broadcast_in_dim_reshape.8
  90.5 0.7 broadcast_in_dim_reshape.9
  (101 shorter events, 12.9 us)
Async XLA Ops:
  0.6 25.2 %collective-permute-start.2 = (s32[2048]{0:T(1024)}, s32[2048]{0:T(1024)S(1)}, u32[]{:S(2)}, u32[]{:S(2)}) collective-permute-start(s32[2048]{0:T(1024)} %bitcast.97), channel_id=1, source_target_pairs={{0,8},{8,16},{16,24},{24,32},{32,40},{40,48},{48,56},{56,64},{64,7... | collective-permute-start | bytes 24584 | tf_op jit(solution)/shard_map/ppermute | solution.py:10
  12.4 13.1 %copy-start.1 = (s32[1,2048]{1,0:T(1,128)S(1)}, s32[1,2048]{1,0:T(1,128)}, u32[]{:S(2)}) copy-start(s32[1,2048]{1,0:T(1,128)} %param.9) | copy-start | bytes 24580
  12.4 13.2 %copy-start = (s32[1,2048]{1,0:T(1,128)S(1)}, s32[1,2048]{1,0:T(1,128)}, u32[]{:S(2)}) copy-start(s32[1,2048]{1,0:T(1,128)} %param.8) | copy-start | bytes 24580
  13.6 33.9 %all-to-all-start = ((bf16[8,2,18432]{2,1,0:T(2,128)(2,1)}), bf16[8,2,18432]{2,1,0:T(2,128)(2,1)S(1)}, u32[]{:S(2)}, u32[]{:S(2)}) async-start(bf16[8,2,18432]{2,1,0:T(2,128)(2,1)} %reshape.207), calls=%async_computation | async-start | bytes 1179648 | tf_op jit(solution)/shard_map/all_to_all | solution.py:106
  49.5 10.7 %collective-permute-start = (bf16[128,2,264]{2,1,0:T(2,128)(2,1)S(1)}, bf16[128,2,264]{2,1,0:T(2,128)(2,1)S(1)}, u32[]{:S(2)}, u32[]{:S(2)}) collective-permute-start(bf16[128,2,264]{2,1,0:T(2,128)(2,1)S(1)} %reshape.175), channel_id=1, source_target_pairs={{0,8},{8,16},{16,24},{24,32},{32,40},{40,48},{48,56},{56,64},{64,7... | collective-permute-start | bytes 405512 | tf_op jit(solution)/shard_map/ppermute | solution.py:10
  51.8 8.0 %collective-permute-start.1 = (bf16[128,264]{0,1:T(8,128)(2,1)S(1)}, bf16[128,264]{0,1:T(8,128)(2,1)S(1)}, u32[]{:S(2)}, u32[]{:S(2)}) collective-permute-start(bf16[128,264]{0,1:T(8,128)(2,1)S(1)} %bitcast.88), channel_id=1, source_target_pairs={{8,0},{16,8},{24,16},{32,24},{40,32},{48,40},{56,48},{64,56},{72,6... | collective-permute-start | bytes 202760 | tf_op jit(solution)/shard_map/ppermute | solution.py:10
  57.7 7.6 %collective-permute-start.3 = (bf16[8,27776]{1,0:T(8,128)(2,1)S(1)}, bf16[8,27776]{1,0:T(8,128)(2,1)S(1)}, u32[]{:S(2)}, u32[]{:S(2)}) collective-permute-start(bf16[8,27776]{1,0:T(8,128)(2,1)S(1)} %slice.194), channel_id=1, source_target_pairs={{0,8},{8,0},{16,24},{24,16},{32,40},{40,32},{48,56},{56,48},{64,72... | collective-permute-start | bytes 1333256 | tf_op jit(solution)/shard_map/ppermute | solution.py:111
  67.6 0.7 copy-start.2
  71.2 0.7 copy-start.3

commit v9 on v8

--- a/solution.py
+++ b/solution.py
@@ -95,15 +95,17 @@
     )
     taps = flat_w.shape[1]
     packed_w = jnp.concatenate(
-        [flat_w, split3(jnp.concatenate([first_bias, second_bias]))], axis=1
-    ).reshape(-1)
+        [flat_w.reshape(-1), split3(jnp.concatenate([first_bias, second_bias])).reshape(-1)]
+    )
     w_len = packed_w.shape[0]
     half = -(-w_len // 256) * 128
     packed_w = jnp.pad(packed_w, (0, 2 * half - w_len))
     second = (lax.axis_index("space") % 2) == 1
     mine = lax.dynamic_slice_in_dim(packed_w, jnp.where(second, half, 0), half)
     sends = jnp.concatenate([wins, jnp.broadcast_to(mine[None], (groups, half))], 1)
-    got = lax.all_to_all(pad_to(sends, 1024), "chan", 0, 0, tiled=True)
+    got = lax.all_to_all(
+        pad_to(sends, 256).reshape(groups, 2, -1), "chan", 0, 0, tiled=True
+    ).reshape(groups, -1)
 
     tile = got[:, :feat_len].reshape(groups * chans, rows, width + 2)
     own_half = got[:, feat_len : feat_len + half]
@@ -114,11 +116,12 @@
         jnp.concatenate([other_half, own_half], 1),
         jnp.concatenate([own_half, other_half], 1),
     )
-    every = every[:, :w_len].reshape(groups, n1 + n2, taps + 3)
-    w1 = every[:, :n1, :taps].reshape((-1,) + first_weight.shape[1:])
-    w2 = every[:, n1:, :taps].reshape((-1,) + second_weight.shape[1:])
-    b1 = join3(every[:, :n1, taps:]).reshape(-1)
-    b2 = join3(every[:, n1:, taps:]).reshape(-1)
+    w_all = every[:, : (n1 + n2) * taps].reshape(groups, n1 + n2, taps)
+    b_all = every[:, (n1 + n2) * taps : w_len].reshape(groups, n1 + n2, 3)
+    w1 = w_all[:, :n1].reshape((-1,) + first_weight.shape[1:])
+    w2 = w_all[:, n1:].reshape((-1,) + second_weight.shape[1:])
+    b1 = join3(b_all[:, :n1]).reshape(-1)
+    b2 = join3(b_all[:, n1:]).reshape(-1)
 
     prior_lower_map = shifted(lower_map, "space", 1)
     prior = shifted(tile, "space", 1)
@@ -150,8 +153,9 @@
     hidden_part = hidden_win[:, :, halo - 1 : halo - 1 + block].reshape(groups, -1)
     coarse_part = coarse_win.reshape(groups, -1)
     back = lax.all_to_all(
-        jnp.concatenate([hidden_part, coarse_part], 1), "chan", 0, 0, tiled=True
-    )
+        jnp.concatenate([hidden_part, coarse_part], 1).reshape(groups, 2, -1),
+        "chan", 0, 0, tiled=True,
+    ).reshape(groups, -1)
     h_len = hidden_part.shape[1]
     hidden_out = back[:, :h_len].reshape((groups, chans, rows, block))
     hidden_out = jnp.moveaxis(hidden_out, 0, 2).reshape(chans, rows, cycle)

time: 91.7 us -> 84.9 us (0.926)
  local copies, waits for them, and re-layouts: 19.3 us -> 14.3 us
  other arithmetic: 8.18 us -> 6.17 us
    unnamed x20 -> x24, local copies, waits for them, and re-layouts: 6.43 us -> 2.49 us
    all_to_all x3 -> x0, other arithmetic: 1.85 us -> none  [the longest x1 1.07 us: per_device(): got = lax.all_to_all(pad_to(sends, 1024), 'chan', 0, 0, tiled=True)]
    reshape x4 -> x6, local copies, waits for them, and re-layouts: 2.5 us -> 1.66 us  [the longest x1 0.99 us: per_device(): pad_to(sends, 256).reshape(groups, 2, -1)]
  transfers between devices with their start and end apart: 5 -> 5, of which waited for: 1 -> 1; matrix products, arithmetic and copies ran while one was open for 19% -> 16% of each run, Pallas kernels for 0% -> 0%
where the time goes in v9:
time: 84.9 us; the launch traced here: 84.3 us
  starting transfers between devices  23.8 us (28%)
  waiting for transfers between devices  21.4 us (25%)
  blocking collectives  15.9 us (19%)
  local copies, waits for them, and re-layouts  14.3 us (17%)
  other arithmetic  6.17 us (7%)
  between operations  1.39 us (2%)
  matrix products  1.31 us (2%)
    all_to_all x1, waiting for transfers between devices, per_device(): lax.all_to_all(pad_to(sends, 256).reshape(groups, 2, -1), 'chan', 0, 0, t...  21.4 us
    all_to_all x1, blocking collectives, per_device(): lax.all_to_all(jnp.concatenate([hidden_part, coarse_part], 1).reshape(gro...  15.9 us
    all_to_all x1, starting transfers between devices, per_device(): lax.all_to_all(pad_to(sends, 256).reshape(groups, 2, -1), 'chan', 0, 0, t...  12 us
    ppermute x3, starting transfers between devices, shifted(): return lax.ppermute(array, axis, pairs)  9.73 us
    unnamed x24, local copies, waits for them, and re-layouts  2.49 us
    ppermute x1, starting transfers between devices, per_device(): lax.ppermute(own_half, 'space', [(i, i ^ 1) for i in range(spaces)])  2.1 us
    slice x3, local copies, waits for them, and re-layouts, column_windows(): jnp.roll(padded, halo, axis=-1).reshape(lead + (groups, block))[..., :halo]  2.04 us
    another operation x3, other arithmetic, per_device(): jnp.stack([jnp.concatenate([above[:, None], inner, below[:, None]], axis=...  2.04 us
  transfers between devices with their start and end apart: 5, of which 1 were waited for; matrix products, arithmetic and copies ran while one was open for 16% of the time, Pallas kernels for 0%

profile of v9, /device:TPU:64, one launch (start us, length us, event | category | flops | bytes accessed | tf_op | source)
XLA Modules:
  0.0 84.3 jit_solution(576521904283064478)
XLA Ops:
  0.6 2.1 %collective-permute-start.2 = (s32[2048]{0:T(1024)}, s32[2048]{0:T(1024)S(1)}, u32[]{:S(2)}, u32[]{:S(2)}) collective-permute-start(s32[2048]{0:T(1024)} %bitcast.104), channel_id=1, source_target_pairs={{0,8},{8,16},{16,24},{24,32},{32,40},{40,48},{48,56},{56,64},{64,7... | collective-permute-start | bytes 24584 | tf_op jit(solution)/shard_map/ppermute | solution.py:10
  2.7 1.0 %reshape_squeeze.6 = bf16[16,2,8,256]{3,2,1,0:T(8,128)(2,1)S(1)} reshape(bf16[1,16,2,2048]{3,2,1,0:T(2,128)(2,1)} %param.7) | data formatting | bytes 262144 | tf_op jit(solution)/shard_map/reshape;squeeze | solution.py:64
  3.7 0.8 fusion.88
  4.5 1.2 %fusion.89 = (bf16[16,2,2044]{2,1,0:T(2,128)(2,1)S(1)}, bf16[16,2,2044]{2,1,0:T(2,128)(2,1)S(1)}) fusion(bf16[16,2,2048]{2,1,0:T(2,128)(2,1)} %bitcast.90), kind=kLoop, calls=%fused_computation.140 | loop fusion | bytes 523264 | tf_op jit(solution)/shard_map/jit(_roll_static)/slice | solution.py:63
  5.8 0.8 reduce-precision_convert_fusion.1
  8.0 0.5 maximum_bitcast_fusion.4
  9.1 1.0 %reshape.189 = bf16[8,2,18176]{2,1,0:T(2,128)(2,1)} reshape(bf16[8,36352]{1,0:T(8,128)(2,1)S(1)} %pad.9) | data formatting | bytes 1163264 | tf_op jit(solution)/shard_map/reshape | solution.py:107
  10.1 12.0 %all-to-all-start = ((bf16[8,2,18176]{2,1,0:T(2,128)(2,1)}), bf16[8,2,18176]{2,1,0:T(2,128)(2,1)S(1)}, u32[]{:S(2)}, u32[]{:S(2)}) async-start(bf16[8,2,18176]{2,1,0:T(2,128)(2,1)} %reshape.189), calls=%async_computation | async-start | bytes 1163264 | tf_op jit(solution)/shard_map/all_to_all | solution.py:106
  22.5 21.4 %all-to-all-done = bf16[8,2,18176]{2,1,0:T(2,128)(2,1)S(1)} async-done(((bf16[8,2,18176]{2,1,0:T(2,128)(2,1)}), bf16[8,2,18176]{2,1,0:T(2,128)(2,1)S(1)}, u32[]{:S(2)}, u32[]{:S(2)}) %all-to-all-start) | async-done | bytes 581664 | tf_op jit(solution)/shard_map/all_to_all | solution.py:106
  44.1 0.4 reshape.191
  44.8 2.1 %collective-permute-start = (bf16[128,2,264]{2,1,0:T(2,128)(2,1)S(1)}, bf16[128,2,264]{2,1,0:T(2,128)(2,1)S(1)}, u32[]{:S(2)}, u32[]{:S(2)}) collective-permute-start(bf16[128,2,264]{2,1,0:T(2,128)(2,1)S(1)} %reshape.191), channel_id=1, source_target_pairs={{0,8},{8,16},{16,24},{24,32},{32,40},{40,48},{48,56},{56,64},{64,7... | collective-permute-start | bytes 405512 | tf_op jit(solution)/shard_map/ppermute | solution.py:10
  47.0 5.6 %collective-permute-start.1 = (bf16[128,264]{0,1:T(8,128)(2,1)S(1)}, bf16[128,264]{0,1:T(8,128)(2,1)S(1)}, u32[]{:S(2)}, u32[]{:S(2)}) collective-permute-start(bf16[128,264]{0,1:T(8,128)(2,1)S(1)} %bitcast.93), channel_id=1, source_target_pairs={{8,0},{16,8},{24,16},{32,24},{40,32},{48,40},{56,48},{64,56},{72,6... | collective-permute-start | bytes 202760 | tf_op jit(solution)/shard_map/ppermute | solution.py:10
  53.0 2.1 %collective-permute-start.3 = (bf16[8,27776]{1,0:T(8,128)(2,1)S(1)}, bf16[8,27776]{1,0:T(8,128)(2,1)S(1)}, u32[]{:S(2)}, u32[]{:S(2)}) collective-permute-start(bf16[8,27776]{1,0:T(8,128)(2,1)S(1)} %slice.198), channel_id=1, source_target_pairs={{0,8},{8,0},{16,24},{24,16},{32,40},{40,32},{48,56},{56,48},{64,72... | collective-permute-start | bytes 1333256 | tf_op jit(solution)/shard_map/ppermute | solution.py:113
  56.4 0.7 maximum_bitcast_fusion.2
  57.3 0.7 maximum_bitcast_fusion.1
  58.0 0.6 maximum_bitcast_fusion
  58.6 1.0 %copy.236 = bf16[128,4,2,262]{0,2,3,1:T(2,128)(2,1)S(1)} copy(bf16[128,4,2,262]{3,1,0,2:T(4,128)(2,1)S(1)} %maximum_bitcast_fusion) | data formatting | bytes 1073152
  59.6 0.4 pad.10.clone
  60.1 0.5 fusion.3
  61.9 0.9 %fusion.15 = bf16[2,16,33,128]{3,1,2,0:T(8,128)(2,1)S(1)} fusion(bf16[128,4,2,8,35]{0,2,4,3,1:T(2,128)(2,1)S(1)} %fusion.3, bf16[128,3,3,128]{3,2,1,0:T(4,128)(2,1)S(1)} %reshape.193, f32[128]{0:T(128)S(1)} %add.183, pred[16,33]{0,1:T(8,128)(4,1)S(1)} %copy-done.5), kind=kOutput, calls=%fused_computation.20 | convolution fusion | flops 312913920 | bytes 1139728 | tf_op jit(solution)/shard_map/conv_general_dilated | solution.py:49
  65.7 0.4 copy-done.6
  67.0 15.9 %all_to_all.10 = bf16[8,2,6144]{2,1,0:T(2,128)(2,1)S(1)} all-to-all(bf16[8,2,6144]{2,1,0:T(2,128)(2,1)S(1)} %copy.228), channel_id=1, replica_groups=mesh['space'=64,'chan'=8] {'chan'}, dimensions={0} | all-to-all | bytes 393216 | tf_op jit(solution)/shard_map/all_to_all | solution.py:155
  83.0 0.7 broadcast_in_dim_reshape.8
  83.7 0.7 broadcast_in_dim_reshape.9
  (109 shorter events, 9.6 us)
Async XLA Ops:
  0.6 6.2 %copy-start.2 = (bf16[16,3,3,128]{3,0,2,1:T(8,128)(2,1)S(1)}, bf16[16,3,3,128]{3,0,2,1:T(8,128)(2,1)}, u32[]{:S(2)}) copy-start(bf16[16,3,3,128]{3,0,2,1:T(8,128)(2,1)} %param.10) | copy-start | bytes 110596
  0.6 6.2 %copy-start.1 = (bf16[32,3,3,128]{3,0,2,1:T(8,128)(2,1)S(1)}, bf16[32,3,3,128]{3,0,2,1:T(8,128)(2,1)}, u32[]{:S(2)}) copy-start(bf16[32,3,3,128]{3,0,2,1:T(8,128)(2,1)} %param.12) | copy-start | bytes 221188
  0.6 21.8 %collective-permute-start.2 = (s32[2048]{0:T(1024)}, s32[2048]{0:T(1024)S(1)}, u32[]{:S(2)}, u32[]{:S(2)}) collective-permute-start(s32[2048]{0:T(1024)} %bitcast.104), channel_id=1, source_target_pairs={{0,8},{8,16},{16,24},{24,32},{32,40},{40,48},{48,56},{56,64},{64,7... | collective-permute-start | bytes 24584 | tf_op jit(solution)/shard_map/ppermute | solution.py:10
  10.1 12.0 %copy-start.4 = (s32[1,2048]{1,0:T(1,128)S(1)}, s32[1,2048]{1,0:T(1,128)}, u32[]{:S(2)}) copy-start(s32[1,2048]{1,0:T(1,128)} %param.9) | copy-start | bytes 24580
  10.1 12.1 %copy-start.3 = (s32[1,2048]{1,0:T(1,128)S(1)}, s32[1,2048]{1,0:T(1,128)}, u32[]{:S(2)}) copy-start(s32[1,2048]{1,0:T(1,128)} %param.8) | copy-start | bytes 24580
  10.1 33.9 %all-to-all-start = ((bf16[8,2,18176]{2,1,0:T(2,128)(2,1)}), bf16[8,2,18176]{2,1,0:T(2,128)(2,1)S(1)}, u32[]{:S(2)}, u32[]{:S(2)}) async-start(bf16[8,2,18176]{2,1,0:T(2,128)(2,1)} %reshape.189), calls=%async_computation | async-start | bytes 1163264 | tf_op jit(solution)/shard_map/all_to_all | solution.py:106
  44.8 10.7 %collective-permute-start = (bf16[128,2,264]{2,1,0:T(2,128)(2,1)S(1)}, bf16[128,2,264]{2,1,0:T(2,128)(2,1)S(1)}, u32[]{:S(2)}, u32[]{:S(2)}) collective-permute-start(bf16[128,2,264]{2,1,0:T(2,128)(2,1)S(1)} %reshape.191), channel_id=1, source_target_pairs={{0,8},{8,16},{16,24},{24,32},{32,40},{40,48},{48,56},{56,64},{64,7... | collective-permute-start | bytes 405512 | tf_op jit(solution)/shard_map/ppermute | solution.py:10
  47.0 8.1 %collective-permute-start.1 = (bf16[128,264]{0,1:T(8,128)(2,1)S(1)}, bf16[128,264]{0,1:T(8,128)(2,1)S(1)}, u32[]{:S(2)}, u32[]{:S(2)}) collective-permute-start(bf16[128,264]{0,1:T(8,128)(2,1)S(1)} %bitcast.93), channel_id=1, source_target_pairs={{8,0},{16,8},{24,16},{32,24},{40,32},{48,40},{56,48},{64,56},{72,6... | collective-permute-start | bytes 202760 | tf_op jit(solution)/shard_map/ppermute | solution.py:10
  53.0 7.6 %collective-permute-start.3 = (bf16[8,27776]{1,0:T(8,128)(2,1)S(1)}, bf16[8,27776]{1,0:T(8,128)(2,1)S(1)}, u32[]{:S(2)}, u32[]{:S(2)}) collective-permute-start(bf16[8,27776]{1,0:T(8,128)(2,1)S(1)} %slice.198), channel_id=1, source_target_pairs={{0,8},{8,0},{16,24},{24,16},{32,40},{40,32},{48,56},{56,48},{64,72... | collective-permute-start | bytes 1333256 | tf_op jit(solution)/shard_map/ppermute | solution.py:113
  61.2 0.7 copy-start.5
  63.3 0.7 copy-start
  64.1 0.9 %slice-start = ((bf16[128,2,260]{0,1,2:T(2,128)(2,1)}), bf16[128,2,258]{0,1,2:T(2,128)(2,1)S(1)}, s32[]{:S(2)}) async-start(bf16[128,2,260]{0,1,2:T(2,128)(2,1)} %copy-done), calls=%async_computation.2 | async-start | bytes 264192 | tf_op jit(solution)/shard_map/slice | solution.py:149
  65.4 0.7 copy-start.6

commit v10 on v9

--- a/solution.py
+++ b/solution.py
@@ -10,20 +10,32 @@
     return lax.ppermute(array, axis, pairs)
 
 
-def remap_window(source, table, first_col, width):
+def rim_code(table, first_col, width):
     cycle = table.shape[0]
     cols = (first_col + jnp.arange(width)) % cycle
     picked = lax.dynamic_slice_in_dim(
         jnp.concatenate([table, table], axis=0), first_col % cycle, width, axis=0
     )
+    code = jnp.where(picked == (cols + cycle - 1) % cycle, -1, 2)
+    code = jnp.where(picked == (cols + 1) % cycle, 1, code)
+    code = jnp.where(picked == cols, 0, code)
+    return code.astype(jnp.bfloat16)
+
+
+def apply_code(source, code):
+    width = code.shape[0]
     same = source[..., 1 : width + 1]
     prev = source[..., 0:width]
     nxt = source[..., 2 : width + 2]
     zero = jnp.zeros_like(same)
-    out = jnp.where(picked == (cols + cycle - 1) % cycle, prev, zero)
-    out = jnp.where(picked == (cols + 1) % cycle, nxt, out)
-    out = jnp.where(picked == cols, same, out)
+    out = jnp.where(code == -1, prev, zero)
+    out = jnp.where(code == 1, nxt, out)
+    out = jnp.where(code == 0, same, out)
     return out
+
+
+def remap_window(source, table, first_col, width):
+    return apply_code(source, rim_code(table, first_col, width))
 
 
 def remap_full(row, table):
@@ -123,13 +135,16 @@
     b1 = join3(b_all[:, :n1]).reshape(-1)
     b2 = join3(b_all[:, n1:]).reshape(-1)
 
-    prior_lower_map = shifted(lower_map, "space", 1)
-    prior = shifted(tile, "space", 1)
+    start = me * block - halo
+    lower_code = rim_code(lower_map, start, width)
+    code_rows = jnp.broadcast_to(jnp.pad(lower_code, (1, 1))[None, None], (1, rows, width + 2))
+    prior_ext = shifted(jnp.concatenate([tile, code_rows], 0), "space", 1)
+    prior = prior_ext[: groups * chans]
+    prior_code = prior_ext[groups * chans, 0, 1 : width + 1]
     below_src = shifted(tile[:, 0, :], "space", -1)
-    start = me * block - halo
     above = remap_window(prior[:, rows - 1, :], upper_map, start, width)
-    below = remap_window(below_src, lower_map, start, width)
-    prior_below = remap_window(tile[:, 0, :], prior_lower_map, start, width)
+    below = apply_code(below_src, lower_code)
+    prior_below = apply_code(tile[:, 0, :], prior_code)
     inner = tile[:, :, 1 : width + 1]
     prior_inner = prior[:, :, 1 : width + 1]
     window = jnp.stack(

time: 84.9 us -> 81.5 us (0.960)
  the two profiles are of different devices: /device:TPU:64 before, /device:TPU:192 now
where the time goes in v10:
time: 81.5 us; the launch traced here: 81.1 us
  starting transfers between devices  23.2 us (28%)
  waiting for transfers between devices  21.1 us (26%)
  local copies, waits for them, and re-layouts  14.4 us (18%)
  blocking collectives  13.3 us (16%)
  other arithmetic  6.42 us (8%)
  between operations  1.38 us (2%)
  matrix products  1.31 us (2%)
    all_to_all x1, waiting for transfers between devices, per_device(): lax.all_to_all(pad_to(sends, 256).reshape(groups, 2, -1), 'chan', 0, 0, t...  16.4 us
    all_to_all x1, blocking collectives, per_device(): lax.all_to_all(jnp.concatenate([hidden_part, coarse_part], 1).reshape(gro...  13.3 us
    ppermute x2, starting transfers between devices, shifted(): return lax.ppermute(array, axis, pairs)  11 us
    all_to_all x1, starting transfers between devices, per_device(): lax.all_to_all(pad_to(sends, 256).reshape(groups, 2, -1), 'chan', 0, 0, t...  10.2 us
    ppermute x2, waiting for transfers between devices, shifted(): return lax.ppermute(array, axis, pairs)  4.69 us
    unnamed x24, local copies, waits for them, and re-layouts  2.48 us
    ppermute x1, starting transfers between devices, per_device(): lax.ppermute(own_half, 'space', [(i, i ^ 1) for i in range(spaces)])  2.1 us
    slice x3, local copies, waits for them, and re-layouts, column_windows(): jnp.roll(padded, halo, axis=-1).reshape(lead + (groups, block))[..., :halo]  2.04 us
  transfers between devices with their start and end apart: 4, of which 2 were waited for; matrix products, arithmetic and copies ran while one was open for 8% of the time, Pallas kernels for 0%

profile of v10, /device:TPU:192, one launch (start us, length us, event | category | flops | bytes accessed | tf_op | source)
XLA Modules:
  0.0 81.1 jit_solution(14480911248488926281)
XLA Ops:
  0.7 1.0 %reshape_squeeze.6 = bf16[16,2,8,256]{3,2,1,0:T(8,128)(2,1)S(1)} reshape(bf16[1,16,2,2048]{3,2,1,0:T(2,128)(2,1)} %param.7) | data formatting | bytes 262144 | tf_op jit(solution)/shard_map/reshape;squeeze | solution.py:76
  1.7 0.8 fusion.73
  2.5 1.2 %fusion.74 = (bf16[16,2,2044]{2,1,0:T(2,128)(2,1)S(1)}, bf16[16,2,2044]{2,1,0:T(2,128)(2,1)S(1)}) fusion(bf16[16,2,2048]{2,1,0:T(2,128)(2,1)} %bitcast.90), kind=kLoop, calls=%fused_computation.143 | loop fusion | bytes 523264 | tf_op jit(solution)/shard_map/jit(_roll_static)/slice | solution.py:75
  3.7 0.8 reduce-precision_convert_fusion.1
  6.0 0.5 maximum_bitcast_fusion.4
  7.0 1.0 %reshape.198 = bf16[8,2,18176]{2,1,0:T(2,128)(2,1)} reshape(bf16[8,36352]{1,0:T(8,128)(2,1)S(1)} %pad.13) | data formatting | bytes 1163264 | tf_op jit(solution)/shard_map/reshape | solution.py:119
  8.0 10.2 %all-to-all-start = ((bf16[8,2,18176]{2,1,0:T(2,128)(2,1)}), bf16[8,2,18176]{2,1,0:T(2,128)(2,1)S(1)}, u32[]{:S(2)}, u32[]{:S(2)}) async-start(bf16[8,2,18176]{2,1,0:T(2,128)(2,1)} %reshape.198), calls=%async_computation | async-start | bytes 1163264 | tf_op jit(solution)/shard_map/all_to_all | solution.py:118
  18.6 16.4 %all-to-all-done = bf16[8,2,18176]{2,1,0:T(2,128)(2,1)S(1)} async-done(((bf16[8,2,18176]{2,1,0:T(2,128)(2,1)}), bf16[8,2,18176]{2,1,0:T(2,128)(2,1)S(1)}, u32[]{:S(2)}, u32[]{:S(2)}) %all-to-all-start) | async-done | bytes 581664 | tf_op jit(solution)/shard_map/all_to_all | solution.py:118
  35.1 0.4 reshape.200
  35.9 9.0 %collective-permute-start.1 = (bf16[128,264]{0,1:T(8,128)(2,1)S(1)}, bf16[128,264]{0,1:T(8,128)(2,1)S(1)}, u32[]{:S(2)}, u32[]{:S(2)}) collective-permute-start(bf16[128,264]{0,1:T(8,128)(2,1)S(1)} %bitcast.93), channel_id=1, source_target_pairs={{8,0},{16,8},{24,16},{32,24},{40,32},{48,40},{56,48},{64,56},{72,6... | collective-permute-start | bytes 202760 | tf_op jit(solution)/shard_map/ppermute | solution.py:10
  45.3 1.9 %collective-permute-start = (bf16[129,2,264]{2,1,0:T(2,128)(2,1)S(1)}, bf16[129,2,264]{2,1,0:T(2,128)(2,1)S(1)}, u32[]{:S(2)}, u32[]{:S(2)}) collective-permute-start(bf16[129,2,264]{2,1,0:T(2,128)(2,1)S(1)} %pad_maximum_fusion.1), channel_id=1, source_target_pairs={{0,8},{8,16},{16,24},{24,32},{32,40},{40,48},{48,56},{56,64},{64,7... | collective-permute-start | bytes 408680 | tf_op jit(solution)/shard_map/ppermute | solution.py:10
  47.2 2.1 %collective-permute-start.2 = (bf16[8,27776]{1,0:T(8,128)(2,1)S(1)}, bf16[8,27776]{1,0:T(8,128)(2,1)S(1)}, u32[]{:S(2)}, u32[]{:S(2)}) collective-permute-start(bf16[8,27776]{1,0:T(8,128)(2,1)S(1)} %slice.206), channel_id=1, source_target_pairs={{0,8},{8,0},{16,24},{24,16},{32,40},{40,32},{48,56},{56,48},{64,72... | collective-permute-start | bytes 1333256 | tf_op jit(solution)/shard_map/ppermute | solution.py:125
  49.7 4.7 %collective-permute-done = bf16[129,2,264]{2,1,0:T(2,128)(2,1)S(1)} collective-permute-done((bf16[129,2,264]{2,1,0:T(2,128)(2,1)S(1)}, bf16[129,2,264]{2,1,0:T(2,128)(2,1)S(1)}, u32[]{:S(2)}, u32[]{:S(2)}) %collective-permute-start) | collective-permute-done | bytes 136256 | tf_op jit(solution)/shard_map/ppermute | solution.py:10
  55.8 0.7 maximum_bitcast_fusion.2
  56.7 0.7 maximum_bitcast_fusion.1
  57.4 0.6 maximum_bitcast_fusion
  58.0 1.0 %copy.236 = bf16[128,4,2,262]{0,2,3,1:T(2,128)(2,1)S(1)} copy(bf16[128,4,2,262]{3,1,0,2:T(4,128)(2,1)S(1)} %maximum_bitcast_fusion) | data formatting | bytes 1073152
  59.0 0.4 pad.15.clone
  59.5 0.5 fusion.3
  61.3 0.9 %fusion.15 = bf16[2,16,33,128]{3,1,2,0:T(8,128)(2,1)S(1)} fusion(bf16[128,4,2,8,35]{0,2,4,3,1:T(2,128)(2,1)S(1)} %fusion.3, bf16[128,3,3,128]{3,2,1,0:T(4,128)(2,1)S(1)} %reshape.202, f32[128]{0:T(128)S(1)} %add.173, pred[16,33]{0,1:T(8,128)(4,1)S(1)} %copy-done.5), kind=kOutput, calls=%fused_computation.20 | convolution fusion | flops 312913920 | bytes 1139728 | tf_op jit(solution)/shard_map/conv_general_dilated | solution.py:61
  65.1 0.4 copy-done.6
  66.3 13.3 %all_to_all.10 = bf16[8,2,6144]{2,1,0:T(2,128)(2,1)S(1)} all-to-all(bf16[8,2,6144]{2,1,0:T(2,128)(2,1)S(1)} %copy.228), channel_id=1, replica_groups=mesh['space'=64,'chan'=8] {'chan'}, dimensions={0} | all-to-all | bytes 393216 | tf_op jit(solution)/shard_map/all_to_all | solution.py:170
  79.7 0.7 broadcast_in_dim_reshape.8
  80.4 0.7 broadcast_in_dim_reshape.9
  (109 shorter events, 9.9 us)
Async XLA Ops:
  0.6 4.1 %copy-start.2 = (bf16[16,3,3,128]{3,0,2,1:T(8,128)(2,1)S(1)}, bf16[16,3,3,128]{3,0,2,1:T(8,128)(2,1)}, u32[]{:S(2)}) copy-start(bf16[16,3,3,128]{3,0,2,1:T(8,128)(2,1)} %param.10) | copy-start | bytes 110596
  0.6 4.2 %copy-start.1 = (bf16[32,3,3,128]{3,0,2,1:T(8,128)(2,1)S(1)}, bf16[32,3,3,128]{3,0,2,1:T(8,128)(2,1)}, u32[]{:S(2)}) copy-start(bf16[32,3,3,128]{3,0,2,1:T(8,128)(2,1)} %param.12) | copy-start | bytes 221188
  8.0 10.2 %copy-start.4 = (s32[1,2048]{1,0:T(1,128)S(1)}, s32[1,2048]{1,0:T(1,128)}, u32[]{:S(2)}) copy-start(s32[1,2048]{1,0:T(1,128)} %param.9) | copy-start | bytes 24580
  8.0 10.4 %copy-start.3 = (s32[1,2048]{1,0:T(1,128)S(1)}, s32[1,2048]{1,0:T(1,128)}, u32[]{:S(2)}) copy-start(s32[1,2048]{1,0:T(1,128)} %param.8) | copy-start | bytes 24580
  8.0 26.9 %all-to-all-start = ((bf16[8,2,18176]{2,1,0:T(2,128)(2,1)}), bf16[8,2,18176]{2,1,0:T(2,128)(2,1)S(1)}, u32[]{:S(2)}, u32[]{:S(2)}) async-start(bf16[8,2,18176]{2,1,0:T(2,128)(2,1)} %reshape.198), calls=%async_computation | async-start | bytes 1163264 | tf_op jit(solution)/shard_map/all_to_all | solution.py:118
  35.9 13.4 %collective-permute-start.1 = (bf16[128,264]{0,1:T(8,128)(2,1)S(1)}, bf16[128,264]{0,1:T(8,128)(2,1)S(1)}, u32[]{:S(2)}, u32[]{:S(2)}) collective-permute-start(bf16[128,264]{0,1:T(8,128)(2,1)S(1)} %bitcast.93), channel_id=1, source_target_pairs={{8,0},{16,8},{24,16},{32,24},{40,32},{48,40},{56,48},{64,56},{72,6... | collective-permute-start | bytes 202760 | tf_op jit(solution)/shard_map/ppermute | solution.py:10
  45.3 9.1 %collective-permute-start = (bf16[129,2,264]{2,1,0:T(2,128)(2,1)S(1)}, bf16[129,2,264]{2,1,0:T(2,128)(2,1)S(1)}, u32[]{:S(2)}, u32[]{:S(2)}) collective-permute-start(bf16[129,2,264]{2,1,0:T(2,128)(2,1)S(1)} %pad_maximum_fusion.1), channel_id=1, source_target_pairs={{0,8},{8,16},{16,24},{24,32},{32,40},{40,48},{48,56},{56,64},{64,7... | collective-permute-start | bytes 408680 | tf_op jit(solution)/shard_map/ppermute | solution.py:10
  47.2 12.7 %collective-permute-start.2 = (bf16[8,27776]{1,0:T(8,128)(2,1)S(1)}, bf16[8,27776]{1,0:T(8,128)(2,1)S(1)}, u32[]{:S(2)}, u32[]{:S(2)}) collective-permute-start(bf16[8,27776]{1,0:T(8,128)(2,1)S(1)} %slice.206), channel_id=1, source_target_pairs={{0,8},{8,0},{16,24},{24,16},{32,40},{40,32},{48,56},{56,48},{64,72... | collective-permute-start | bytes 1333256 | tf_op jit(solution)/shard_map/ppermute | solution.py:125
  60.6 0.7 copy-start.5
  62.7 0.7 copy-start
  63.5 0.9 %slice-start = ((bf16[128,2,260]{0,1,2:T(2,128)(2,1)}), bf16[128,2,258]{0,1,2:T(2,128)(2,1)S(1)}, s32[]{:S(2)}) async-start(bf16[128,2,260]{0,1,2:T(2,128)(2,1)} %copy-done), calls=%async_computation.2 | async-start | bytes 264192 | tf_op jit(solution)/shard_map/slice | solution.py:164
  64.8 0.7 copy-start.6

commit v11 on v10

--- a/solution.py
+++ b/solution.py
@@ -77,6 +77,20 @@
     right = jnp.roll(padded, -halo, axis=-1).reshape(lead + (groups, block))[..., block - halo :]
     wins = jnp.concatenate([left, mid, right], axis=-1)
     return jnp.moveaxis(wins, -2, 0)
+
+
+def gather_low_bits(part, share):
+    count = lax.axis_size("space")
+    me = lax.axis_index("space")
+    acc = part[None]
+    bit = share // 2
+    while bit >= 1:
+        recv = lax.ppermute(acc, "space", [(i, i ^ bit) for i in range(count)])
+        low = (me & bit) == 0
+        pair = jnp.where(low, jnp.stack([acc, recv], 1), jnp.stack([recv, acc], 1))
+        acc = pair.reshape((-1,) + part.shape)
+        bit //= 2
+    return acc
 
 
 def pad_to(flat, multiple):
@@ -110,24 +124,19 @@
         [flat_w.reshape(-1), split3(jnp.concatenate([first_bias, second_bias])).reshape(-1)]
     )
     w_len = packed_w.shape[0]
-    half = -(-w_len // 256) * 128
-    packed_w = jnp.pad(packed_w, (0, 2 * half - w_len))
-    second = (lax.axis_index("space") % 2) == 1
-    mine = lax.dynamic_slice_in_dim(packed_w, jnp.where(second, half, 0), half)
-    sends = jnp.concatenate([wins, jnp.broadcast_to(mine[None], (groups, half))], 1)
+    share = 4
+    quarter = -(-w_len // (share * 128)) * 128
+    packed_w = jnp.pad(packed_w, (0, share * quarter - w_len))
+    where_me = lax.axis_index("space") % share
+    mine = lax.dynamic_slice_in_dim(packed_w, where_me * quarter, quarter)
+    sends = jnp.concatenate([wins, jnp.broadcast_to(mine[None], (groups, quarter))], 1)
     got = lax.all_to_all(
         pad_to(sends, 256).reshape(groups, 2, -1), "chan", 0, 0, tiled=True
     ).reshape(groups, -1)
 
     tile = got[:, :feat_len].reshape(groups * chans, rows, width + 2)
-    own_half = got[:, feat_len : feat_len + half]
-    spaces = lax.axis_size("space")
-    other_half = lax.ppermute(own_half, "space", [(i, i ^ 1) for i in range(spaces)])
-    every = jnp.where(
-        second,
-        jnp.concatenate([other_half, own_half], 1),
-        jnp.concatenate([own_half, other_half], 1),
-    )
+    pieces = gather_low_bits(got[:, feat_len : feat_len + quarter], share)
+    every = jnp.moveaxis(pieces, 0, 1).reshape(groups, -1)
     w_all = every[:, : (n1 + n2) * taps].reshape(groups, n1 + n2, taps)
     b_all = every[:, (n1 + n2) * taps : w_len].reshape(groups, n1 + n2, 3)
     w1 = w_all[:, :n1].reshape((-1,) + first_weight.shape[1:])

time: 81.5 us -> 80.8 us (level)
  waiting for transfers between devices: 21.1 us -> 20.2 us
    all_to_all x1, waiting for transfers between devices: 16.4 us -> 13.9 us  [per_device(): lax.all_to_all(pad_to(sends, 256).reshape(groups, 2, -1), 'chan', 0, 0, t...]
    ppermute x2, starting transfers between devices: 11 us -> 8.71 us  [shifted(): return lax.ppermute(array, axis, pairs)]
    ppermute x1 -> x2, starting transfers between devices: 2.1 us -> 4.02 us  [gather_low_bits(): recv = lax.ppermute(acc, 'space', [(i, i ^ bit) for i in range(count)])]
    ppermute x1 -> x2, waiting for transfers between devices: 0.01 us -> 1.44 us  [gather_low_bits(): recv = lax.ppermute(acc, 'space', [(i, i ^ bit) for i in range(count)])]
  transfers between devices with their start and end apart: 4 -> 5, of which waited for: 2 -> 3; matrix products, arithmetic and copies ran while one was open for 8% -> 8% of each run, Pallas kernels for 0% -> 0%
where the time goes in v11:
time: 80.8 us; the launch traced here: 80.3 us
  starting transfers between devices  22.8 us (28%)
  waiting for transfers between devices  20.2 us (25%)
  local copies, waits for them, and re-layouts  14.4 us (18%)
  blocking collectives  13.5 us (17%)
  other arithmetic  6.68 us (8%)
  between operations  1.42 us (2%)
  matrix products  1.3 us (2%)
    all_to_all x1, waiting for transfers between devices, per_device(): lax.all_to_all(pad_to(sends, 256).reshape(groups, 2, -1), 'chan', 0, 0, t...  13.9 us
    all_to_all x1, blocking collectives, per_device(): lax.all_to_all(jnp.concatenate([hidden_part, coarse_part], 1).reshape(gro...  13.5 us
    all_to_all x1, starting transfers between devices, per_device(): lax.all_to_all(pad_to(sends, 256).reshape(groups, 2, -1), 'chan', 0, 0, t...  10 us
    ppermute x2, starting transfers between devices, shifted(): return lax.ppermute(array, axis, pairs)  8.71 us
    ppermute x2, waiting for transfers between devices, shifted(): return lax.ppermute(array, axis, pairs)  4.87 us
    ppermute x2, starting transfers between devices, gather_low_bits(): recv = lax.ppermute(acc, 'space', [(i, i ^ bit) for i in range(count)])  4.02 us
    unnamed x24, local copies, waits for them, and re-layouts  2.49 us
    slice x3, local copies, waits for them, and re-layouts, column_windows(): jnp.roll(padded, halo, axis=-1).reshape(lead + (groups, block))[..., :halo]  2.04 us
  transfers between devices with their start and end apart: 5, of which 3 were waited for; matrix products, arithmetic and copies ran while one was open for 8% of the time, Pallas kernels for 0%

profile of v11, /device:TPU:192, one launch (start us, length us, event | category | flops | bytes accessed | tf_op | source)
XLA Modules:
  0.0 80.3 jit_solution(13276517473349080053)
XLA Ops:
  0.7 1.0 %reshape_squeeze.6 = bf16[16,2,8,256]{3,2,1,0:T(8,128)(2,1)S(1)} reshape(bf16[1,16,2,2048]{3,2,1,0:T(2,128)(2,1)} %param.7) | data formatting | bytes 262144 | tf_op jit(solution)/shard_map/reshape;squeeze | solution.py:76
  1.7 0.8 fusion.73
  2.5 1.2 %fusion.74 = (bf16[16,2,2044]{2,1,0:T(2,128)(2,1)S(1)}, bf16[16,2,2044]{2,1,0:T(2,128)(2,1)S(1)}) fusion(bf16[16,2,2048]{2,1,0:T(2,128)(2,1)} %bitcast.103), kind=kLoop, calls=%fused_computation.147 | loop fusion | bytes 523264 | tf_op jit(solution)/shard_map/jit(_roll_static)/slice | solution.py:75
  3.7 0.8 reduce-precision_convert_fusion.1
  6.0 0.5 maximum_bitcast_fusion.4
  7.0 1.0 %reshape.287 = bf16[8,2,11264]{2,1,0:T(2,128)(2,1)} reshape(bf16[8,22528]{1,0:T(8,128)(2,1)S(1)} %pad.13) | data formatting | bytes 720896 | tf_op jit(solution)/shard_map/reshape | solution.py:134
  8.0 10.0 %all-to-all-start = ((bf16[8,2,11264]{2,1,0:T(2,128)(2,1)}), bf16[8,2,11264]{2,1,0:T(2,128)(2,1)S(1)}, u32[]{:S(2)}, u32[]{:S(2)}) async-start(bf16[8,2,11264]{2,1,0:T(2,128)(2,1)} %reshape.287), calls=%async_computation | async-start | bytes 720896 | tf_op jit(solution)/shard_map/all_to_all | solution.py:133
  18.4 13.9 %all-to-all-done = bf16[8,2,11264]{2,1,0:T(2,128)(2,1)S(1)} async-done(((bf16[8,2,11264]{2,1,0:T(2,128)(2,1)}), bf16[8,2,11264]{2,1,0:T(2,128)(2,1)S(1)}, u32[]{:S(2)}, u32[]{:S(2)}) %all-to-all-start) | async-done | bytes 360480 | tf_op jit(solution)/shard_map/all_to_all | solution.py:133
  33.3 6.8 %collective-permute-start.1 = (bf16[128,264]{0,1:T(8,128)(2,1)S(1)}, bf16[128,264]{0,1:T(8,128)(2,1)S(1)}, u32[]{:S(2)}, u32[]{:S(2)}) collective-permute-start(bf16[128,264]{0,1:T(8,128)(2,1)S(1)} %bitcast.106), channel_id=1, source_target_pairs={{8,0},{16,8},{24,16},{32,24},{40,32},{48,40},{56,48},{64,56},{72,6... | collective-permute-start | bytes 202760 | tf_op jit(solution)/shard_map/ppermute | solution.py:10
  40.4 1.9 %collective-permute-start = (bf16[129,2,264]{2,1,0:T(2,128)(2,1)S(1)}, bf16[129,2,264]{2,1,0:T(2,128)(2,1)S(1)}, u32[]{:S(2)}, u32[]{:S(2)}) collective-permute-start(bf16[129,2,264]{2,1,0:T(2,128)(2,1)S(1)} %pad_maximum_fusion.1), channel_id=1, source_target_pairs={{0,8},{8,16},{16,24},{24,32},{32,40},{40,48},{48,56},{56,64},{64,7... | collective-permute-start | bytes 408680 | tf_op jit(solution)/shard_map/ppermute | solution.py:10
  42.4 1.9 %collective-permute-start.2 = (bf16[1,8,13952]{2,1,0:T(8,128)(2,1)S(1)}, bf16[1,8,13952]{2,1,0:T(8,128)(2,1)S(1)}, u32[]{:S(2)}, u32[]{:S(2)}) collective-permute-start(bf16[1,8,13952]{2,1,0:T(8,128)(2,1)S(1)} %get-tuple-element.14), channel_id=1, source_target_pairs={{0,16},{8,24},{16,0},{24,8},{32,48},{40,56},{48,32},{56,40},{64,80... | collective-permute-start | bytes 669704 | tf_op jit(solution)/shard_map/ppermute | solution.py:88
  44.7 4.9 %collective-permute-done = bf16[129,2,264]{2,1,0:T(2,128)(2,1)S(1)} collective-permute-done((bf16[129,2,264]{2,1,0:T(2,128)(2,1)S(1)}, bf16[129,2,264]{2,1,0:T(2,128)(2,1)S(1)}, u32[]{:S(2)}, u32[]{:S(2)}) %collective-permute-start) | collective-permute-done | bytes 136256 | tf_op jit(solution)/shard_map/ppermute | solution.py:10
  51.1 0.7 maximum_bitcast_fusion.2
  51.8 0.7 maximum_bitcast_fusion.1
  52.5 0.6 maximum_bitcast_fusion
  53.2 1.0 %copy.234 = bf16[128,4,2,262]{0,2,3,1:T(2,128)(2,1)S(1)} copy(bf16[128,4,2,262]{3,1,0,2:T(4,128)(2,1)S(1)} %maximum_bitcast_fusion) | data formatting | bytes 1073152
  54.1 0.4 pad.15.clone
  54.6 0.5 fusion.3
  55.3 2.1 %collective-permute-start.3 = (bf16[2,8,13952]{2,1,0:T(8,128)(2,1)S(1)}, bf16[2,8,13952]{2,1,0:T(8,128)(2,1)S(1)}, u32[]{:S(2)}, u32[]{:S(2)}) collective-permute-start(bf16[2,8,13952]{2,1,0:T(8,128)(2,1)S(1)} %maximum_select_fusion.2), channel_id=1, source_target_pairs={{0,8},{8,0},{16,24},{24,16},{32,40},{40,32},{48,56},{56,48},{64,72... | collective-permute-start | bytes 1339400 | tf_op jit(solution)/shard_map/ppermute | solution.py:88
  57.5 1.4 %collective-permute-done.3 = bf16[2,8,13952]{2,1,0:T(8,128)(2,1)S(1)} collective-permute-done((bf16[2,8,13952]{2,1,0:T(8,128)(2,1)S(1)}, bf16[2,8,13952]{2,1,0:T(8,128)(2,1)S(1)}, u32[]{:S(2)}, u32[]{:S(2)}) %collective-permute-start.3) | collective-permute-done | bytes 446496 | tf_op jit(solution)/shard_map/ppermute | solution.py:88
  60.3 0.9 %fusion.15 = bf16[2,16,33,128]{3,1,2,0:T(8,128)(2,1)S(1)} fusion(bf16[128,4,2,8,35]{0,2,4,3,1:T(2,128)(2,1)S(1)} %fusion.3, bf16[128,3,3,128]{3,2,1,0:T(4,128)(2,1)S(1)} %reshape.292, f32[128]{0:T(128)S(1)} %add.176, pred[16,33]{0,1:T(8,128)(4,1)S(1)} %copy-done.5), kind=kOutput, calls=%fused_computation.19 | convolution fusion | flops 312913920 | bytes 1139728 | tf_op jit(solution)/shard_map/conv_general_dilated | solution.py:61
  65.3 13.5 %all_to_all.10 = bf16[8,2,6144]{2,1,0:T(2,128)(2,1)S(1)} all-to-all(bf16[8,2,6144]{2,1,0:T(2,128)(2,1)S(1)} %copy.226), channel_id=1, replica_groups=mesh['space'=64,'chan'=8] {'chan'}, dimensions={0} | all-to-all | bytes 393216 | tf_op jit(solution)/shard_map/all_to_all | solution.py:179
  78.9 0.7 broadcast_in_dim_reshape.8
  79.6 0.7 broadcast_in_dim_reshape.9
  (113 shorter events, 10.9 us)
Async XLA Ops:
  0.6 4.1 %copy-start.2 = (bf16[16,3,3,128]{3,0,2,1:T(8,128)(2,1)S(1)}, bf16[16,3,3,128]{3,0,2,1:T(8,128)(2,1)}, u32[]{:S(2)}) copy-start(bf16[16,3,3,128]{3,0,2,1:T(8,128)(2,1)} %param.10) | copy-start | bytes 110596
  0.6 4.2 %copy-start.1 = (bf16[32,3,3,128]{3,0,2,1:T(8,128)(2,1)S(1)}, bf16[32,3,3,128]{3,0,2,1:T(8,128)(2,1)}, u32[]{:S(2)}) copy-start(bf16[32,3,3,128]{3,0,2,1:T(8,128)(2,1)} %param.12) | copy-start | bytes 221188
  7.0 11.1 %copy-start.3 = (s32[1,2048]{1,0:T(1,128)S(1)}, s32[1,2048]{1,0:T(1,128)}, u32[]{:S(2)}) copy-start(s32[1,2048]{1,0:T(1,128)} %param.8) | copy-start | bytes 24580
  7.0 11.2 %copy-start.4 = (s32[1,2048]{1,0:T(1,128)S(1)}, s32[1,2048]{1,0:T(1,128)}, u32[]{:S(2)}) copy-start(s32[1,2048]{1,0:T(1,128)} %param.9) | copy-start | bytes 24580
  8.0 24.3 %all-to-all-start = ((bf16[8,2,11264]{2,1,0:T(2,128)(2,1)}), bf16[8,2,11264]{2,1,0:T(2,128)(2,1)S(1)}, u32[]{:S(2)}, u32[]{:S(2)}) async-start(bf16[8,2,11264]{2,1,0:T(2,128)(2,1)} %reshape.287), calls=%async_computation | async-start | bytes 720896 | tf_op jit(solution)/shard_map/all_to_all | solution.py:133
  33.3 11.0 %collective-permute-start.1 = (bf16[128,264]{0,1:T(8,128)(2,1)S(1)}, bf16[128,264]{0,1:T(8,128)(2,1)S(1)}, u32[]{:S(2)}, u32[]{:S(2)}) collective-permute-start(bf16[128,264]{0,1:T(8,128)(2,1)S(1)} %bitcast.106), channel_id=1, source_target_pairs={{8,0},{16,8},{24,16},{32,24},{40,32},{48,40},{56,48},{64,56},{72,6... | collective-permute-start | bytes 202760 | tf_op jit(solution)/shard_map/ppermute | solution.py:10
  40.4 9.1 %collective-permute-start = (bf16[129,2,264]{2,1,0:T(2,128)(2,1)S(1)}, bf16[129,2,264]{2,1,0:T(2,128)(2,1)S(1)}, u32[]{:S(2)}, u32[]{:S(2)}) collective-permute-start(bf16[129,2,264]{2,1,0:T(2,128)(2,1)S(1)} %pad_maximum_fusion.1), channel_id=1, source_target_pairs={{0,8},{8,16},{16,24},{24,32},{32,40},{40,48},{48,56},{56,64},{64,7... | collective-permute-start | bytes 408680 | tf_op jit(solution)/shard_map/ppermute | solution.py:10
  42.4 12.7 %collective-permute-start.2 = (bf16[1,8,13952]{2,1,0:T(8,128)(2,1)S(1)}, bf16[1,8,13952]{2,1,0:T(8,128)(2,1)S(1)}, u32[]{:S(2)}, u32[]{:S(2)}) collective-permute-start(bf16[1,8,13952]{2,1,0:T(8,128)(2,1)S(1)} %get-tuple-element.14), channel_id=1, source_target_pairs={{0,16},{8,24},{16,0},{24,8},{32,48},{40,56},{48,32},{56,40},{64,80... | collective-permute-start | bytes 669704 | tf_op jit(solution)/shard_map/ppermute | solution.py:88
  55.3 3.7 %collective-permute-start.3 = (bf16[2,8,13952]{2,1,0:T(8,128)(2,1)S(1)}, bf16[2,8,13952]{2,1,0:T(8,128)(2,1)S(1)}, u32[]{:S(2)}, u32[]{:S(2)}) collective-permute-start(bf16[2,8,13952]{2,1,0:T(8,128)(2,1)S(1)} %maximum_select_fusion.2), channel_id=1, source_target_pairs={{0,8},{8,0},{16,24},{24,16},{32,40},{40,32},{48,56},{56,48},{64,72... | collective-permute-start | bytes 1339400 | tf_op jit(solution)/shard_map/ppermute | solution.py:88
  59.6 0.7 copy-start.5
  61.7 0.7 copy-start
  62.5 0.9 %slice-start = ((bf16[128,2,260]{0,1,2:T(2,128)(2,1)}), bf16[128,2,258]{0,1,2:T(2,128)(2,1)S(1)}, s32[]{:S(2)}) async-start(bf16[128,2,260]{0,1,2:T(2,128)(2,1)} %copy-done), calls=%async_computation.2 | async-start | bytes 264192 | tf_op jit(solution)/shard_map/slice | solution.py:173
  63.8 0.7 copy-start.6

commit v12 on v10

--- a/solution.py
+++ b/solution.py
@@ -121,8 +121,21 @@
 
     tile = got[:, :feat_len].reshape(groups * chans, rows, width + 2)
     own_half = got[:, feat_len : feat_len + half]
+
+    start = me * block - halo
+    lower_code = rim_code(lower_map, start, width)
+    line = rows * (width + 2)
+    code_line = jnp.broadcast_to(jnp.pad(lower_code, (1, 1))[None], (rows, width + 2))
+    w_lines = -(-own_half.size // line)
+    w_flat = jnp.pad(own_half.reshape(-1), (0, w_lines * line - own_half.size))
+    outgoing = jnp.concatenate(
+        [tile.reshape(-1, line), code_line.reshape(1, line), w_flat.reshape(w_lines, line)], 0
+    )
     spaces = lax.axis_size("space")
-    other_half = lax.ppermute(own_half, "space", [(i, i ^ 1) for i in range(spaces)])
+    incoming = lax.ppermute(outgoing, "space", [(i, (i + 1) % spaces) for i in range(spaces)])
+    prior = incoming[: groups * chans].reshape(tile.shape)
+    prior_code = incoming[groups * chans].reshape(rows, width + 2)[0, 1 : width + 1]
+    other_half = incoming[groups * chans + 1 :].reshape(-1)[: own_half.size].reshape(own_half.shape)
     every = jnp.where(
         second,
         jnp.concatenate([other_half, own_half], 1),
@@ -135,14 +148,10 @@
     b1 = join3(b_all[:, :n1]).reshape(-1)
     b2 = join3(b_all[:, n1:]).reshape(-1)
 
-    start = me * block - halo
-    lower_code = rim_code(lower_map, start, width)
-    code_rows = jnp.broadcast_to(jnp.pad(lower_code, (1, 1))[None, None], (1, rows, width + 2))
-    prior_ext = shifted(jnp.concatenate([tile, code_rows], 0), "space", 1)
-    prior = prior_ext[: groups * chans]
-    prior_code = prior_ext[groups * chans, 0, 1 : width + 1]
     below_src = shifted(tile[:, 0, :], "space", -1)
+    has_prior = lax.axis_index("space") > 0
     above = remap_window(prior[:, rows - 1, :], upper_map, start, width)
+    above = jnp.where(has_prior, above, jnp.zeros_like(above))
     below = apply_code(below_src, lower_code)
     prior_below = apply_code(tile[:, 0, :], prior_code)
     inner = tile[:, :, 1 : width + 1]
@@ -158,7 +167,6 @@
     pre1 = conv(window, w1, (1, 1))
     both = jax.nn.gelu(pre1 + b1[None, :, None, None]).astype(jnp.bfloat16)
     hidden_win = both[0]
-    has_prior = lax.axis_index("space") > 0
     rim_src = jnp.where(has_prior, both[1, :, 0, :], jnp.zeros_like(both[1, :, 0, :]))
     rim = remap_window(rim_src, upper_map, me * block - 1, block + 2)
     stacked = jnp.concatenate([rim[:, None], hidden_win[:, :, 1 : block + 3]], axis=1)

time: 81.5 us -> 83.4 us (1.023)
  the two profiles are of different devices: /device:TPU:192 before, /device:TPU:64 now
where the time goes in v12:
time: 83.4 us; the launch traced here: 82.9 us
  waiting for transfers between devices  25.4 us (30%)
  starting transfers between devices  19.8 us (24%)
  local copies, waits for them, and re-layouts  17.3 us (21%)
  blocking collectives  13.3 us (16%)
  other arithmetic  4.34 us (5%)
  between operations  1.41 us (2%)
  matrix products  1.31 us (2%)
    all_to_all x1, waiting for transfers between devices, per_device(): lax.all_to_all(pad_to(sends, 256).reshape(groups, 2, -1), 'chan', 0, 0, t...  20.5 us
    all_to_all x1, blocking collectives, per_device(): lax.all_to_all(jnp.concatenate([hidden_part, coarse_part], 1).reshape(gro...  13.3 us
    all_to_all x1, starting transfers between devices, per_device(): lax.all_to_all(pad_to(sends, 256).reshape(groups, 2, -1), 'chan', 0, 0, t...  12 us
    ppermute x1, starting transfers between devices, shifted(): return lax.ppermute(array, axis, pairs)  5.93 us
    ppermute x1, waiting for transfers between devices, per_device(): lax.ppermute(outgoing, 'space', [(i, (i + 1) % spaces) for i in range(spa...  3.77 us
    unnamed x26, local copies, waits for them, and re-layouts  2.47 us
    slice x3, local copies, waits for them, and re-layouts, column_windows(): jnp.roll(padded, halo, axis=-1).reshape(lead + (groups, block))[..., :halo]  2.04 us
    ppermute x1, starting transfers between devices, per_device(): lax.ppermute(outgoing, 'space', [(i, (i + 1) % spaces) for i in range(spa...  1.92 us
  transfers between devices with their start and end apart: 3, of which 3 were waited for; matrix products, arithmetic and copies ran while one was open for 2% of the time, Pallas kernels for 0%

profile of v12, /device:TPU:64, one launch (start us, length us, event | category | flops | bytes accessed | tf_op | source)
XLA Modules:
  0.0 82.9 jit_solution(1164282773527457435)
XLA Ops:
  0.7 1.0 %reshape_squeeze.9 = bf16[16,2,8,256]{3,2,1,0:T(8,128)(2,1)S(1)} reshape(bf16[1,16,2,2048]{3,2,1,0:T(2,128)(2,1)} %param.7) | data formatting | bytes 262144 | tf_op jit(solution)/shard_map/reshape;squeeze | solution.py:76
  1.7 0.8 fusion.74
  2.5 1.2 %fusion.75 = (bf16[16,2,2044]{2,1,0:T(2,128)(2,1)S(1)}, bf16[16,2,2044]{2,1,0:T(2,128)(2,1)S(1)}) fusion(bf16[16,2,2048]{2,1,0:T(2,128)(2,1)} %bitcast.92), kind=kLoop, calls=%fused_computation.146 | loop fusion | bytes 523264 | tf_op jit(solution)/shard_map/jit(_roll_static)/slice | solution.py:75
  3.7 0.8 reduce-precision_convert_fusion.1
  6.0 0.5 maximum_bitcast_fusion.4
  7.0 1.0 %reshape.214 = bf16[8,2,18176]{2,1,0:T(2,128)(2,1)} reshape(bf16[8,36352]{1,0:T(8,128)(2,1)S(1)} %pad.17) | data formatting | bytes 1163264 | tf_op jit(solution)/shard_map/reshape | solution.py:119
  8.0 12.0 %all-to-all-start = ((bf16[8,2,18176]{2,1,0:T(2,128)(2,1)}), bf16[8,2,18176]{2,1,0:T(2,128)(2,1)S(1)}, u32[]{:S(2)}, u32[]{:S(2)}) async-start(bf16[8,2,18176]{2,1,0:T(2,128)(2,1)} %reshape.214), calls=%async_computation | async-start | bytes 1163264 | tf_op jit(solution)/shard_map/all_to_all | solution.py:118
  20.4 20.5 %all-to-all-done = bf16[8,2,18176]{2,1,0:T(2,128)(2,1)S(1)} async-done(((bf16[8,2,18176]{2,1,0:T(2,128)(2,1)}), bf16[8,2,18176]{2,1,0:T(2,128)(2,1)S(1)}, u32[]{:S(2)}, u32[]{:S(2)}) %all-to-all-start) | async-done | bytes 581664 | tf_op jit(solution)/shard_map/all_to_all | solution.py:118
  41.2 0.7 reshape.217
  41.9 0.8 reshape.218
  43.2 1.9 %collective-permute-start = (bf16[550,528]{0,1:T(8,128)(2,1)S(1)}, bf16[550,528]{0,1:T(8,128)(2,1)S(1)}, u32[]{:S(2)}, u32[]{:S(2)}) collective-permute-start(bf16[550,528]{0,1:T(8,128)(2,1)S(1)} %copy.120), channel_id=1, source_target_pairs={{0,8},{8,16},{16,24},{24,32},{32,40},{40,48},{48,56},{56,64},{64,7... | collective-permute-start | bytes 1742408 | tf_op jit(solution)/shard_map/ppermute | solution.py:135
  45.8 5.9 %collective-permute-start.1 = (bf16[128,264]{0,1:T(8,128)(2,1)S(1)}, bf16[128,264]{0,1:T(8,128)(2,1)S(1)}, u32[]{:S(2)}, u32[]{:S(2)}) collective-permute-start(bf16[128,264]{0,1:T(8,128)(2,1)S(1)} %bitcast.95), channel_id=1, source_target_pairs={{8,0},{16,8},{24,16},{32,24},{40,32},{48,40},{56,48},{64,56},{72,6... | collective-permute-start | bytes 202760 | tf_op jit(solution)/shard_map/ppermute | solution.py:10
  52.3 1.2 %collective-permute-done.1 = bf16[128,264]{0,1:T(8,128)(2,1)S(1)} collective-permute-done((bf16[128,264]{0,1:T(8,128)(2,1)S(1)}, bf16[128,264]{0,1:T(8,128)(2,1)S(1)}, u32[]{:S(2)}, u32[]{:S(2)}) %collective-permute-start.1) | collective-permute-done | bytes 67616 | tf_op jit(solution)/shard_map/ppermute | solution.py:10
  53.6 3.8 %collective-permute-done = bf16[550,528]{0,1:T(8,128)(2,1)S(1)} collective-permute-done((bf16[550,528]{0,1:T(8,128)(2,1)S(1)}, bf16[550,528]{0,1:T(8,128)(2,1)S(1)}, u32[]{:S(2)}, u32[]{:S(2)}) %collective-permute-start) | collective-permute-done | bytes 580832 | tf_op jit(solution)/shard_map/ppermute | solution.py:135
  58.0 0.8 reshape.221
  58.8 0.5 reshape.222
  61.0 0.4 copy.151
  61.5 0.4 pad.20.clone
  61.9 0.5 fusion.3
  62.6 0.6 copy-done.5
  63.1 0.9 %fusion.15 = bf16[2,16,33,128]{3,1,2,0:T(8,128)(2,1)S(1)} fusion(bf16[128,4,2,8,35]{0,2,4,3,1:T(2,128)(2,1)S(1)} %fusion.3, bf16[128,3,3,128]{3,2,1,0:T(4,128)(2,1)S(1)} %reshape.224, f32[128]{0:T(128)S(1)} %add.175, pred[16,33]{0,1:T(8,128)(4,1)S(1)} %copy-done.5), kind=kOutput, calls=%fused_computation.20 | convolution fusion | flops 312913920 | bytes 1139728 | tf_op jit(solution)/shard_map/conv_general_dilated | solution.py:61
  68.2 13.3 %all_to_all.10 = bf16[8,2,6144]{2,1,0:T(2,128)(2,1)S(1)} all-to-all(bf16[8,2,6144]{2,1,0:T(2,128)(2,1)S(1)} %copy.141), channel_id=1, replica_groups=mesh['space'=64,'chan'=8] {'chan'}, dimensions={0} | all-to-all | bytes 393216 | tf_op jit(solution)/shard_map/all_to_all | solution.py:178
  81.6 0.7 broadcast_in_dim_reshape.8
  82.3 0.7 broadcast_in_dim_reshape.9
  (118 shorter events, 10.9 us)
Async XLA Ops:
  0.6 4.1 %copy-start.2 = (bf16[16,3,3,128]{3,0,2,1:T(8,128)(2,1)S(1)}, bf16[16,3,3,128]{3,0,2,1:T(8,128)(2,1)}, u32[]{:S(2)}) copy-start(bf16[16,3,3,128]{3,0,2,1:T(8,128)(2,1)} %param.10) | copy-start | bytes 110596
  0.6 4.2 %copy-start.1 = (bf16[32,3,3,128]{3,0,2,1:T(8,128)(2,1)S(1)}, bf16[32,3,3,128]{3,0,2,1:T(8,128)(2,1)}, u32[]{:S(2)}) copy-start(bf16[32,3,3,128]{3,0,2,1:T(8,128)(2,1)} %param.12) | copy-start | bytes 221188
  8.0 12.0 %copy-start.4 = (s32[1,2048]{1,0:T(1,128)S(1)}, s32[1,2048]{1,0:T(1,128)}, u32[]{:S(2)}) copy-start(s32[1,2048]{1,0:T(1,128)} %param.9) | copy-start | bytes 24580
  8.0 12.2 %copy-start.3 = (s32[1,2048]{1,0:T(1,128)S(1)}, s32[1,2048]{1,0:T(1,128)}, u32[]{:S(2)}) copy-start(s32[1,2048]{1,0:T(1,128)} %param.8) | copy-start | bytes 24580
  8.0 32.8 %all-to-all-start = ((bf16[8,2,18176]{2,1,0:T(2,128)(2,1)}), bf16[8,2,18176]{2,1,0:T(2,128)(2,1)S(1)}, u32[]{:S(2)}, u32[]{:S(2)}) async-start(bf16[8,2,18176]{2,1,0:T(2,128)(2,1)} %reshape.214), calls=%async_computation | async-start | bytes 1163264 | tf_op jit(solution)/shard_map/all_to_all | solution.py:118
  43.2 14.2 %collective-permute-start = (bf16[550,528]{0,1:T(8,128)(2,1)S(1)}, bf16[550,528]{0,1:T(8,128)(2,1)S(1)}, u32[]{:S(2)}, u32[]{:S(2)}) collective-permute-start(bf16[550,528]{0,1:T(8,128)(2,1)S(1)} %copy.120), channel_id=1, source_target_pairs={{0,8},{8,16},{16,24},{24,32},{32,40},{40,48},{48,56},{56,64},{64,7... | collective-permute-start | bytes 1742408 | tf_op jit(solution)/shard_map/ppermute | solution.py:135
  45.8 7.7 %collective-permute-start.1 = (bf16[128,264]{0,1:T(8,128)(2,1)S(1)}, bf16[128,264]{0,1:T(8,128)(2,1)S(1)}, u32[]{:S(2)}, u32[]{:S(2)}) collective-permute-start(bf16[128,264]{0,1:T(8,128)(2,1)S(1)} %bitcast.95), channel_id=1, source_target_pairs={{8,0},{16,8},{24,16},{32,24},{40,32},{48,40},{56,48},{64,56},{72,6... | collective-permute-start | bytes 202760 | tf_op jit(solution)/shard_map/ppermute | solution.py:10
  62.4 0.7 copy-start.5
  64.7 0.7 copy-start
  65.3 0.9 %slice-start = ((bf16[128,2,260]{0,1,2:T(2,128)(2,1)}), bf16[128,2,258]{0,1,2:T(2,128)(2,1)S(1)}, s32[]{:S(2)}) async-start(bf16[128,2,260]{0,1,2:T(2,128)(2,1)} %copy-done), calls=%async_computation.2 | async-start | bytes 264192 | tf_op jit(solution)/shard_map/slice | solution.py:172
  66.6 0.7 copy-start.6

commit v13 on v10

--- a/solution.py
+++ b/solution.py
@@ -72,9 +72,9 @@
     cycle = padded.shape[-1]
     block = cycle // groups
     lead = padded.shape[:-1]
-    left = jnp.roll(padded, halo, axis=-1).reshape(lead + (groups, block))[..., :halo]
     mid = padded.reshape(lead + (groups, block))
-    right = jnp.roll(padded, -halo, axis=-1).reshape(lead + (groups, block))[..., block - halo :]
+    left = jnp.roll(mid[..., block - halo :], 1, axis=-2)
+    right = jnp.roll(mid[..., :halo], -1, axis=-2)
     wins = jnp.concatenate([left, mid, right], axis=-1)
     return jnp.moveaxis(wins, -2, 0)
 

time: 81.5 us -> 80.4 us (0.987)
    slice x4 -> x2, local copies, waits for them, and re-layouts: 2.12 us -> 0.18 us  [column_windows(): left = jnp.roll(mid[..., block - halo:], 1, axis=-2)]
    unnamed x24 -> x18, local copies, waits for them, and re-layouts: 2.48 us -> 4.04 us
    another operation x3 -> x2, other arithmetic: 2.04 us -> 2.03 us  [per_device(): jnp.stack([jnp.concatenate([above[:, None], inner, below[:, None]], axis=...]
where the time goes in v13:
time: 80.4 us; the launch traced here: 79.9 us
  starting transfers between devices  23.2 us (29%)
  waiting for transfers between devices  21.1 us (26%)
  local copies, waits for them, and re-layouts  13.9 us (17%)
  blocking collectives  13.3 us (17%)
  other arithmetic  5.83 us (7%)
  matrix products  1.3 us (2%)
  between operations  1.27 us (2%)
    all_to_all x1, waiting for transfers between devices, per_device(): lax.all_to_all(pad_to(sends, 256).reshape(groups, 2, -1), 'chan', 0, 0, t...  16.4 us
    all_to_all x1, blocking collectives, per_device(): lax.all_to_all(jnp.concatenate([hidden_part, coarse_part], 1).reshape(gro...  13.3 us
    ppermute x2, starting transfers between devices, shifted(): return lax.ppermute(array, axis, pairs)  11 us
    all_to_all x1, starting transfers between devices, per_device(): lax.all_to_all(pad_to(sends, 256).reshape(groups, 2, -1), 'chan', 0, 0, t...  10.2 us
    ppermute x2, waiting for transfers between devices, shifted(): return lax.ppermute(array, axis, pairs)  4.69 us
    unnamed x18, local copies, waits for them, and re-layouts  4.04 us
    ppermute x1, starting transfers between devices, per_device(): lax.ppermute(own_half, 'space', [(i, i ^ 1) for i in range(spaces)])  2.1 us
    another operation x2, other arithmetic, per_device(): jnp.stack([jnp.concatenate([above[:, None], inner, below[:, None]], axis=...  2.03 us
  transfers between devices with their start and end apart: 4, of which 2 were waited for; matrix products, arithmetic and copies ran while one was open for 8% of the time, Pallas kernels for 0%

profile of v13, /device:TPU:192, one launch (start us, length us, event | category | flops | bytes accessed | tf_op | source)
XLA Modules:
  0.0 79.9 jit_solution(10063485122285315833)
XLA Ops:
  0.6 1.0 %reshape.224 = bf16[16,2,8,256]{3,2,1,0:T(8,128)(2,1)S(1)} reshape(bf16[1,16,2,2048]{3,2,1,0:T(2,128)(2,1)} %param.7) | data formatting | bytes 262144 | tf_op jit(solution)/shard_map/reshape;squeeze | solution.py:75
  1.8 0.8 reduce-precision_convert_fusion.1
  2.9 0.8 copy.276
  3.7 0.9 %copy.277 = bf16[32,3,3,128]{3,2,1,0:T(4,128)(2,1)S(1)} copy(bf16[32,3,3,128]{3,0,2,1:T(8,128)(2,1)} %param.12) | data formatting | bytes 147456 | tf_op args[5]
  5.9 1.0 %reshape.190 = bf16[8,2,18176]{2,1,0:T(2,128)(2,1)} reshape(bf16[8,36352]{1,0:T(8,128)(2,1)S(1)} %pad.13) | data formatting | bytes 1163264 | tf_op jit(solution)/shard_map/reshape | solution.py:119
  6.8 10.2 %all-to-all-start = ((bf16[8,2,18176]{2,1,0:T(2,128)(2,1)}), bf16[8,2,18176]{2,1,0:T(2,128)(2,1)S(1)}, u32[]{:S(2)}, u32[]{:S(2)}) async-start(bf16[8,2,18176]{2,1,0:T(2,128)(2,1)} %reshape.190), calls=%async_computation | async-start | bytes 1163264 | tf_op jit(solution)/shard_map/all_to_all | solution.py:118
  17.4 16.4 %all-to-all-done = bf16[8,2,18176]{2,1,0:T(2,128)(2,1)S(1)} async-done(((bf16[8,2,18176]{2,1,0:T(2,128)(2,1)}), bf16[8,2,18176]{2,1,0:T(2,128)(2,1)S(1)}, u32[]{:S(2)}, u32[]{:S(2)}) %all-to-all-start) | async-done | bytes 581664 | tf_op jit(solution)/shard_map/all_to_all | solution.py:118
  33.9 0.4 reshape.192
  34.8 9.0 %collective-permute-start.1 = (bf16[128,264]{0,1:T(8,128)(2,1)S(1)}, bf16[128,264]{0,1:T(8,128)(2,1)S(1)}, u32[]{:S(2)}, u32[]{:S(2)}) collective-permute-start(bf16[128,264]{0,1:T(8,128)(2,1)S(1)} %bitcast.90), channel_id=1, source_target_pairs={{8,0},{16,8},{24,16},{32,24},{40,32},{48,40},{56,48},{64,56},{72,6... | collective-permute-start | bytes 202760 | tf_op jit(solution)/shard_map/ppermute | solution.py:10
  44.1 1.9 %collective-permute-start = (bf16[129,2,264]{2,1,0:T(2,128)(2,1)S(1)}, bf16[129,2,264]{2,1,0:T(2,128)(2,1)S(1)}, u32[]{:S(2)}, u32[]{:S(2)}) collective-permute-start(bf16[129,2,264]{2,1,0:T(2,128)(2,1)S(1)} %pad_maximum_fusion.1), channel_id=1, source_target_pairs={{0,8},{8,16},{16,24},{24,32},{32,40},{40,48},{48,56},{56,64},{64,7... | collective-permute-start | bytes 408680 | tf_op jit(solution)/shard_map/ppermute | solution.py:10
  46.0 2.1 %collective-permute-start.2 = (bf16[8,27776]{1,0:T(8,128)(2,1)S(1)}, bf16[8,27776]{1,0:T(8,128)(2,1)S(1)}, u32[]{:S(2)}, u32[]{:S(2)}) collective-permute-start(bf16[8,27776]{1,0:T(8,128)(2,1)S(1)} %slice.202), channel_id=1, source_target_pairs={{0,8},{8,0},{16,24},{24,16},{32,40},{40,32},{48,56},{56,48},{64,72... | collective-permute-start | bytes 1333256 | tf_op jit(solution)/shard_map/ppermute | solution.py:125
  48.5 4.7 %collective-permute-done = bf16[129,2,264]{2,1,0:T(2,128)(2,1)S(1)} collective-permute-done((bf16[129,2,264]{2,1,0:T(2,128)(2,1)S(1)}, bf16[129,2,264]{2,1,0:T(2,128)(2,1)S(1)}, u32[]{:S(2)}, u32[]{:S(2)}) %collective-permute-start) | collective-permute-done | bytes 136256 | tf_op jit(solution)/shard_map/ppermute | solution.py:10
  54.8 1.4 %maximum_bitcast_fusion.1 = (bf16[1,128,4,262]{3,2,1,0:T(4,128)(2,1)S(1)}, bf16[1,128,4,262]{3,2,1,0:T(4,128)(2,1)S(1)}) fusion(bf16[128,1,262]{2,1,0:T(2,128)(2,1)S(1)} %copy.282, bf16[128,2,262]{2,1,0:T(2,128)(2,1)S(1)} %slice.191, bf16[128,1,262]{2,1,0:T(2,128)(2,1)S(1)} %copy.281, bf16[128,1,262]{2,1,0:T(2,128)(2,1)S(1)} %copy.283, ...), kind=kLoop, calls=%fused_computation.23 | loop fusion | flops 1609728 | bytes 1006080 | tf_op jit(solution)/shard_map/stack | solution.py:150
  56.2 0.6 maximum_bitcast_fusion
  56.8 1.0 %copy.309 = bf16[128,4,2,262]{0,2,3,1:T(2,128)(2,1)S(1)} copy(bf16[128,4,2,262]{3,1,0,2:T(4,128)(2,1)S(1)} %maximum_bitcast_fusion) | data formatting | bytes 1073152
  57.8 0.4 pad.15.clone
  58.3 0.5 fusion.3
  59.7 0.4 copy-done.3
  60.1 0.9 %fusion.15 = bf16[2,16,33,128]{3,1,2,0:T(8,128)(2,1)S(1)} fusion(bf16[128,4,2,8,35]{0,2,4,3,1:T(2,128)(2,1)S(1)} %fusion.3, bf16[128,3,3,128]{3,2,1,0:T(4,128)(2,1)S(1)} %reshape.194, f32[128]{0:T(128)S(1)} %add.173, pred[16,33]{0,1:T(8,128)(4,1)S(1)} %copy-done.3), kind=kOutput, calls=%fused_computation.20 | convolution fusion | flops 312913920 | bytes 1139728 | tf_op jit(solution)/shard_map/conv_general_dilated | solution.py:61
  63.9 0.4 copy-done.4
  64.3 0.4 fusion.37
  65.1 13.3 %all_to_all.10 = bf16[8,2,6144]{2,1,0:T(2,128)(2,1)S(1)} all-to-all(bf16[8,2,6144]{2,1,0:T(2,128)(2,1)S(1)} %copy.302), channel_id=1, replica_groups=mesh['space'=64,'chan'=8] {'chan'}, dimensions={0} | all-to-all | bytes 393216 | tf_op jit(solution)/shard_map/all_to_all | solution.py:170
  78.5 0.7 broadcast_in_dim_reshape.8
  79.2 0.7 broadcast_in_dim_reshape.9
  (97 shorter events, 8.8 us)
Async XLA Ops:
  6.8 10.2 %copy-start.2 = (s32[1,2048]{1,0:T(1,128)S(1)}, s32[1,2048]{1,0:T(1,128)}, u32[]{:S(2)}) copy-start(s32[1,2048]{1,0:T(1,128)} %param.9) | copy-start | bytes 24580
  6.8 10.4 %copy-start.1 = (s32[1,2048]{1,0:T(1,128)S(1)}, s32[1,2048]{1,0:T(1,128)}, u32[]{:S(2)}) copy-start(s32[1,2048]{1,0:T(1,128)} %param.8) | copy-start | bytes 24580
  6.8 26.9 %all-to-all-start = ((bf16[8,2,18176]{2,1,0:T(2,128)(2,1)}), bf16[8,2,18176]{2,1,0:T(2,128)(2,1)S(1)}, u32[]{:S(2)}, u32[]{:S(2)}) async-start(bf16[8,2,18176]{2,1,0:T(2,128)(2,1)} %reshape.190), calls=%async_computation | async-start | bytes 1163264 | tf_op jit(solution)/shard_map/all_to_all | solution.py:118
  34.8 13.4 %collective-permute-start.1 = (bf16[128,264]{0,1:T(8,128)(2,1)S(1)}, bf16[128,264]{0,1:T(8,128)(2,1)S(1)}, u32[]{:S(2)}, u32[]{:S(2)}) collective-permute-start(bf16[128,264]{0,1:T(8,128)(2,1)S(1)} %bitcast.90), channel_id=1, source_target_pairs={{8,0},{16,8},{24,16},{32,24},{40,32},{48,40},{56,48},{64,56},{72,6... | collective-permute-start | bytes 202760 | tf_op jit(solution)/shard_map/ppermute | solution.py:10
  44.1 9.1 %collective-permute-start = (bf16[129,2,264]{2,1,0:T(2,128)(2,1)S(1)}, bf16[129,2,264]{2,1,0:T(2,128)(2,1)S(1)}, u32[]{:S(2)}, u32[]{:S(2)}) collective-permute-start(bf16[129,2,264]{2,1,0:T(2,128)(2,1)S(1)} %pad_maximum_fusion.1), channel_id=1, source_target_pairs={{0,8},{8,16},{16,24},{24,32},{32,40},{40,48},{48,56},{56,64},{64,7... | collective-permute-start | bytes 408680 | tf_op jit(solution)/shard_map/ppermute | solution.py:10
  46.0 12.7 %collective-permute-start.2 = (bf16[8,27776]{1,0:T(8,128)(2,1)S(1)}, bf16[8,27776]{1,0:T(8,128)(2,1)S(1)}, u32[]{:S(2)}, u32[]{:S(2)}) collective-permute-start(bf16[8,27776]{1,0:T(8,128)(2,1)S(1)} %slice.202), channel_id=1, source_target_pairs={{0,8},{8,0},{16,24},{24,16},{32,40},{40,32},{48,56},{56,48},{64,72... | collective-permute-start | bytes 1333256 | tf_op jit(solution)/shard_map/ppermute | solution.py:125
  59.4 0.7 copy-start.3
  61.5 0.7 copy-start
  62.3 0.9 %slice-start = ((bf16[128,2,260]{0,1,2:T(2,128)(2,1)}), bf16[128,2,258]{0,1,2:T(2,128)(2,1)S(1)}, s32[]{:S(2)}) async-start(bf16[128,2,260]{0,1,2:T(2,128)(2,1)} %copy-done), calls=%async_computation.2 | async-start | bytes 264192 | tf_op jit(solution)/shard_map/slice | solution.py:164
  63.6 0.7 copy-start.4

commit v14 on v13

--- a/solution.py
+++ b/solution.py
@@ -63,7 +63,7 @@
         w,
         window_strides=stride,
         padding="VALID",
-        dimension_numbers=("NCHW", "OHWI", "NCHW"),
+        dimension_numbers=("NCHW", "HWOI", "NCHW"),
         preferred_element_type=jnp.float32,
     )
 
@@ -102,12 +102,14 @@
     wins = column_windows(x, groups, halo + 1).reshape(groups, -1)
     feat_len = wins.shape[1]
 
-    flat_w = jnp.concatenate(
-        [first_weight.reshape(n1, -1), second_weight.reshape(n2, -1)], axis=0
-    )
-    taps = flat_w.shape[1]
+    w1_len = first_weight.size
+    w_total = w1_len + second_weight.size
     packed_w = jnp.concatenate(
-        [flat_w.reshape(-1), split3(jnp.concatenate([first_bias, second_bias])).reshape(-1)]
+        [
+            jnp.transpose(first_weight, (1, 2, 0, 3)).reshape(-1),
+            jnp.transpose(second_weight, (1, 2, 0, 3)).reshape(-1),
+            split3(jnp.concatenate([first_bias, second_bias])).reshape(-1),
+        ]
     )
     w_len = packed_w.shape[0]
     half = -(-w_len // 256) * 128
@@ -128,10 +130,13 @@
         jnp.concatenate([other_half, own_half], 1),
         jnp.concatenate([own_half, other_half], 1),
     )
-    w_all = every[:, : (n1 + n2) * taps].reshape(groups, n1 + n2, taps)
-    b_all = every[:, (n1 + n2) * taps : w_len].reshape(groups, n1 + n2, 3)
-    w1 = w_all[:, :n1].reshape((-1,) + first_weight.shape[1:])
-    w2 = w_all[:, n1:].reshape((-1,) + second_weight.shape[1:])
+    k1 = first_weight.shape[1:3]
+    k2 = second_weight.shape[1:3]
+    w1 = every[:, :w1_len].reshape((groups,) + k1 + (n1, first_weight.shape[3]))
+    w1 = jnp.moveaxis(w1, 0, 2).reshape(k1 + (groups * n1, first_weight.shape[3]))
+    w2 = every[:, w1_len:w_total].reshape((groups,) + k2 + (n2, second_weight.shape[3]))
+    w2 = jnp.moveaxis(w2, 0, 2).reshape(k2 + (groups * n2, second_weight.shape[3]))
+    b_all = every[:, w_total:w_len].reshape(groups, n1 + n2, 3)
     b1 = join3(b_all[:, :n1]).reshape(-1)
     b2 = join3(b_all[:, n1:]).reshape(-1)
 

time: 80.4 us -> 77.5 us (0.964)
  local copies, waits for them, and re-layouts: 13.9 us -> 11 us
    unnamed x18 -> x20, local copies, waits for them, and re-layouts: 4.04 us -> 1.73 us
where the time goes in v14:
time: 77.5 us; the launch traced here: 77.1 us
  starting transfers between devices  23.2 us (30%)
  waiting for transfers between devices  21.1 us (27%)
  blocking collectives  13.3 us (17%)
  local copies, waits for them, and re-layouts  11 us (14%)
  other arithmetic  5.94 us (8%)
  matrix products  1.31 us (2%)
  between operations  1.27 us (2%)
    all_to_all x1, waiting for transfers between devices, per_device(): lax.all_to_all(pad_to(sends, 256).reshape(groups, 2, -1), 'chan', 0, 0, t...  16.4 us
    all_to_all x1, blocking collectives, per_device(): lax.all_to_all(jnp.concatenate([hidden_part, coarse_part], 1).reshape(gro...  13.3 us
    ppermute x2, starting transfers between devices, shifted(): return lax.ppermute(array, axis, pairs)  11 us
    all_to_all x1, starting transfers between devices, per_device(): lax.all_to_all(pad_to(sends, 256).reshape(groups, 2, -1), 'chan', 0, 0, t...  10.2 us
    ppermute x2, waiting for transfers between devices, shifted(): return lax.ppermute(array, axis, pairs)  4.69 us
    ppermute x1, starting transfers between devices, per_device(): lax.ppermute(own_half, 'space', [(i, i ^ 1) for i in range(spaces)])  2.1 us
    another operation x2, other arithmetic, per_device(): jnp.stack([jnp.concatenate([above[:, None], inner, below[:, None]], axis=...  2.03 us
    unnamed x20, local copies, waits for them, and re-layouts  1.73 us
  transfers between devices with their start and end apart: 4, of which 2 were waited for; matrix products, arithmetic and copies ran while one was open for 8% of the time, Pallas kernels for 0%

profile of v14, /device:TPU:192, one launch (start us, length us, event | category | flops | bytes accessed | tf_op | source)
XLA Modules:
  0.0 77.1 jit_solution(10843834886481716623)
XLA Ops:
  0.7 1.0 %reshape.224 = bf16[16,2,8,256]{3,2,1,0:T(8,128)(2,1)S(1)} reshape(bf16[1,16,2,2048]{3,2,1,0:T(2,128)(2,1)} %param.7) | data formatting | bytes 262144 | tf_op jit(solution)/shard_map/reshape;squeeze | solution.py:75
  1.9 0.8 reduce-precision_convert_fusion.1
  4.0 1.0 %reshape.189 = bf16[8,2,18176]{2,1,0:T(2,128)(2,1)} reshape(bf16[8,36352]{1,0:T(8,128)(2,1)S(1)} %pad.13) | data formatting | bytes 1163264 | tf_op jit(solution)/shard_map/reshape | solution.py:121
  5.0 10.2 %all-to-all-start = ((bf16[8,2,18176]{2,1,0:T(2,128)(2,1)}), bf16[8,2,18176]{2,1,0:T(2,128)(2,1)S(1)}, u32[]{:S(2)}, u32[]{:S(2)}) async-start(bf16[8,2,18176]{2,1,0:T(2,128)(2,1)} %reshape.189), calls=%async_computation | async-start | bytes 1163264 | tf_op jit(solution)/shard_map/all_to_all | solution.py:120
  15.6 16.4 %all-to-all-done = bf16[8,2,18176]{2,1,0:T(2,128)(2,1)S(1)} async-done(((bf16[8,2,18176]{2,1,0:T(2,128)(2,1)}), bf16[8,2,18176]{2,1,0:T(2,128)(2,1)S(1)}, u32[]{:S(2)}, u32[]{:S(2)}) %all-to-all-start) | async-done | bytes 581664 | tf_op jit(solution)/shard_map/all_to_all | solution.py:120
  32.1 0.4 reshape.191
  32.5 0.3 slice.187
  32.9 9.0 %collective-permute-start.1 = (bf16[128,264]{0,1:T(8,128)(2,1)S(1)}, bf16[128,264]{0,1:T(8,128)(2,1)S(1)}, u32[]{:S(2)}, u32[]{:S(2)}) collective-permute-start(bf16[128,264]{0,1:T(8,128)(2,1)S(1)} %bitcast.113), channel_id=1, source_target_pairs={{8,0},{16,8},{24,16},{32,24},{40,32},{48,40},{56,48},{64,56},{72,6... | collective-permute-start | bytes 202760 | tf_op jit(solution)/shard_map/ppermute | solution.py:10
  42.0 0.3 pad_maximum_fusion.1
  42.3 1.9 %collective-permute-start = (bf16[129,2,264]{2,1,0:T(2,128)(2,1)S(1)}, bf16[129,2,264]{2,1,0:T(2,128)(2,1)S(1)}, u32[]{:S(2)}, u32[]{:S(2)}) collective-permute-start(bf16[129,2,264]{2,1,0:T(2,128)(2,1)S(1)} %pad_maximum_fusion.1), channel_id=1, source_target_pairs={{0,8},{8,16},{16,24},{24,32},{32,40},{40,48},{48,56},{56,64},{64,7... | collective-permute-start | bytes 408680 | tf_op jit(solution)/shard_map/ppermute | solution.py:10
  44.2 2.1 %collective-permute-start.2 = (bf16[8,27776]{1,0:T(8,128)(2,1)S(1)}, bf16[8,27776]{1,0:T(8,128)(2,1)S(1)}, u32[]{:S(2)}, u32[]{:S(2)}) collective-permute-start(bf16[8,27776]{1,0:T(8,128)(2,1)S(1)} %slice.198), channel_id=1, source_target_pairs={{0,8},{8,0},{16,24},{24,16},{32,40},{40,32},{48,56},{56,48},{64,72... | collective-permute-start | bytes 1333256 | tf_op jit(solution)/shard_map/ppermute | solution.py:127
  46.7 4.7 %collective-permute-done = bf16[129,2,264]{2,1,0:T(2,128)(2,1)S(1)} collective-permute-done((bf16[129,2,264]{2,1,0:T(2,128)(2,1)S(1)}, bf16[129,2,264]{2,1,0:T(2,128)(2,1)S(1)}, u32[]{:S(2)}, u32[]{:S(2)}) %collective-permute-start) | collective-permute-done | bytes 136256 | tf_op jit(solution)/shard_map/ppermute | solution.py:10
  52.7 0.3 slice.192
  53.0 1.4 %maximum_bitcast_fusion.1 = (bf16[1,128,4,262]{3,2,1,0:T(4,128)(2,1)S(1)}, bf16[1,128,4,262]{3,2,1,0:T(4,128)(2,1)S(1)}) fusion(bf16[128,1,262]{2,1,0:T(2,128)(2,1)S(1)} %copy.248, bf16[128,2,262]{2,1,0:T(2,128)(2,1)S(1)} %slice.187, bf16[128,1,262]{2,1,0:T(2,128)(2,1)S(1)} %copy.247, bf16[128,1,262]{2,1,0:T(2,128)(2,1)S(1)} %copy.249, ...), kind=kLoop, calls=%fused_computation.23 | loop fusion | flops 1609728 | bytes 1006080 | tf_op jit(solution)/shard_map/stack | solution.py:155
  54.4 0.6 maximum_bitcast_fusion
  55.0 1.0 %copy.271 = bf16[128,4,2,262]{0,2,3,1:T(2,128)(2,1)S(1)} copy(bf16[128,4,2,262]{3,1,0,2:T(4,128)(2,1)S(1)} %maximum_bitcast_fusion) | data formatting | bytes 1073152
  56.0 0.4 pad.15.clone
  56.4 0.5 fusion.2
  57.9 0.9 %fusion.14 = bf16[2,16,33,128]{3,1,2,0:T(8,128)(2,1)S(1)} fusion(bf16[3,3,128,128]{3,2,1,0:T(8,128)(2,1)S(1)} %bitcast.123, bf16[128,4,2,8,35]{0,2,4,3,1:T(2,128)(2,1)S(1)} %fusion.2, f32[128]{0:T(128)S(1)} %add.173, pred[16,33]{0,1:T(8,128)(4,1)S(1)} %copy-done.5), kind=kOutput, calls=%fused_computation.20 | convolution fusion | flops 312913920 | bytes 1139728 | tf_op jit(solution)/shard_map/conv_general_dilated | solution.py:61
  60.7 0.3 copy-done.6
  61.0 0.4 fusion.33
  62.4 13.3 %all_to_all.10 = bf16[8,2,6144]{2,1,0:T(2,128)(2,1)S(1)} all-to-all(bf16[8,2,6144]{2,1,0:T(2,128)(2,1)S(1)} %copy.266), channel_id=1, replica_groups=mesh['space'=64,'chan'=8] {'chan'}, dimensions={0} | all-to-all | bytes 393216 | tf_op jit(solution)/shard_map/all_to_all | solution.py:175
  75.7 0.7 broadcast_in_dim_reshape.8
  76.4 0.7 broadcast_in_dim_reshape.9
  (92 shorter events, 7.3 us)
Async XLA Ops:
  0.6 2.9 %copy-start.1 = (bf16[32,3,3,128]{3,0,2,1:T(8,128)(2,1)S(1)}, bf16[32,3,3,128]{3,0,2,1:T(8,128)(2,1)}, u32[]{:S(2)}) copy-start(bf16[32,3,3,128]{3,0,2,1:T(8,128)(2,1)} %param.12) | copy-start | bytes 221188
  0.6 2.9 %copy-start.2 = (bf16[16,3,3,128]{3,0,2,1:T(8,128)(2,1)S(1)}, bf16[16,3,3,128]{3,0,2,1:T(8,128)(2,1)}, u32[]{:S(2)}) copy-start(bf16[16,3,3,128]{3,0,2,1:T(8,128)(2,1)} %param.10) | copy-start | bytes 110596
  5.0 10.2 %copy-start.4 = (s32[1,2048]{1,0:T(1,128)S(1)}, s32[1,2048]{1,0:T(1,128)}, u32[]{:S(2)}) copy-start(s32[1,2048]{1,0:T(1,128)} %param.9) | copy-start | bytes 24580
  5.0 10.4 %copy-start.3 = (s32[1,2048]{1,0:T(1,128)S(1)}, s32[1,2048]{1,0:T(1,128)}, u32[]{:S(2)}) copy-start(s32[1,2048]{1,0:T(1,128)} %param.8) | copy-start | bytes 24580
  5.0 26.9 %all-to-all-start = ((bf16[8,2,18176]{2,1,0:T(2,128)(2,1)}), bf16[8,2,18176]{2,1,0:T(2,128)(2,1)S(1)}, u32[]{:S(2)}, u32[]{:S(2)}) async-start(bf16[8,2,18176]{2,1,0:T(2,128)(2,1)} %reshape.189), calls=%async_computation | async-start | bytes 1163264 | tf_op jit(solution)/shard_map/all_to_all | solution.py:120
  32.9 13.4 %collective-permute-start.1 = (bf16[128,264]{0,1:T(8,128)(2,1)S(1)}, bf16[128,264]{0,1:T(8,128)(2,1)S(1)}, u32[]{:S(2)}, u32[]{:S(2)}) collective-permute-start(bf16[128,264]{0,1:T(8,128)(2,1)S(1)} %bitcast.113), channel_id=1, source_target_pairs={{8,0},{16,8},{24,16},{32,24},{40,32},{48,40},{56,48},{64,56},{72,6... | collective-permute-start | bytes 202760 | tf_op jit(solution)/shard_map/ppermute | solution.py:10
  42.3 9.1 %collective-permute-start = (bf16[129,2,264]{2,1,0:T(2,128)(2,1)S(1)}, bf16[129,2,264]{2,1,0:T(2,128)(2,1)S(1)}, u32[]{:S(2)}, u32[]{:S(2)}) collective-permute-start(bf16[129,2,264]{2,1,0:T(2,128)(2,1)S(1)} %pad_maximum_fusion.1), channel_id=1, source_target_pairs={{0,8},{8,16},{16,24},{24,32},{32,40},{40,48},{48,56},{56,64},{64,7... | collective-permute-start | bytes 408680 | tf_op jit(solution)/shard_map/ppermute | solution.py:10
  44.2 12.7 %collective-permute-start.2 = (bf16[8,27776]{1,0:T(8,128)(2,1)S(1)}, bf16[8,27776]{1,0:T(8,128)(2,1)S(1)}, u32[]{:S(2)}, u32[]{:S(2)}) collective-permute-start(bf16[8,27776]{1,0:T(8,128)(2,1)S(1)} %slice.198), channel_id=1, source_target_pairs={{0,8},{8,0},{16,24},{24,16},{32,40},{40,32},{48,56},{56,48},{64,72... | collective-permute-start | bytes 1333256 | tf_op jit(solution)/shard_map/ppermute | solution.py:127
  57.2 0.7 copy-start.5
  59.4 0.8 %copy-start = (bf16[128,2,260]{0,1,2:T(2,128)(2,1)}, bf16[128,2,260]{0,1,2:T(2,128)(2,1)S(1)}, u32[]{:S(2)}) copy-start(bf16[128,2,260]{0,1,2:T(2,128)(2,1)S(1)} %slice_bitcast_fusion.3) | copy-start | bytes 399364
  60.3 0.7 copy-start.6
  61.0 0.9 %slice-start = ((bf16[128,2,260]{0,1,2:T(2,128)(2,1)}), bf16[128,2,256]{0,1,2:T(2,128)(2,1)S(1)}, s32[]{:S(2)}) async-start(bf16[128,2,260]{0,1,2:T(2,128)(2,1)} %copy-done), calls=%async_computation.2 | async-start | bytes 262144 | tf_op jit(solution)/shard_map/slice | solution.py:173

commit v15 on v11

--- a/solution.py
+++ b/solution.py
@@ -63,7 +63,7 @@
         w,
         window_strides=stride,
         padding="VALID",
-        dimension_numbers=("NCHW", "OHWI", "NCHW"),
+        dimension_numbers=("NCHW", "HWOI", "NCHW"),
         preferred_element_type=jnp.float32,
     )
 
@@ -72,9 +72,9 @@
     cycle = padded.shape[-1]
     block = cycle // groups
     lead = padded.shape[:-1]
-    left = jnp.roll(padded, halo, axis=-1).reshape(lead + (groups, block))[..., :halo]
     mid = padded.reshape(lead + (groups, block))
-    right = jnp.roll(padded, -halo, axis=-1).reshape(lead + (groups, block))[..., block - halo :]
+    left = jnp.roll(mid[..., block - halo :], 1, axis=-2)
+    right = jnp.roll(mid[..., :halo], -1, axis=-2)
     wins = jnp.concatenate([left, mid, right], axis=-1)
     return jnp.moveaxis(wins, -2, 0)
 
@@ -116,12 +116,14 @@
     wins = column_windows(x, groups, halo + 1).reshape(groups, -1)
     feat_len = wins.shape[1]
 
-    flat_w = jnp.concatenate(
-        [first_weight.reshape(n1, -1), second_weight.reshape(n2, -1)], axis=0
-    )
-    taps = flat_w.shape[1]
+    w1_len = first_weight.size
+    w_total = w1_len + second_weight.size
     packed_w = jnp.concatenate(
-        [flat_w.reshape(-1), split3(jnp.concatenate([first_bias, second_bias])).reshape(-1)]
+        [
+            jnp.transpose(first_weight, (1, 2, 0, 3)).reshape(-1),
+            jnp.transpose(second_weight, (1, 2, 0, 3)).reshape(-1),
+            split3(jnp.concatenate([first_bias, second_bias])).reshape(-1),
+        ]
     )
     w_len = packed_w.shape[0]
     share = 4
@@ -137,10 +139,13 @@
     tile = got[:, :feat_len].reshape(groups * chans, rows, width + 2)
     pieces = gather_low_bits(got[:, feat_len : feat_len + quarter], share)
     every = jnp.moveaxis(pieces, 0, 1).reshape(groups, -1)
-    w_all = every[:, : (n1 + n2) * taps].reshape(groups, n1 + n2, taps)
-    b_all = every[:, (n1 + n2) * taps : w_len].reshape(groups, n1 + n2, 3)
-    w1 = w_all[:, :n1].reshape((-1,) + first_weight.shape[1:])
-    w2 = w_all[:, n1:].reshape((-1,) + second_weight.shape[1:])
+    k1 = first_weight.shape[1:3]
+    k2 = second_weight.shape[1:3]
+    w1 = every[:, :w1_len].reshape((groups,) + k1 + (n1, first_weight.shape[3]))
+    w1 = jnp.moveaxis(w1, 0, 2).reshape(k1 + (groups * n1, first_weight.shape[3]))
+    w2 = every[:, w1_len:w_total].reshape((groups,) + k2 + (n2, second_weight.shape[3]))
+    w2 = jnp.moveaxis(w2, 0, 2).reshape(k2 + (groups * n2, second_weight.shape[3]))
+    b_all = every[:, w_total:w_len].reshape(groups, n1 + n2, 3)
     b1 = join3(b_all[:, :n1]).reshape(-1)
     b2 = join3(b_all[:, n1:]).reshape(-1)
 

time: 80.8 us -> 76.7 us (0.949)
  local copies, waits for them, and re-layouts: 14.4 us -> 11 us
    slice x9 -> x4, local copies, waits for them, and re-layouts: 2.37 us -> 0.3 us  [the longest x2 0.18 us: column_windows(): left = jnp.roll(mid[..., block - halo:], 1, axis=-2)]
    unnamed x24 -> x20, local copies, waits for them, and re-layouts: 2.49 us -> 1.74 us
    another operation x3 -> x2, other arithmetic: 2.04 us -> 2.03 us  [per_device(): jnp.stack([jnp.concatenate([above[:, None], inner, below[:, None]], axis=...]
  transfers between devices with their start and end apart: 5 -> 5, of which waited for: 3 -> 3; matrix products, arithmetic and copies ran while one was open for 8% -> 9% of each run, Pallas kernels for 0% -> 0%
where the time goes in v15:
time: 76.7 us; the launch traced here: 76.3 us
  starting transfers between devices  22.8 us (30%)
  waiting for transfers between devices  20.2 us (26%)
  blocking collectives  13.5 us (18%)
  local copies, waits for them, and re-layouts  11 us (14%)
  other arithmetic  6.19 us (8%)
  matrix products  1.31 us (2%)
  between operations  1.31 us (2%)
    all_to_all x1, waiting for transfers between devices, per_device(): lax.all_to_all(pad_to(sends, 256).reshape(groups, 2, -1), 'chan', 0, 0, t...  13.9 us
    all_to_all x1, blocking collectives, per_device(): lax.all_to_all(jnp.concatenate([hidden_part, coarse_part], 1).reshape(gro...  13.5 us
    all_to_all x1, starting transfers between devices, per_device(): lax.all_to_all(pad_to(sends, 256).reshape(groups, 2, -1), 'chan', 0, 0, t...  10 us
    ppermute x2, starting transfers between devices, shifted(): return lax.ppermute(array, axis, pairs)  8.71 us
    ppermute x2, waiting for transfers between devices, shifted(): return lax.ppermute(array, axis, pairs)  4.87 us
    ppermute x2, starting transfers between devices, gather_low_bits(): recv = lax.ppermute(acc, 'space', [(i, i ^ bit) for i in range(count)])  4.02 us
    another operation x2, other arithmetic, per_device(): jnp.stack([jnp.concatenate([above[:, None], inner, below[:, None]], axis=...  2.03 us
    unnamed x20, local copies, waits for them, and re-layouts  1.74 us
  transfers between devices with their start and end apart: 5, of which 3 were waited for; matrix products, arithmetic and copies ran while one was open for 9% of the time, Pallas kernels for 0%

profile of v15, /device:TPU:192, one launch (start us, length us, event | category | flops | bytes accessed | tf_op | source)
XLA Modules:
  0.0 76.3 jit_solution(15140865290843660406)
XLA Ops:
  0.7 1.0 %reshape.314 = bf16[16,2,8,256]{3,2,1,0:T(8,128)(2,1)S(1)} reshape(bf16[1,16,2,2048]{3,2,1,0:T(2,128)(2,1)} %param.7) | data formatting | bytes 262144 | tf_op jit(solution)/shard_map/reshape;squeeze | solution.py:75
  1.9 0.8 reduce-precision_convert_fusion.1
  4.0 1.0 %reshape.278 = bf16[8,2,11264]{2,1,0:T(2,128)(2,1)} reshape(bf16[8,22528]{1,0:T(8,128)(2,1)S(1)} %pad.13) | data formatting | bytes 720896 | tf_op jit(solution)/shard_map/reshape | solution.py:136
  5.0 10.0 %all-to-all-start = ((bf16[8,2,11264]{2,1,0:T(2,128)(2,1)}), bf16[8,2,11264]{2,1,0:T(2,128)(2,1)S(1)}, u32[]{:S(2)}, u32[]{:S(2)}) async-start(bf16[8,2,11264]{2,1,0:T(2,128)(2,1)} %reshape.278), calls=%async_computation | async-start | bytes 720896 | tf_op jit(solution)/shard_map/all_to_all | solution.py:135
  15.4 13.9 %all-to-all-done = bf16[8,2,11264]{2,1,0:T(2,128)(2,1)S(1)} async-done(((bf16[8,2,11264]{2,1,0:T(2,128)(2,1)}), bf16[8,2,11264]{2,1,0:T(2,128)(2,1)S(1)}, u32[]{:S(2)}, u32[]{:S(2)}) %all-to-all-start) | async-done | bytes 360480 | tf_op jit(solution)/shard_map/all_to_all | solution.py:135
  29.4 0.4 reshape.280
  30.3 6.8 %collective-permute-start.1 = (bf16[128,264]{0,1:T(8,128)(2,1)S(1)}, bf16[128,264]{0,1:T(8,128)(2,1)S(1)}, u32[]{:S(2)}, u32[]{:S(2)}) collective-permute-start(bf16[128,264]{0,1:T(8,128)(2,1)S(1)} %bitcast.127), channel_id=1, source_target_pairs={{8,0},{16,8},{24,16},{32,24},{40,32},{48,40},{56,48},{64,56},{72,6... | collective-permute-start | bytes 202760 | tf_op jit(solution)/shard_map/ppermute | solution.py:10
  37.1 0.3 pad_maximum_fusion.1
  37.4 1.9 %collective-permute-start = (bf16[129,2,264]{2,1,0:T(2,128)(2,1)S(1)}, bf16[129,2,264]{2,1,0:T(2,128)(2,1)S(1)}, u32[]{:S(2)}, u32[]{:S(2)}) collective-permute-start(bf16[129,2,264]{2,1,0:T(2,128)(2,1)S(1)} %pad_maximum_fusion.1), channel_id=1, source_target_pairs={{0,8},{8,16},{16,24},{24,32},{32,40},{40,48},{48,56},{56,64},{64,7... | collective-permute-start | bytes 408680 | tf_op jit(solution)/shard_map/ppermute | solution.py:10
  39.3 1.9 %collective-permute-start.2 = (bf16[1,8,13952]{2,1,0:T(8,128)(2,1)S(1)}, bf16[1,8,13952]{2,1,0:T(8,128)(2,1)S(1)}, u32[]{:S(2)}, u32[]{:S(2)}) collective-permute-start(bf16[1,8,13952]{2,1,0:T(8,128)(2,1)S(1)} %get-tuple-element.14), channel_id=1, source_target_pairs={{0,16},{8,24},{16,0},{24,8},{32,48},{40,56},{48,32},{56,40},{64,80... | collective-permute-start | bytes 669704 | tf_op jit(solution)/shard_map/ppermute | solution.py:88
  41.6 4.9 %collective-permute-done = bf16[129,2,264]{2,1,0:T(2,128)(2,1)S(1)} collective-permute-done((bf16[129,2,264]{2,1,0:T(2,128)(2,1)S(1)}, bf16[129,2,264]{2,1,0:T(2,128)(2,1)S(1)}, u32[]{:S(2)}, u32[]{:S(2)}) %collective-permute-start) | collective-permute-done | bytes 136256 | tf_op jit(solution)/shard_map/ppermute | solution.py:10
  48.1 1.4 %maximum_bitcast_fusion.1 = (bf16[1,128,4,262]{3,2,1,0:T(4,128)(2,1)S(1)}, bf16[1,128,4,262]{3,2,1,0:T(4,128)(2,1)S(1)}) fusion(bf16[128,1,262]{2,1,0:T(2,128)(2,1)S(1)} %copy.248, bf16[128,2,262]{2,1,0:T(2,128)(2,1)S(1)} %slice.187, bf16[128,1,262]{2,1,0:T(2,128)(2,1)S(1)} %copy.247, bf16[128,1,262]{2,1,0:T(2,128)(2,1)S(1)} %copy.249, ...), kind=kLoop, calls=%fused_computation.24 | loop fusion | flops 1609728 | bytes 1006080 | tf_op jit(solution)/shard_map/stack | solution.py:164
  49.5 0.6 maximum_bitcast_fusion
  50.1 1.0 %copy.271 = bf16[128,4,2,262]{0,2,3,1:T(2,128)(2,1)S(1)} copy(bf16[128,4,2,262]{3,1,0,2:T(4,128)(2,1)S(1)} %maximum_bitcast_fusion) | data formatting | bytes 1073152
  51.1 0.4 pad.15.clone
  51.6 0.5 fusion.2
  52.2 2.1 %collective-permute-start.3 = (bf16[2,8,13952]{2,1,0:T(8,128)(2,1)S(1)}, bf16[2,8,13952]{2,1,0:T(8,128)(2,1)S(1)}, u32[]{:S(2)}, u32[]{:S(2)}) collective-permute-start(bf16[2,8,13952]{2,1,0:T(8,128)(2,1)S(1)} %maximum_select_fusion.2), channel_id=1, source_target_pairs={{0,8},{8,0},{16,24},{24,16},{32,40},{40,32},{48,56},{56,48},{64,72... | collective-permute-start | bytes 1339400 | tf_op jit(solution)/shard_map/ppermute | solution.py:88
  54.5 1.4 %collective-permute-done.3 = bf16[2,8,13952]{2,1,0:T(8,128)(2,1)S(1)} collective-permute-done((bf16[2,8,13952]{2,1,0:T(8,128)(2,1)S(1)}, bf16[2,8,13952]{2,1,0:T(8,128)(2,1)S(1)}, u32[]{:S(2)}, u32[]{:S(2)}) %collective-permute-start.3) | collective-permute-done | bytes 446496 | tf_op jit(solution)/shard_map/ppermute | solution.py:88
  56.9 0.9 %fusion.14 = bf16[2,16,33,128]{3,1,2,0:T(8,128)(2,1)S(1)} fusion(bf16[3,3,128,128]{3,2,1,0:T(8,128)(2,1)S(1)} %bitcast.139, bf16[128,4,2,8,35]{0,2,4,3,1:T(2,128)(2,1)S(1)} %fusion.2, f32[128]{0:T(128)S(1)} %add.176, pred[16,33]{0,1:T(8,128)(4,1)S(1)} %copy-done.5), kind=kOutput, calls=%fused_computation.19 | convolution fusion | flops 312913920 | bytes 1139728 | tf_op jit(solution)/shard_map/conv_general_dilated | solution.py:61
  59.7 0.3 copy-done.6
  60.0 0.4 fusion.33
  61.4 13.5 %all_to_all.10 = bf16[8,2,6144]{2,1,0:T(2,128)(2,1)S(1)} all-to-all(bf16[8,2,6144]{2,1,0:T(2,128)(2,1)S(1)} %copy.266), channel_id=1, replica_groups=mesh['space'=64,'chan'=8] {'chan'}, dimensions={0} | all-to-all | bytes 393216 | tf_op jit(solution)/shard_map/all_to_all | solution.py:184
  74.9 0.7 broadcast_in_dim_reshape.8
  75.6 0.7 broadcast_in_dim_reshape.9
  (96 shorter events, 8.2 us)
Async XLA Ops:
  0.6 2.9 %copy-start.1 = (bf16[32,3,3,128]{3,0,2,1:T(8,128)(2,1)S(1)}, bf16[32,3,3,128]{3,0,2,1:T(8,128)(2,1)}, u32[]{:S(2)}) copy-start(bf16[32,3,3,128]{3,0,2,1:T(8,128)(2,1)} %param.12) | copy-start | bytes 221188
  0.7 2.9 %copy-start.2 = (bf16[16,3,3,128]{3,0,2,1:T(8,128)(2,1)S(1)}, bf16[16,3,3,128]{3,0,2,1:T(8,128)(2,1)}, u32[]{:S(2)}) copy-start(bf16[16,3,3,128]{3,0,2,1:T(8,128)(2,1)} %param.10) | copy-start | bytes 110596
  3.9 11.1 %copy-start.4 = (s32[1,2048]{1,0:T(1,128)S(1)}, s32[1,2048]{1,0:T(1,128)}, u32[]{:S(2)}) copy-start(s32[1,2048]{1,0:T(1,128)} %param.9) | copy-start | bytes 24580
  4.0 11.2 %copy-start.3 = (s32[1,2048]{1,0:T(1,128)S(1)}, s32[1,2048]{1,0:T(1,128)}, u32[]{:S(2)}) copy-start(s32[1,2048]{1,0:T(1,128)} %param.8) | copy-start | bytes 24580
  5.0 24.3 %all-to-all-start = ((bf16[8,2,11264]{2,1,0:T(2,128)(2,1)}), bf16[8,2,11264]{2,1,0:T(2,128)(2,1)S(1)}, u32[]{:S(2)}, u32[]{:S(2)}) async-start(bf16[8,2,11264]{2,1,0:T(2,128)(2,1)} %reshape.278), calls=%async_computation | async-start | bytes 720896 | tf_op jit(solution)/shard_map/all_to_all | solution.py:135
  30.3 11.0 %collective-permute-start.1 = (bf16[128,264]{0,1:T(8,128)(2,1)S(1)}, bf16[128,264]{0,1:T(8,128)(2,1)S(1)}, u32[]{:S(2)}, u32[]{:S(2)}) collective-permute-start(bf16[128,264]{0,1:T(8,128)(2,1)S(1)} %bitcast.127), channel_id=1, source_target_pairs={{8,0},{16,8},{24,16},{32,24},{40,32},{48,40},{56,48},{64,56},{72,6... | collective-permute-start | bytes 202760 | tf_op jit(solution)/shard_map/ppermute | solution.py:10
  37.4 9.1 %collective-permute-start = (bf16[129,2,264]{2,1,0:T(2,128)(2,1)S(1)}, bf16[129,2,264]{2,1,0:T(2,128)(2,1)S(1)}, u32[]{:S(2)}, u32[]{:S(2)}) collective-permute-start(bf16[129,2,264]{2,1,0:T(2,128)(2,1)S(1)} %pad_maximum_fusion.1), channel_id=1, source_target_pairs={{0,8},{8,16},{16,24},{24,32},{32,40},{40,48},{48,56},{56,64},{64,7... | collective-permute-start | bytes 408680 | tf_op jit(solution)/shard_map/ppermute | solution.py:10
  39.3 12.7 %collective-permute-start.2 = (bf16[1,8,13952]{2,1,0:T(8,128)(2,1)S(1)}, bf16[1,8,13952]{2,1,0:T(8,128)(2,1)S(1)}, u32[]{:S(2)}, u32[]{:S(2)}) collective-permute-start(bf16[1,8,13952]{2,1,0:T(8,128)(2,1)S(1)} %get-tuple-element.14), channel_id=1, source_target_pairs={{0,16},{8,24},{16,0},{24,8},{32,48},{40,56},{48,32},{56,40},{64,80... | collective-permute-start | bytes 669704 | tf_op jit(solution)/shard_map/ppermute | solution.py:88
  52.2 3.7 %collective-permute-start.3 = (bf16[2,8,13952]{2,1,0:T(8,128)(2,1)S(1)}, bf16[2,8,13952]{2,1,0:T(8,128)(2,1)S(1)}, u32[]{:S(2)}, u32[]{:S(2)}) collective-permute-start(bf16[2,8,13952]{2,1,0:T(8,128)(2,1)S(1)} %maximum_select_fusion.2), channel_id=1, source_target_pairs={{0,8},{8,0},{16,24},{24,16},{32,40},{40,32},{48,56},{56,48},{64,72... | collective-permute-start | bytes 1339400 | tf_op jit(solution)/shard_map/ppermute | solution.py:88
  56.2 0.7 copy-start.5
  58.4 0.8 %copy-start = (bf16[128,2,260]{0,1,2:T(2,128)(2,1)}, bf16[128,2,260]{0,1,2:T(2,128)(2,1)S(1)}, u32[]{:S(2)}) copy-start(bf16[128,2,260]{0,1,2:T(2,128)(2,1)S(1)} %slice_bitcast_fusion.5) | copy-start | bytes 399364
  59.3 0.7 copy-start.6
  60.0 0.9 %slice-start = ((bf16[128,2,260]{0,1,2:T(2,128)(2,1)}), bf16[128,2,256]{0,1,2:T(2,128)(2,1)S(1)}, s32[]{:S(2)}) async-start(bf16[128,2,260]{0,1,2:T(2,128)(2,1)} %copy-done), calls=%async_computation.2 | async-start | bytes 262144 | tf_op jit(solution)/shard_map/slice | solution.py:182

commit v16 on v15

--- a/solution.py
+++ b/solution.py
@@ -126,7 +126,7 @@
         ]
     )
     w_len = packed_w.shape[0]
-    share = 4
+    share = 8
     quarter = -(-w_len // (share * 128)) * 128
     packed_w = jnp.pad(packed_w, (0, share * quarter - w_len))
     where_me = lax.axis_index("space") % share

time: 76.7 us -> 86.5 us (1.13)
  the two profiles are of different devices: /device:TPU:192 before, /device:TPU:64 now
where the time goes in v16:
time: 86.5 us; the launch traced here: 85.8 us
  starting transfers between devices  25.5 us (29%)
  waiting for transfers between devices  25.4 us (29%)
  blocking collectives  15.3 us (18%)
  local copies, waits for them, and re-layouts  10.9 us (13%)
  other arithmetic  6.01 us (7%)
  between operations  1.33 us (2%)
  matrix products  1.3 us (2%)
    all_to_all x1, blocking collectives, per_device(): lax.all_to_all(jnp.concatenate([hidden_part, coarse_part], 1).reshape(gro...  15.3 us
    all_to_all x1, waiting for transfers between devices, per_device(): lax.all_to_all(pad_to(sends, 256).reshape(groups, 2, -1), 'chan', 0, 0, t...  13.4 us
    ppermute x3, waiting for transfers between devices, gather_low_bits(): recv = lax.ppermute(acc, 'space', [(i, i ^ bit) for i in range(count)])  12 us
    all_to_all x1, starting transfers between devices, per_device(): lax.all_to_all(pad_to(sends, 256).reshape(groups, 2, -1), 'chan', 0, 0, t...  11.8 us
    ppermute x3, starting transfers between devices, gather_low_bits(): recv = lax.ppermute(acc, 'space', [(i, i ^ bit) for i in range(count)])  9.3 us
    ppermute x2, starting transfers between devices, shifted(): return lax.ppermute(array, axis, pairs)  4.33 us
    another operation x2, other arithmetic, per_device(): jnp.stack([jnp.concatenate([above[:, None], inner, below[:, None]], axis=...  2.03 us
  transfers between devices with their start and end apart: 6, of which 3 were waited for; matrix products, arithmetic and copies ran while one was open for 8% of the time, Pallas kernels for 0%

profile of v16, /device:TPU:64, one launch (start us, length us, event | category | flops | bytes accessed | tf_op | source)
XLA Modules:
  0.0 85.8 jit_solution(13266034865011537598)
XLA Ops:
  0.7 1.0 %reshape.338 = bf16[16,2,8,256]{3,2,1,0:T(8,128)(2,1)S(1)} reshape(bf16[1,16,2,2048]{3,2,1,0:T(2,128)(2,1)} %param.7) | data formatting | bytes 262144 | tf_op jit(solution)/shard_map/reshape;squeeze | solution.py:75
  1.9 0.8 reduce-precision_convert_fusion.1
  3.9 0.9 %copy.254 = bf16[8,2,7808]{2,1,0:T(2,128)(2,1)} copy(bf16[8,2,7808]{2,0,1:T(8,128)(2,1)S(1)} %bitcast.134) | data formatting | bytes 499712 | tf_op jit(solution)/shard_map/reshape | solution.py:136
  4.8 11.8 %all-to-all-start = ((bf16[8,2,7808]{2,1,0:T(2,128)(2,1)}), bf16[8,2,7808]{2,1,0:T(2,128)(2,1)S(1)}, u32[]{:S(2)}, u32[]{:S(2)}) async-start(bf16[8,2,7808]{2,1,0:T(2,128)(2,1)} %copy.254), calls=%async_computation | async-start | bytes 499712 | tf_op jit(solution)/shard_map/all_to_all | solution.py:135
  17.0 13.4 %all-to-all-done = bf16[8,2,7808]{2,1,0:T(2,128)(2,1)S(1)} async-done(((bf16[8,2,7808]{2,1,0:T(2,128)(2,1)}), bf16[8,2,7808]{2,1,0:T(2,128)(2,1)S(1)}, u32[]{:S(2)}, u32[]{:S(2)}) %all-to-all-start) | async-done | bytes 249888 | tf_op jit(solution)/shard_map/all_to_all | solution.py:135
  30.5 0.4 reshape.304
  31.4 1.9 %collective-permute-start.1 = (bf16[128,264]{0,1:T(8,128)(2,1)S(1)}, bf16[128,264]{0,1:T(8,128)(2,1)S(1)}, u32[]{:S(2)}, u32[]{:S(2)}) collective-permute-start(bf16[128,264]{0,1:T(8,128)(2,1)S(1)} %bitcast.130), channel_id=1, source_target_pairs={{8,0},{16,8},{24,16},{32,24},{40,32},{48,40},{56,48},{64,56},{72,6... | collective-permute-start | bytes 202760 | tf_op jit(solution)/shard_map/ppermute | solution.py:10
  33.6 2.4 %collective-permute-start = (bf16[129,2,264]{2,1,0:T(2,128)(2,1)S(1)}, bf16[129,2,264]{2,1,0:T(2,128)(2,1)S(1)}, u32[]{:S(2)}, u32[]{:S(2)}) collective-permute-start(bf16[129,2,264]{2,1,0:T(2,128)(2,1)S(1)} %pad_maximum_fusion.1), channel_id=1, source_target_pairs={{0,8},{8,16},{16,24},{24,32},{32,40},{40,48},{48,56},{56,64},{64,7... | collective-permute-start | bytes 408680 | tf_op jit(solution)/shard_map/ppermute | solution.py:10
  36.0 4.5 %collective-permute-start.2 = (bf16[1,8,7040]{2,1,0:T(8,128)(2,1)S(1)}, bf16[1,8,7040]{2,1,0:T(8,128)(2,1)S(1)}, u32[]{:S(2)}, u32[]{:S(2)}) collective-permute-start(bf16[1,8,7040]{2,1,0:T(8,128)(2,1)S(1)} %get-tuple-element.14), channel_id=1, source_target_pairs={{0,32},{8,40},{16,48},{24,56},{32,0},{40,8},{48,16},{56,24},{64,96... | collective-permute-start | bytes 337928 | tf_op jit(solution)/shard_map/ppermute | solution.py:88
  40.9 6.1 %collective-permute-done.2 = bf16[1,8,7040]{2,1,0:T(8,128)(2,1)S(1)} collective-permute-done((bf16[1,8,7040]{2,1,0:T(8,128)(2,1)S(1)}, bf16[1,8,7040]{2,1,0:T(8,128)(2,1)S(1)}, u32[]{:S(2)}, u32[]{:S(2)}) %collective-permute-start.2) | collective-permute-done | bytes 112672 | tf_op jit(solution)/shard_map/ppermute | solution.py:88
  47.0 2.7 %collective-permute-start.3 = (bf16[2,8,7040]{2,1,0:T(8,128)(2,1)S(1)}, bf16[2,8,7040]{2,1,0:T(8,128)(2,1)S(1)}, u32[]{:S(2)}, u32[]{:S(2)}) collective-permute-start(bf16[2,8,7040]{2,1,0:T(8,128)(2,1)S(1)} %maximum_select_fusion.3), channel_id=1, source_target_pairs={{0,16},{8,24},{16,0},{24,8},{32,48},{40,56},{48,32},{56,40},{64,80... | collective-permute-start | bytes 675848 | tf_op jit(solution)/shard_map/ppermute | solution.py:88
  50.5 6.0 %collective-permute-done.3 = bf16[2,8,7040]{2,1,0:T(8,128)(2,1)S(1)} collective-permute-done((bf16[2,8,7040]{2,1,0:T(8,128)(2,1)S(1)}, bf16[2,8,7040]{2,1,0:T(8,128)(2,1)S(1)}, u32[]{:S(2)}, u32[]{:S(2)}) %collective-permute-start.3) | collective-permute-done | bytes 225312 | tf_op jit(solution)/shard_map/ppermute | solution.py:88
  56.6 2.1 %collective-permute-start.4 = (bf16[4,8,7040]{2,1,0:T(8,128)(2,1)S(1)}, bf16[4,8,7040]{2,1,0:T(8,128)(2,1)S(1)}, u32[]{:S(2)}, u32[]{:S(2)}) collective-permute-start(bf16[4,8,7040]{2,1,0:T(8,128)(2,1)S(1)} %bitcast.125), channel_id=1, source_target_pairs={{0,8},{8,0},{16,24},{24,16},{32,40},{40,32},{48,56},{56,48},{64,72... | collective-permute-start | bytes 1351688 | tf_op jit(solution)/shard_map/ppermute | solution.py:88
  59.6 1.4 %maximum_bitcast_fusion.1 = (bf16[1,128,4,262]{3,2,1,0:T(4,128)(2,1)S(1)}, bf16[1,128,4,262]{3,2,1,0:T(4,128)(2,1)S(1)}) fusion(bf16[128,1,262]{2,1,0:T(2,128)(2,1)S(1)} %copy.258, bf16[128,2,262]{2,1,0:T(2,128)(2,1)S(1)} %slice.187, bf16[128,1,262]{2,1,0:T(2,128)(2,1)S(1)} %copy.257, bf16[128,1,262]{2,1,0:T(2,128)(2,1)S(1)} %copy.259, ...), kind=kLoop, calls=%fused_computation.23 | loop fusion | flops 1609728 | bytes 1006080 | tf_op jit(solution)/shard_map/stack | solution.py:164
  61.0 0.6 maximum_bitcast_fusion
  61.6 1.0 %copy.282 = bf16[128,4,2,262]{0,2,3,1:T(2,128)(2,1)S(1)} copy(bf16[128,4,2,262]{3,1,0,2:T(4,128)(2,1)S(1)} %maximum_bitcast_fusion) | data formatting | bytes 1073152
  62.6 0.4 pad.15.clone
  63.1 0.5 fusion.2
  64.6 0.9 %fusion.14 = bf16[2,16,33,128]{3,1,2,0:T(8,128)(2,1)S(1)} fusion(bf16[3,3,128,128]{3,2,1,0:T(8,128)(2,1)S(1)} %bitcast.146, bf16[128,4,2,8,35]{0,2,4,3,1:T(2,128)(2,1)S(1)} %fusion.2, f32[128]{0:T(128)S(1)} %add.176, pred[16,33]{0,1:T(8,128)(4,1)S(1)} %copy-done.5), kind=kOutput, calls=%fused_computation.19 | convolution fusion | flops 312913920 | bytes 1139728 | tf_op jit(solution)/shard_map/conv_general_dilated | solution.py:61
  67.3 0.3 copy-done.6
  67.7 0.4 fusion.33
  69.0 15.3 %all_to_all.10 = bf16[8,2,6144]{2,1,0:T(2,128)(2,1)S(1)} all-to-all(bf16[8,2,6144]{2,1,0:T(2,128)(2,1)S(1)} %copy.277), channel_id=1, replica_groups=mesh['space'=64,'chan'=8] {'chan'}, dimensions={0} | all-to-all | bytes 393216 | tf_op jit(solution)/shard_map/all_to_all | solution.py:184
  84.4 0.7 broadcast_in_dim_reshape.8
  85.1 0.7 broadcast_in_dim_reshape.9
  (100 shorter events, 8.3 us)
Async XLA Ops:
  0.6 2.9 %copy-start.1 = (bf16[32,3,3,128]{3,0,2,1:T(8,128)(2,1)S(1)}, bf16[32,3,3,128]{3,0,2,1:T(8,128)(2,1)}, u32[]{:S(2)}) copy-start(bf16[32,3,3,128]{3,0,2,1:T(8,128)(2,1)} %param.12) | copy-start | bytes 221188
  0.7 2.9 %copy-start.2 = (bf16[16,3,3,128]{3,0,2,1:T(8,128)(2,1)S(1)}, bf16[16,3,3,128]{3,0,2,1:T(8,128)(2,1)}, u32[]{:S(2)}) copy-start(bf16[16,3,3,128]{3,0,2,1:T(8,128)(2,1)} %param.10) | copy-start | bytes 110596
  3.8 12.8 %copy-start.4 = (s32[1,2048]{1,0:T(1,128)S(1)}, s32[1,2048]{1,0:T(1,128)}, u32[]{:S(2)}) copy-start(s32[1,2048]{1,0:T(1,128)} %param.9) | copy-start | bytes 24580
  3.8 13.0 %copy-start.3 = (s32[1,2048]{1,0:T(1,128)S(1)}, s32[1,2048]{1,0:T(1,128)}, u32[]{:S(2)}) copy-start(s32[1,2048]{1,0:T(1,128)} %param.8) | copy-start | bytes 24580
  4.8 25.6 %all-to-all-start = ((bf16[8,2,7808]{2,1,0:T(2,128)(2,1)}), bf16[8,2,7808]{2,1,0:T(2,128)(2,1)S(1)}, u32[]{:S(2)}, u32[]{:S(2)}) async-start(bf16[8,2,7808]{2,1,0:T(2,128)(2,1)} %copy.254), calls=%async_computation | async-start | bytes 499712 | tf_op jit(solution)/shard_map/all_to_all | solution.py:135
  31.4 9.2 %collective-permute-start.1 = (bf16[128,264]{0,1:T(8,128)(2,1)S(1)}, bf16[128,264]{0,1:T(8,128)(2,1)S(1)}, u32[]{:S(2)}, u32[]{:S(2)}) collective-permute-start(bf16[128,264]{0,1:T(8,128)(2,1)S(1)} %bitcast.130), channel_id=1, source_target_pairs={{8,0},{16,8},{24,16},{32,24},{40,32},{48,40},{56,48},{64,56},{72,6... | collective-permute-start | bytes 202760 | tf_op jit(solution)/shard_map/ppermute | solution.py:10
  33.6 16.2 %collective-permute-start = (bf16[129,2,264]{2,1,0:T(2,128)(2,1)S(1)}, bf16[129,2,264]{2,1,0:T(2,128)(2,1)S(1)}, u32[]{:S(2)}, u32[]{:S(2)}) collective-permute-start(bf16[129,2,264]{2,1,0:T(2,128)(2,1)S(1)} %pad_maximum_fusion.1), channel_id=1, source_target_pairs={{0,8},{8,16},{16,24},{24,32},{32,40},{40,48},{48,56},{56,64},{64,7... | collective-permute-start | bytes 408680 | tf_op jit(solution)/shard_map/ppermute | solution.py:10
  36.0 11.0 %collective-permute-start.2 = (bf16[1,8,7040]{2,1,0:T(8,128)(2,1)S(1)}, bf16[1,8,7040]{2,1,0:T(8,128)(2,1)S(1)}, u32[]{:S(2)}, u32[]{:S(2)}) collective-permute-start(bf16[1,8,7040]{2,1,0:T(8,128)(2,1)S(1)} %get-tuple-element.14), channel_id=1, source_target_pairs={{0,32},{8,40},{16,48},{24,56},{32,0},{40,8},{48,16},{56,24},{64,96... | collective-permute-start | bytes 337928 | tf_op jit(solution)/shard_map/ppermute | solution.py:88
  47.0 9.4 %collective-permute-start.3 = (bf16[2,8,7040]{2,1,0:T(8,128)(2,1)S(1)}, bf16[2,8,7040]{2,1,0:T(8,128)(2,1)S(1)}, u32[]{:S(2)}, u32[]{:S(2)}) collective-permute-start(bf16[2,8,7040]{2,1,0:T(8,128)(2,1)S(1)} %maximum_select_fusion.3), channel_id=1, source_target_pairs={{0,16},{8,24},{16,0},{24,8},{32,48},{40,56},{48,32},{56,40},{64,80... | collective-permute-start | bytes 675848 | tf_op jit(solution)/shard_map/ppermute | solution.py:88
  56.6 7.0 %collective-permute-start.4 = (bf16[4,8,7040]{2,1,0:T(8,128)(2,1)S(1)}, bf16[4,8,7040]{2,1,0:T(8,128)(2,1)S(1)}, u32[]{:S(2)}, u32[]{:S(2)}) collective-permute-start(bf16[4,8,7040]{2,1,0:T(8,128)(2,1)S(1)} %bitcast.125), channel_id=1, source_target_pairs={{0,8},{8,0},{16,24},{24,16},{32,40},{40,32},{48,56},{56,48},{64,72... | collective-permute-start | bytes 1351688 | tf_op jit(solution)/shard_map/ppermute | solution.py:88
  63.9 0.7 copy-start.5
  66.0 0.8 copy-start
  67.0 0.7 copy-start.6
  67.7 0.9 %slice-start = ((bf16[128,2,260]{0,1,2:T(2,128)(2,1)}), bf16[128,2,256]{0,1,2:T(2,128)(2,1)S(1)}, s32[]{:S(2)}) async-start(bf16[128,2,260]{0,1,2:T(2,128)(2,1)} %copy-done), calls=%async_computation.2 | async-start | bytes 262144 | tf_op jit(solution)/shard_map/slice | solution.py:182

commit v17 on v15

--- a/solution.py
+++ b/solution.py
@@ -116,36 +116,36 @@
     wins = column_windows(x, groups, halo + 1).reshape(groups, -1)
     feat_len = wins.shape[1]
 
-    w1_len = first_weight.size
-    w_total = w1_len + second_weight.size
-    packed_w = jnp.concatenate(
+    head = jnp.concatenate(
         [
             jnp.transpose(first_weight, (1, 2, 0, 3)).reshape(-1),
-            jnp.transpose(second_weight, (1, 2, 0, 3)).reshape(-1),
             split3(jnp.concatenate([first_bias, second_bias])).reshape(-1),
         ]
     )
-    w_len = packed_w.shape[0]
+    head = jnp.pad(head, (0, (-head.shape[0]) % 128))
+    tail = jnp.transpose(second_weight, (1, 2, 0, 3)).reshape(-1)
     share = 4
-    quarter = -(-w_len // (share * 128)) * 128
-    packed_w = jnp.pad(packed_w, (0, share * quarter - w_len))
+    quarter = -(-tail.shape[0] // (share * 128)) * 128
+    tail = jnp.pad(tail, (0, share * quarter - tail.shape[0]))
     where_me = lax.axis_index("space") % share
-    mine = lax.dynamic_slice_in_dim(packed_w, where_me * quarter, quarter)
-    sends = jnp.concatenate([wins, jnp.broadcast_to(mine[None], (groups, quarter))], 1)
+    mine = jnp.concatenate([head, lax.dynamic_slice_in_dim(tail, where_me * quarter, quarter)])
+    sends = jnp.concatenate([wins, jnp.broadcast_to(mine[None], (groups, mine.shape[0]))], 1)
     got = lax.all_to_all(
         pad_to(sends, 256).reshape(groups, 2, -1), "chan", 0, 0, tiled=True
     ).reshape(groups, -1)
 
     tile = got[:, :feat_len].reshape(groups * chans, rows, width + 2)
-    pieces = gather_low_bits(got[:, feat_len : feat_len + quarter], share)
-    every = jnp.moveaxis(pieces, 0, 1).reshape(groups, -1)
+    heads = got[:, feat_len : feat_len + head.shape[0]]
+    pieces = gather_low_bits(got[:, feat_len + head.shape[0] : feat_len + mine.shape[0]], share)
+    tails = jnp.moveaxis(pieces, 0, 1).reshape(groups, -1)
     k1 = first_weight.shape[1:3]
     k2 = second_weight.shape[1:3]
-    w1 = every[:, :w1_len].reshape((groups,) + k1 + (n1, first_weight.shape[3]))
+    w1_len = first_weight.size
+    w1 = heads[:, :w1_len].reshape((groups,) + k1 + (n1, first_weight.shape[3]))
     w1 = jnp.moveaxis(w1, 0, 2).reshape(k1 + (groups * n1, first_weight.shape[3]))
-    w2 = every[:, w1_len:w_total].reshape((groups,) + k2 + (n2, second_weight.shape[3]))
+    b_all = heads[:, w1_len : w1_len + (n1 + n2) * 3].reshape(groups, n1 + n2, 3)
+    w2 = tails[:, : second_weight.size].reshape((groups,) + k2 + (n2, second_weight.shape[3]))
     w2 = jnp.moveaxis(w2, 0, 2).reshape(k2 + (groups * n2, second_weight.shape[3]))
-    b_all = every[:, w_total:w_len].reshape(groups, n1 + n2, 3)
     b1 = join3(b_all[:, :n1]).reshape(-1)
     b2 = join3(b_all[:, n1:]).reshape(-1)
 

time: 76.7 us -> 82.6 us (1.077)
  the two profiles are of different devices: /device:TPU:192 before, /device:TPU:89 now
where the time goes in v17:
time: 82.6 us; the launch traced here: 82 us
  starting transfers between devices  23.6 us (29%)
  waiting for transfers between devices  23.6 us (29%)
  blocking collectives  14.4 us (17%)
  local copies, waits for them, and re-layouts  12.3 us (15%)
  other arithmetic  5.58 us (7%)
  matrix products  1.31 us (2%)
  between operations  1.27 us (2%)
    all_to_all x1, waiting for transfers between devices, per_device(): lax.all_to_all(pad_to(sends, 256).reshape(groups, 2, -1), 'chan', 0, 0, t...  19.5 us
    all_to_all x1, blocking collectives, per_device(): lax.all_to_all(jnp.concatenate([hidden_part, coarse_part], 1).reshape(gro...  14.4 us
    all_to_all x1, starting transfers between devices, per_device(): lax.all_to_all(pad_to(sends, 256).reshape(groups, 2, -1), 'chan', 0, 0, t...  11.7 us
    ppermute x2, starting transfers between devices, shifted(): return lax.ppermute(array, axis, pairs)  8.09 us
    ppermute x2, starting transfers between devices, gather_low_bits(): recv = lax.ppermute(acc, 'space', [(i, i ^ bit) for i in range(count)])  3.83 us
    ppermute x2, waiting for transfers between devices, shifted(): return lax.ppermute(array, axis, pairs)  2.56 us
    another operation x2, other arithmetic, per_device(): jnp.stack([jnp.concatenate([above[:, None], inner, below[:, None]], axis=...  2.03 us
    unnamed x15, local copies, waits for them, and re-layouts  1.92 us
  transfers between devices with their start and end apart: 5, of which 3 were waited for; matrix products, arithmetic and copies ran while one was open for 11% of the time, Pallas kernels for 0%

profile of v17, /device:TPU:89, one launch (start us, length us, event | category | flops | bytes accessed | tf_op | source)
XLA Modules:
  0.0 82.0 jit_solution(12180886130196125868)
XLA Ops:
  0.6 1.0 %reshape.306 = bf16[16,2,8,256]{3,2,1,0:T(8,128)(2,1)S(1)} reshape(bf16[1,16,2,2048]{3,2,1,0:T(2,128)(2,1)} %param.7) | data formatting | bytes 262144 | tf_op jit(solution)/shard_map/reshape;squeeze | solution.py:75
  1.9 0.8 reduce-precision_convert_fusion.1
  3.5 0.7 dynamic_slice.13
  4.4 1.0 %reshape.272 = bf16[8,2,18176]{2,1,0:T(2,128)(2,1)} reshape(bf16[8,36352]{1,0:T(8,128)(2,1)S(1)} %pad_maximum_fusion) | data formatting | bytes 1163264 | tf_op jit(solution)/shard_map/reshape | solution.py:134
  5.4 11.7 %all-to-all-start = ((bf16[8,2,18176]{2,1,0:T(2,128)(2,1)}), bf16[8,2,18176]{2,1,0:T(2,128)(2,1)S(1)}, u32[]{:S(2)}, u32[]{:S(2)}) async-start(bf16[8,2,18176]{2,1,0:T(2,128)(2,1)} %reshape.272), calls=%async_computation | async-start | bytes 1163264 | tf_op jit(solution)/shard_map/all_to_all | solution.py:133
  17.5 19.5 %all-to-all-done = bf16[8,2,18176]{2,1,0:T(2,128)(2,1)S(1)} async-done(((bf16[8,2,18176]{2,1,0:T(2,128)(2,1)}), bf16[8,2,18176]{2,1,0:T(2,128)(2,1)S(1)}, u32[]{:S(2)}, u32[]{:S(2)}) %all-to-all-start) | async-done | bytes 581664 | tf_op jit(solution)/shard_map/all_to_all | solution.py:133
  37.3 0.4 reshape.274
  38.4 6.2 %collective-permute-start = (bf16[129,2,264]{2,1,0:T(2,128)(2,1)S(1)}, bf16[129,2,264]{2,1,0:T(2,128)(2,1)S(1)}, u32[]{:S(2)}, u32[]{:S(2)}) collective-permute-start(bf16[129,2,264]{2,1,0:T(2,128)(2,1)S(1)} %pad_maximum_fusion.1), channel_id=1, source_target_pairs={{0,8},{8,16},{16,24},{24,32},{32,40},{40,48},{48,56},{56,64},{64,7... | collective-permute-start | bytes 408680 | tf_op jit(solution)/shard_map/ppermute | solution.py:10
  44.7 1.9 %collective-permute-start.1 = (bf16[128,264]{0,1:T(8,128)(2,1)S(1)}, bf16[128,264]{0,1:T(8,128)(2,1)S(1)}, u32[]{:S(2)}, u32[]{:S(2)}) collective-permute-start(bf16[128,264]{0,1:T(8,128)(2,1)S(1)} %bitcast.119), channel_id=1, source_target_pairs={{8,0},{16,8},{24,16},{32,24},{40,32},{48,40},{56,48},{64,56},{72,6... | collective-permute-start | bytes 202760 | tf_op jit(solution)/shard_map/ppermute | solution.py:10
  46.8 1.9 %collective-permute-start.2 = (bf16[1,8,9216]{2,1,0:T(8,128)(2,1)S(1)}, bf16[1,8,9216]{2,1,0:T(8,128)(2,1)S(1)}, u32[]{:S(2)}, u32[]{:S(2)}) collective-permute-start(bf16[1,8,9216]{2,1,0:T(8,128)(2,1)S(1)} %get-tuple-element.14), channel_id=1, source_target_pairs={{0,16},{8,24},{16,0},{24,8},{32,48},{40,56},{48,32},{56,40},{64,80... | collective-permute-start | bytes 442376 | tf_op jit(solution)/shard_map/ppermute | solution.py:88
  49.0 2.6 %collective-permute-done.1 = bf16[128,264]{0,1:T(8,128)(2,1)S(1)} collective-permute-done((bf16[128,264]{0,1:T(8,128)(2,1)S(1)}, bf16[128,264]{0,1:T(8,128)(2,1)S(1)}, u32[]{:S(2)}, u32[]{:S(2)}) %collective-permute-start.1) | collective-permute-done | bytes 67616 | tf_op jit(solution)/shard_map/ppermute | solution.py:10
  53.5 1.4 %maximum_bitcast_fusion.1 = (bf16[1,128,4,262]{3,2,1,0:T(4,128)(2,1)S(1)}, bf16[1,128,4,262]{3,2,1,0:T(4,128)(2,1)S(1)}) fusion(bf16[128,1,262]{2,1,0:T(2,128)(2,1)S(1)} %copy.255, bf16[128,2,262]{2,1,0:T(2,128)(2,1)S(1)} %slice.186, bf16[128,1,262]{2,1,0:T(2,128)(2,1)S(1)} %copy.254, bf16[128,1,262]{2,1,0:T(2,128)(2,1)S(1)} %copy.256, ...), kind=kLoop, calls=%fused_computation.22 | loop fusion | flops 1609728 | bytes 1006080 | tf_op jit(solution)/shard_map/stack | solution.py:164
  54.9 0.6 maximum_bitcast_fusion
  55.5 1.0 %copy.279 = bf16[128,4,2,262]{0,2,3,1:T(2,128)(2,1)S(1)} copy(bf16[128,4,2,262]{3,1,0,2:T(4,128)(2,1)S(1)} %maximum_bitcast_fusion) | data formatting | bytes 1073152
  56.5 0.4 pad.10.clone
  56.9 0.5 fusion.2
  57.6 0.9 %fusion.14 = bf16[2,16,33,128]{3,1,2,0:T(8,128)(2,1)S(1)} fusion(bf16[3,3,128,128]{3,2,1,0:T(8,128)(2,1)S(1)} %bitcast.130, bf16[128,4,2,8,35]{0,2,4,3,1:T(2,128)(2,1)S(1)} %fusion.2, f32[128]{0:T(128)S(1)} %add.174, pred[16,33]{0,1:T(8,128)(4,1)S(1)} %copy-done.3), kind=kOutput, calls=%fused_computation.19 | convolution fusion | flops 312913920 | bytes 1139728 | tf_op jit(solution)/shard_map/conv_general_dilated | solution.py:61
  60.4 1.9 %collective-permute-start.3 = (bf16[2,8,9216]{2,1,0:T(8,128)(2,1)S(1)}, bf16[2,8,9216]{2,1,0:T(8,128)(2,1)S(1)}, u32[]{:S(2)}, u32[]{:S(2)}) collective-permute-start(bf16[2,8,9216]{2,1,0:T(8,128)(2,1)S(1)} %maximum_select_fusion.2), channel_id=1, source_target_pairs={{0,8},{8,0},{16,24},{24,16},{32,40},{40,32},{48,56},{56,48},{64,72... | collective-permute-start | bytes 884744 | tf_op jit(solution)/shard_map/ppermute | solution.py:88
  62.4 1.5 %collective-permute-done.3 = bf16[2,8,9216]{2,1,0:T(8,128)(2,1)S(1)} collective-permute-done((bf16[2,8,9216]{2,1,0:T(8,128)(2,1)S(1)}, bf16[2,8,9216]{2,1,0:T(8,128)(2,1)S(1)}, u32[]{:S(2)}, u32[]{:S(2)}) %collective-permute-start.3) | collective-permute-done | bytes 294944 | tf_op jit(solution)/shard_map/ppermute | solution.py:88
  63.9 0.5 copy.269
  64.7 0.6 copy-done.4
  66.2 14.4 %all_to_all.10 = bf16[8,2,6144]{2,1,0:T(2,128)(2,1)S(1)} all-to-all(bf16[8,2,6144]{2,1,0:T(2,128)(2,1)S(1)} %copy.274), channel_id=1, replica_groups=mesh['space'=64,'chan'=8] {'chan'}, dimensions={0} | all-to-all | bytes 393216 | tf_op jit(solution)/shard_map/all_to_all | solution.py:184
  80.7 0.7 broadcast_in_dim_reshape.8
  81.4 0.7 broadcast_in_dim_reshape.9
  (92 shorter events, 8.1 us)
Async XLA Ops:
  1.6 2.6 %copy-start = (bf16[16,3,3,128]{3,0,2,1:T(8,128)(2,1)S(1)}, bf16[16,3,3,128]{3,0,2,1:T(8,128)(2,1)}, u32[]{:S(2)}) copy-start(bf16[16,3,3,128]{3,0,2,1:T(8,128)(2,1)} %param.10) | copy-start | bytes 110596
  5.4 11.7 %copy-start.2 = (s32[1,2048]{1,0:T(1,128)S(1)}, s32[1,2048]{1,0:T(1,128)}, u32[]{:S(2)}) copy-start(s32[1,2048]{1,0:T(1,128)} %param.9) | copy-start | bytes 24580
  5.4 11.9 %copy-start.1 = (s32[1,2048]{1,0:T(1,128)S(1)}, s32[1,2048]{1,0:T(1,128)}, u32[]{:S(2)}) copy-start(s32[1,2048]{1,0:T(1,128)} %param.8) | copy-start | bytes 24580
  5.4 31.6 %all-to-all-start = ((bf16[8,2,18176]{2,1,0:T(2,128)(2,1)}), bf16[8,2,18176]{2,1,0:T(2,128)(2,1)S(1)}, u32[]{:S(2)}, u32[]{:S(2)}) async-start(bf16[8,2,18176]{2,1,0:T(2,128)(2,1)} %reshape.272), calls=%async_computation | async-start | bytes 1163264 | tf_op jit(solution)/shard_map/all_to_all | solution.py:133
  38.4 13.5 %collective-permute-start = (bf16[129,2,264]{2,1,0:T(2,128)(2,1)S(1)}, bf16[129,2,264]{2,1,0:T(2,128)(2,1)S(1)}, u32[]{:S(2)}, u32[]{:S(2)}) collective-permute-start(bf16[129,2,264]{2,1,0:T(2,128)(2,1)S(1)} %pad_maximum_fusion.1), channel_id=1, source_target_pairs={{0,8},{8,16},{16,24},{24,32},{32,40},{40,48},{48,56},{56,64},{64,7... | collective-permute-start | bytes 408680 | tf_op jit(solution)/shard_map/ppermute | solution.py:10
  44.7 6.8 %collective-permute-start.1 = (bf16[128,264]{0,1:T(8,128)(2,1)S(1)}, bf16[128,264]{0,1:T(8,128)(2,1)S(1)}, u32[]{:S(2)}, u32[]{:S(2)}) collective-permute-start(bf16[128,264]{0,1:T(8,128)(2,1)S(1)} %bitcast.119), channel_id=1, source_target_pairs={{8,0},{16,8},{24,16},{32,24},{40,32},{48,40},{56,48},{64,56},{72,6... | collective-permute-start | bytes 202760 | tf_op jit(solution)/shard_map/ppermute | solution.py:10
  46.8 13.5 %collective-permute-start.2 = (bf16[1,8,9216]{2,1,0:T(8,128)(2,1)S(1)}, bf16[1,8,9216]{2,1,0:T(8,128)(2,1)S(1)}, u32[]{:S(2)}, u32[]{:S(2)}) collective-permute-start(bf16[1,8,9216]{2,1,0:T(8,128)(2,1)S(1)} %get-tuple-element.14), channel_id=1, source_target_pairs={{0,16},{8,24},{16,0},{24,8},{32,48},{40,56},{48,32},{56,40},{64,80... | collective-permute-start | bytes 442376 | tf_op jit(solution)/shard_map/ppermute | solution.py:88
  56.9 0.7 copy-start.3
  60.4 3.5 %collective-permute-start.3 = (bf16[2,8,9216]{2,1,0:T(8,128)(2,1)S(1)}, bf16[2,8,9216]{2,1,0:T(8,128)(2,1)S(1)}, u32[]{:S(2)}, u32[]{:S(2)}) collective-permute-start(bf16[2,8,9216]{2,1,0:T(8,128)(2,1)S(1)} %maximum_select_fusion.2), channel_id=1, source_target_pairs={{0,8},{8,0},{16,24},{24,16},{32,40},{40,32},{48,56},{56,48},{64,72... | collective-permute-start | bytes 884744 | tf_op jit(solution)/shard_map/ppermute | solution.py:88
  64.6 0.7 copy-start.4

commit v18 on v15

--- a/solution.py
+++ b/solution.py
@@ -161,19 +161,15 @@
     prior_below = apply_code(tile[:, 0, :], prior_code)
     inner = tile[:, :, 1 : width + 1]
     prior_inner = prior[:, :, 1 : width + 1]
-    window = jnp.stack(
-        [
-            jnp.concatenate([above[:, None], inner, below[:, None]], axis=1),
-            jnp.concatenate([prior_inner, prior_below[:, None], prior_below[:, None]], axis=1),
-        ],
-        0,
-    )
-
-    pre1 = conv(window, w1, (1, 1))
-    both = jax.nn.gelu(pre1 + b1[None, :, None, None]).astype(jnp.bfloat16)
-    hidden_win = both[0]
+    window = jnp.concatenate([above[:, None], inner, below[:, None]], axis=1)
+    prior_window = jnp.concatenate([prior_inner, prior_below[:, None]], axis=1)
+
+    pre1 = conv(window[None], w1, (1, 1))
+    hidden_win = jax.nn.gelu(pre1 + b1[None, :, None, None]).astype(jnp.bfloat16)[0]
+    pre_prior = conv(prior_window[None], w1, (1, 1))
+    prior_hidden = jax.nn.gelu(pre_prior + b1[None, :, None, None]).astype(jnp.bfloat16)[0, :, 0, :]
     has_prior = lax.axis_index("space") > 0
-    rim_src = jnp.where(has_prior, both[1, :, 0, :], jnp.zeros_like(both[1, :, 0, :]))
+    rim_src = jnp.where(has_prior, prior_hidden, jnp.zeros_like(prior_hidden))
     rim = remap_window(rim_src, upper_map, me * block - 1, block + 2)
     stacked = jnp.concatenate([rim[:, None], hidden_win[:, :, 1 : block + 3]], axis=1)
     pre2 = conv(stacked[None], w2, (1, 2))

time: 76.7 us -> 77.8 us (1.014)
  local copies, waits for them, and re-layouts: 11 us -> 15.4 us
  other arithmetic: 6.19 us -> 4.02 us
  waiting for transfers between devices: 20.2 us -> 19.1 us
    unnamed x20 -> x24, local copies, waits for them, and re-layouts: 1.74 us -> 5.25 us
    another operation x4 -> x2, other arithmetic: 2.79 us -> 0.08 us  [the longest x2 2.03 us: per_device(): jnp.stack([jnp.concatenate([above[:, None], inner, below[:, None]], axis=...]
    all_to_all x1, waiting for transfers between devices: 13.9 us -> 12.6 us  [per_device(): lax.all_to_all(pad_to(sends, 256).reshape(groups, 2, -1), 'chan', 0, 0, t...]
    broadcast_in_dim x3 -> x5, other arithmetic: 0.53 us -> 1.69 us  [the longest x1 0.72 us: per_device(): pre1 = conv(window[None], w1, (1, 1))]
  transfers between devices with their start and end apart: 5 -> 5, of which waited for: 3 -> 3; matrix products, arithmetic and copies ran while one was open for 9% -> 6% of each run, Pallas kernels for 0% -> 0%
where the time goes in v18:
time: 77.8 us; the launch traced here: 77.2 us
  starting transfers between devices  22.6 us (29%)
  waiting for transfers between devices  19.1 us (25%)
  local copies, waits for them, and re-layouts  15.4 us (20%)
  blocking collectives  13.5 us (17%)
  other arithmetic  4.02 us (5%)
  between operations  1.32 us (2%)
  matrix products  1.31 us (2%)
    all_to_all x1, blocking collectives, per_device(): lax.all_to_all(jnp.concatenate([hidden_part, coarse_part], 1).reshape(gro...  13.5 us
    all_to_all x1, waiting for transfers between devices, per_device(): lax.all_to_all(pad_to(sends, 256).reshape(groups, 2, -1), 'chan', 0, 0, t...  12.6 us
    all_to_all x1, starting transfers between devices, per_device(): lax.all_to_all(pad_to(sends, 256).reshape(groups, 2, -1), 'chan', 0, 0, t...  10 us
    ppermute x2, starting transfers between devices, shifted(): return lax.ppermute(array, axis, pairs)  8.71 us
    unnamed x24, local copies, waits for them, and re-layouts  5.25 us
    ppermute x2, waiting for transfers between devices, shifted(): return lax.ppermute(array, axis, pairs)  4.87 us
    ppermute x2, starting transfers between devices, gather_low_bits(): recv = lax.ppermute(acc, 'space', [(i, i ^ bit) for i in range(count)])  3.84 us
    ppermute x2, waiting for transfers between devices, gather_low_bits(): recv = lax.ppermute(acc, 'space', [(i, i ^ bit) for i in range(count)])  1.62 us
  transfers between devices with their start and end apart: 5, of which 3 were waited for; matrix products, arithmetic and copies ran while one was open for 6% of the time, Pallas kernels for 0%

profile of v18, /device:TPU:192, one launch (start us, length us, event | category | flops | bytes accessed | tf_op | source)
XLA Modules:
  0.0 77.2 jit_solution(49174034708968146)
XLA Ops:
  0.6 1.0 %reshape.332 = bf16[16,2,8,256]{3,2,1,0:T(8,128)(2,1)S(1)} reshape(bf16[1,16,2,2048]{3,2,1,0:T(2,128)(2,1)} %param.7) | data formatting | bytes 262144 | tf_op jit(solution)/shard_map/reshape;squeeze | solution.py:75
  1.9 0.6 copy-done.5
  3.6 0.6 copy-done.1
  4.5 1.0 %reshape.282 = bf16[8,2,11264]{2,1,0:T(2,128)(2,1)} reshape(bf16[8,22528]{1,0:T(8,128)(2,1)S(1)} %pad.13) | data formatting | bytes 720896 | tf_op jit(solution)/shard_map/reshape | solution.py:136
  5.5 10.0 %all-to-all-start = ((bf16[8,2,11264]{2,1,0:T(2,128)(2,1)}), bf16[8,2,11264]{2,1,0:T(2,128)(2,1)S(1)}, u32[]{:S(2)}, u32[]{:S(2)}) async-start(bf16[8,2,11264]{2,1,0:T(2,128)(2,1)} %reshape.282), calls=%async_computation | async-start | bytes 720896 | tf_op jit(solution)/shard_map/all_to_all | solution.py:135
  15.6 0.7 copy-done.3
  16.4 0.6 copy-done.4
  17.2 12.6 %all-to-all-done = bf16[8,2,11264]{2,1,0:T(2,128)(2,1)S(1)} async-done(((bf16[8,2,11264]{2,1,0:T(2,128)(2,1)}), bf16[8,2,11264]{2,1,0:T(2,128)(2,1)S(1)}, u32[]{:S(2)}, u32[]{:S(2)}) %all-to-all-start) | async-done | bytes 360480 | tf_op jit(solution)/shard_map/all_to_all | solution.py:135
  30.8 6.8 %collective-permute-start.1 = (bf16[128,264]{0,1:T(8,128)(2,1)S(1)}, bf16[128,264]{0,1:T(8,128)(2,1)S(1)}, u32[]{:S(2)}, u32[]{:S(2)}) collective-permute-start(bf16[128,264]{0,1:T(8,128)(2,1)S(1)} %bitcast.138), channel_id=1, source_target_pairs={{8,0},{16,8},{24,16},{32,24},{40,32},{48,40},{56,48},{64,56},{72,6... | collective-permute-start | bytes 202760 | tf_op jit(solution)/shard_map/ppermute | solution.py:10
  37.9 1.9 %collective-permute-start = (bf16[129,2,264]{2,1,0:T(2,128)(2,1)S(1)}, bf16[129,2,264]{2,1,0:T(2,128)(2,1)S(1)}, u32[]{:S(2)}, u32[]{:S(2)}) collective-permute-start(bf16[129,2,264]{2,1,0:T(2,128)(2,1)S(1)} %pad_maximum_fusion.1), channel_id=1, source_target_pairs={{0,8},{8,16},{16,24},{24,32},{32,40},{40,48},{48,56},{56,64},{64,7... | collective-permute-start | bytes 408680 | tf_op jit(solution)/shard_map/ppermute | solution.py:10
  39.8 1.9 %collective-permute-start.2 = (bf16[1,8,13952]{2,1,0:T(8,128)(2,1)S(1)}, bf16[1,8,13952]{2,1,0:T(8,128)(2,1)S(1)}, u32[]{:S(2)}, u32[]{:S(2)}) collective-permute-start(bf16[1,8,13952]{2,1,0:T(8,128)(2,1)S(1)} %get-tuple-element.14), channel_id=1, source_target_pairs={{0,16},{8,24},{16,0},{24,8},{32,48},{40,56},{48,32},{56,40},{64,80... | collective-permute-start | bytes 669704 | tf_op jit(solution)/shard_map/ppermute | solution.py:88
  42.2 4.9 %collective-permute-done = bf16[129,2,264]{2,1,0:T(2,128)(2,1)S(1)} collective-permute-done((bf16[129,2,264]{2,1,0:T(2,128)(2,1)S(1)}, bf16[129,2,264]{2,1,0:T(2,128)(2,1)S(1)}, u32[]{:S(2)}, u32[]{:S(2)}) %collective-permute-start) | collective-permute-done | bytes 136256 | tf_op jit(solution)/shard_map/ppermute | solution.py:10
  49.5 0.7 maximum_bitcast_fusion
  50.8 1.9 %collective-permute-start.3 = (bf16[2,8,13952]{2,1,0:T(8,128)(2,1)S(1)}, bf16[2,8,13952]{2,1,0:T(8,128)(2,1)S(1)}, u32[]{:S(2)}, u32[]{:S(2)}) collective-permute-start(bf16[2,8,13952]{2,1,0:T(8,128)(2,1)S(1)} %maximum_select_fusion.2), channel_id=1, source_target_pairs={{0,8},{8,0},{16,24},{24,16},{32,40},{40,32},{48,56},{56,48},{64,72... | collective-permute-start | bytes 1339400 | tf_op jit(solution)/shard_map/ppermute | solution.py:88
  52.9 1.6 %collective-permute-done.3 = bf16[2,8,13952]{2,1,0:T(8,128)(2,1)S(1)} collective-permute-done((bf16[2,8,13952]{2,1,0:T(8,128)(2,1)S(1)}, bf16[2,8,13952]{2,1,0:T(8,128)(2,1)S(1)}, u32[]{:S(2)}, u32[]{:S(2)}) %collective-permute-start.3) | collective-permute-done | bytes 446496 | tf_op jit(solution)/shard_map/ppermute | solution.py:88
  55.3 0.6 copy-done.7
  55.9 0.6 fusion.21
  56.7 0.6 copy-done
  58.4 0.8 %slice-done = bf16[128,2,256]{0,1,2:T(2,128)(2,1)S(1)} async-done(((bf16[128,2,260]{0,1,2:T(2,128)(2,1)}), bf16[128,2,256]{0,1,2:T(2,128)(2,1)S(1)}, s32[]{:S(2)}) %slice-start) | async-done | bytes 131096 | tf_op jit(solution)/shard_map/slice | solution.py:178
  59.5 0.8 %slice-done.1 = bf16[128,2,258]{0,1,2:T(2,128)(2,1)S(1)} async-done(((bf16[128,2,260]{0,1,2:T(2,128)(2,1)}), bf16[128,2,258]{0,1,2:T(2,128)(2,1)S(1)}, s32[]{:S(2)}) %slice-start.1) | async-done | bytes 132120 | tf_op jit(solution)/shard_map/slice | solution.py:174
  60.7 0.7 copy-done.8
  62.3 13.5 %all_to_all.10 = bf16[8,2,6144]{2,1,0:T(2,128)(2,1)S(1)} all-to-all(bf16[8,2,6144]{2,1,0:T(2,128)(2,1)S(1)} %copy.299), channel_id=1, replica_groups=mesh['space'=64,'chan'=8] {'chan'}, dimensions={0} | all-to-all | bytes 393216 | tf_op jit(solution)/shard_map/all_to_all | solution.py:180
  75.8 0.7 broadcast_in_dim_reshape.4
  76.5 0.7 broadcast_in_dim_reshape.10
  (107 shorter events, 10.0 us)
Async XLA Ops:
  1.8 0.7 copy-start.5
  1.9 0.7 copy-start.6
  3.3 0.9 %copy-start.1 = (bf16[32,3,3,128]{3,0,2,1:T(8,128)(2,1)S(1)}, bf16[32,3,3,128]{3,0,2,1:T(8,128)(2,1)}, u32[]{:S(2)}) copy-start(bf16[32,3,3,128]{3,0,2,1:T(8,128)(2,1)} %param.12) | copy-start | bytes 221188
  3.3 0.9 %copy-start.2 = (bf16[16,3,3,128]{3,0,2,1:T(8,128)(2,1)S(1)}, bf16[16,3,3,128]{3,0,2,1:T(8,128)(2,1)}, u32[]{:S(2)}) copy-start(bf16[16,3,3,128]{3,0,2,1:T(8,128)(2,1)} %param.10) | copy-start | bytes 110596
  5.5 24.3 %all-to-all-start = ((bf16[8,2,11264]{2,1,0:T(2,128)(2,1)}), bf16[8,2,11264]{2,1,0:T(2,128)(2,1)S(1)}, u32[]{:S(2)}, u32[]{:S(2)}) async-start(bf16[8,2,11264]{2,1,0:T(2,128)(2,1)} %reshape.282), calls=%async_computation | async-start | bytes 720896 | tf_op jit(solution)/shard_map/all_to_all | solution.py:135
  15.5 0.7 copy-start.3
  16.3 0.7 copy-start.4
  30.8 11.0 %collective-permute-start.1 = (bf16[128,264]{0,1:T(8,128)(2,1)S(1)}, bf16[128,264]{0,1:T(8,128)(2,1)S(1)}, u32[]{:S(2)}, u32[]{:S(2)}) collective-permute-start(bf16[128,264]{0,1:T(8,128)(2,1)S(1)} %bitcast.138), channel_id=1, source_target_pairs={{8,0},{16,8},{24,16},{32,24},{40,32},{48,40},{56,48},{64,56},{72,6... | collective-permute-start | bytes 202760 | tf_op jit(solution)/shard_map/ppermute | solution.py:10
  37.9 9.1 %collective-permute-start = (bf16[129,2,264]{2,1,0:T(2,128)(2,1)S(1)}, bf16[129,2,264]{2,1,0:T(2,128)(2,1)S(1)}, u32[]{:S(2)}, u32[]{:S(2)}) collective-permute-start(bf16[129,2,264]{2,1,0:T(2,128)(2,1)S(1)} %pad_maximum_fusion.1), channel_id=1, source_target_pairs={{0,8},{8,16},{16,24},{24,32},{32,40},{40,48},{48,56},{56,64},{64,7... | collective-permute-start | bytes 408680 | tf_op jit(solution)/shard_map/ppermute | solution.py:10
  39.8 10.8 %collective-permute-start.2 = (bf16[1,8,13952]{2,1,0:T(8,128)(2,1)S(1)}, bf16[1,8,13952]{2,1,0:T(8,128)(2,1)S(1)}, u32[]{:S(2)}, u32[]{:S(2)}) collective-permute-start(bf16[1,8,13952]{2,1,0:T(8,128)(2,1)S(1)} %get-tuple-element.14), channel_id=1, source_target_pairs={{0,16},{8,24},{16,0},{24,8},{32,48},{40,56},{48,32},{56,40},{64,80... | collective-permute-start | bytes 669704 | tf_op jit(solution)/shard_map/ppermute | solution.py:88
  50.8 3.7 %collective-permute-start.3 = (bf16[2,8,13952]{2,1,0:T(8,128)(2,1)S(1)}, bf16[2,8,13952]{2,1,0:T(8,128)(2,1)S(1)}, u32[]{:S(2)}, u32[]{:S(2)}) collective-permute-start(bf16[2,8,13952]{2,1,0:T(8,128)(2,1)S(1)} %maximum_select_fusion.2), channel_id=1, source_target_pairs={{0,8},{8,0},{16,24},{24,16},{32,40},{40,32},{48,56},{56,48},{64,72... | collective-permute-start | bytes 1339400 | tf_op jit(solution)/shard_map/ppermute | solution.py:88
  55.3 0.7 copy-start.7
  56.7 0.7 copy-start
  58.3 0.9 %slice-start = ((bf16[128,2,260]{0,1,2:T(2,128)(2,1)}), bf16[128,2,256]{0,1,2:T(2,128)(2,1)S(1)}, s32[]{:S(2)}) async-start(bf16[128,2,260]{0,1,2:T(2,128)(2,1)} %copy-done), calls=%async_computation.2 | async-start | bytes 262144 | tf_op jit(solution)/shard_map/slice | solution.py:178
  59.4 0.9 %slice-start.1 = ((bf16[128,2,260]{0,1,2:T(2,128)(2,1)}), bf16[128,2,258]{0,1,2:T(2,128)(2,1)S(1)}, s32[]{:S(2)}) async-start(bf16[128,2,260]{0,1,2:T(2,128)(2,1)} %copy-done), calls=%async_computation.3 | async-start | bytes 264192 | tf_op jit(solution)/shard_map/slice | solution.py:174
  60.7 0.7 copy-start.8

commit v19 on v15

--- a/solution.py
+++ b/solution.py
@@ -83,13 +83,13 @@
     count = lax.axis_size("space")
     me = lax.axis_index("space")
     acc = part[None]
-    bit = share // 2
-    while bit >= 1:
+    bit = 1
+    while bit < share:
         recv = lax.ppermute(acc, "space", [(i, i ^ bit) for i in range(count)])
         low = (me & bit) == 0
-        pair = jnp.where(low, jnp.stack([acc, recv], 1), jnp.stack([recv, acc], 1))
+        pair = jnp.where(low, jnp.stack([acc, recv], 0), jnp.stack([recv, acc], 0))
         acc = pair.reshape((-1,) + part.shape)
-        bit //= 2
+        bit *= 2
     return acc
 
 

time: 76.7 us -> 84.8 us (1.11)
  the two profiles are of different devices: /device:TPU:192 before, /device:TPU:88 now
where the time goes in v19:
time: 84.8 us; the launch traced here: 84.4 us
  waiting for transfers between devices  26.8 us (32%)
  starting transfers between devices  22.9 us (27%)
  blocking collectives  14.9 us (18%)
  local copies, waits for them, and re-layouts  11 us (13%)
  other arithmetic  6.09 us (7%)
  between operations  1.32 us (2%)
  matrix products  1.31 us (2%)
    all_to_all x1, waiting for transfers between devices, per_device(): lax.all_to_all(pad_to(sends, 256).reshape(groups, 2, -1), 'chan', 0, 0, t...  15 us
    all_to_all x1, blocking collectives, per_device(): lax.all_to_all(jnp.concatenate([hidden_part, coarse_part], 1).reshape(gro...  14.9 us
    all_to_all x1, starting transfers between devices, per_device(): lax.all_to_all(pad_to(sends, 256).reshape(groups, 2, -1), 'chan', 0, 0, t...  11.8 us
    ppermute x2, waiting for transfers between devices, gather_low_bits(): recv = lax.ppermute(acc, 'space', [(i, i ^ bit) for i in range(count)])  11.8 us
    ppermute x2, starting transfers between devices, gather_low_bits(): recv = lax.ppermute(acc, 'space', [(i, i ^ bit) for i in range(count)])  6.72 us
    ppermute x2, starting transfers between devices, shifted(): return lax.ppermute(array, axis, pairs)  4.33 us
    another operation x2, other arithmetic, per_device(): jnp.stack([jnp.concatenate([above[:, None], inner, below[:, None]], axis=...  2.03 us
    unnamed x20, local copies, waits for them, and re-layouts  1.74 us
  transfers between devices with their start and end apart: 5, of which 2 were waited for; matrix products, arithmetic and copies ran while one was open for 8% of the time, Pallas kernels for 0%

profile of v19, /device:TPU:88, one launch (start us, length us, event | category | flops | bytes accessed | tf_op | source)
XLA Modules:
  0.0 84.4 jit_solution(7325314123016030162)
XLA Ops:
  0.7 1.0 %reshape.314 = bf16[16,2,8,256]{3,2,1,0:T(8,128)(2,1)S(1)} reshape(bf16[1,16,2,2048]{3,2,1,0:T(2,128)(2,1)} %param.7) | data formatting | bytes 262144 | tf_op jit(solution)/shard_map/reshape;squeeze | solution.py:75
  1.9 0.8 reduce-precision_convert_fusion.1
  4.0 1.0 %reshape.278 = bf16[8,2,11264]{2,1,0:T(2,128)(2,1)} reshape(bf16[8,22528]{1,0:T(8,128)(2,1)S(1)} %pad.13) | data formatting | bytes 720896 | tf_op jit(solution)/shard_map/reshape | solution.py:136
  5.0 11.8 %all-to-all-start = ((bf16[8,2,11264]{2,1,0:T(2,128)(2,1)}), bf16[8,2,11264]{2,1,0:T(2,128)(2,1)S(1)}, u32[]{:S(2)}, u32[]{:S(2)}) async-start(bf16[8,2,11264]{2,1,0:T(2,128)(2,1)} %reshape.278), calls=%async_computation | async-start | bytes 720896 | tf_op jit(solution)/shard_map/all_to_all | solution.py:135
  17.2 15.0 %all-to-all-done = bf16[8,2,11264]{2,1,0:T(2,128)(2,1)S(1)} async-done(((bf16[8,2,11264]{2,1,0:T(2,128)(2,1)}), bf16[8,2,11264]{2,1,0:T(2,128)(2,1)S(1)}, u32[]{:S(2)}, u32[]{:S(2)}) %all-to-all-start) | async-done | bytes 360480 | tf_op jit(solution)/shard_map/all_to_all | solution.py:135
  32.4 0.4 reshape.280
  33.2 1.9 %collective-permute-start.1 = (bf16[128,264]{0,1:T(8,128)(2,1)S(1)}, bf16[128,264]{0,1:T(8,128)(2,1)S(1)}, u32[]{:S(2)}, u32[]{:S(2)}) collective-permute-start(bf16[128,264]{0,1:T(8,128)(2,1)S(1)} %bitcast.127), channel_id=1, source_target_pairs={{8,0},{16,8},{24,16},{32,24},{40,32},{48,40},{56,48},{64,56},{72,6... | collective-permute-start | bytes 202760 | tf_op jit(solution)/shard_map/ppermute | solution.py:10
  35.2 0.3 pad_maximum_fusion.1
  35.5 2.4 %collective-permute-start = (bf16[129,2,264]{2,1,0:T(2,128)(2,1)S(1)}, bf16[129,2,264]{2,1,0:T(2,128)(2,1)S(1)}, u32[]{:S(2)}, u32[]{:S(2)}) collective-permute-start(bf16[129,2,264]{2,1,0:T(2,128)(2,1)S(1)} %pad_maximum_fusion.1), channel_id=1, source_target_pairs={{0,8},{8,16},{16,24},{24,32},{32,40},{40,48},{48,56},{56,64},{64,7... | collective-permute-start | bytes 408680 | tf_op jit(solution)/shard_map/ppermute | solution.py:10
  37.9 4.3 %collective-permute-start.2 = (bf16[1,8,13952]{2,1,0:T(8,128)(2,1)S(1)}, bf16[1,8,13952]{2,1,0:T(8,128)(2,1)S(1)}, u32[]{:S(2)}, u32[]{:S(2)}) collective-permute-start(bf16[1,8,13952]{2,1,0:T(8,128)(2,1)S(1)} %get-tuple-element.14), channel_id=1, source_target_pairs={{0,8},{8,0},{16,24},{24,16},{32,40},{40,32},{48,56},{56,48},{64,72... | collective-permute-start | bytes 669704 | tf_op jit(solution)/shard_map/ppermute | solution.py:88
  43.9 0.3 slice.192
  44.2 1.4 %maximum_bitcast_fusion.1 = (bf16[1,128,4,262]{3,2,1,0:T(4,128)(2,1)S(1)}, bf16[1,128,4,262]{3,2,1,0:T(4,128)(2,1)S(1)}) fusion(bf16[128,1,262]{2,1,0:T(2,128)(2,1)S(1)} %copy.248, bf16[128,2,262]{2,1,0:T(2,128)(2,1)S(1)} %slice.187, bf16[128,1,262]{2,1,0:T(2,128)(2,1)S(1)} %copy.247, bf16[128,1,262]{2,1,0:T(2,128)(2,1)S(1)} %copy.249, ...), kind=kLoop, calls=%fused_computation.24 | loop fusion | flops 1609728 | bytes 1006080 | tf_op jit(solution)/shard_map/stack | solution.py:164
  45.6 0.6 maximum_bitcast_fusion
  46.2 1.0 %copy.271 = bf16[128,4,2,262]{0,2,3,1:T(2,128)(2,1)S(1)} copy(bf16[128,4,2,262]{3,1,0,2:T(4,128)(2,1)S(1)} %maximum_bitcast_fusion) | data formatting | bytes 1073152
  47.2 0.4 pad.15.clone
  47.6 0.5 fusion.2
  48.3 2.4 %collective-permute-start.3 = (bf16[2,8,13952]{2,1,0:T(8,128)(2,1)S(1)}, bf16[2,8,13952]{2,1,0:T(8,128)(2,1)S(1)}, u32[]{:S(2)}, u32[]{:S(2)}) collective-permute-start(bf16[2,8,13952]{2,1,0:T(8,128)(2,1)S(1)} %maximum_select_fusion.2), channel_id=1, source_target_pairs={{0,16},{8,24},{16,0},{24,8},{32,48},{40,56},{48,32},{56,40},{64,80... | collective-permute-start | bytes 1339400 | tf_op jit(solution)/shard_map/ppermute | solution.py:88
  50.9 11.8 %collective-permute-done.3 = bf16[2,8,13952]{2,1,0:T(8,128)(2,1)S(1)} collective-permute-done((bf16[2,8,13952]{2,1,0:T(8,128)(2,1)S(1)}, bf16[2,8,13952]{2,1,0:T(8,128)(2,1)S(1)}, u32[]{:S(2)}, u32[]{:S(2)}) %collective-permute-start.3) | collective-permute-done | bytes 446496 | tf_op jit(solution)/shard_map/ppermute | solution.py:88
  63.6 0.9 %fusion.14 = bf16[2,16,33,128]{3,1,2,0:T(8,128)(2,1)S(1)} fusion(bf16[3,3,128,128]{3,2,1,0:T(8,128)(2,1)S(1)} %bitcast.139, bf16[128,4,2,8,35]{0,2,4,3,1:T(2,128)(2,1)S(1)} %fusion.2, f32[128]{0:T(128)S(1)} %add.176, pred[16,33]{0,1:T(8,128)(4,1)S(1)} %copy-done.5), kind=kOutput, calls=%fused_computation.19 | convolution fusion | flops 312913920 | bytes 1139728 | tf_op jit(solution)/shard_map/conv_general_dilated | solution.py:61
  66.3 0.3 copy-done.6
  66.6 0.4 fusion.33
  68.0 14.9 %all_to_all.10 = bf16[8,2,6144]{2,1,0:T(2,128)(2,1)S(1)} all-to-all(bf16[8,2,6144]{2,1,0:T(2,128)(2,1)S(1)} %copy.266), channel_id=1, replica_groups=mesh['space'=64,'chan'=8] {'chan'}, dimensions={0} | all-to-all | bytes 393216 | tf_op jit(solution)/shard_map/all_to_all | solution.py:184
  83.1 0.7 broadcast_in_dim_reshape.8
  83.7 0.7 broadcast_in_dim_reshape.9
  (96 shorter events, 7.8 us)
Async XLA Ops:
  0.6 2.9 %copy-start.1 = (bf16[32,3,3,128]{3,0,2,1:T(8,128)(2,1)S(1)}, bf16[32,3,3,128]{3,0,2,1:T(8,128)(2,1)}, u32[]{:S(2)}) copy-start(bf16[32,3,3,128]{3,0,2,1:T(8,128)(2,1)} %param.12) | copy-start | bytes 221188
  0.7 2.9 %copy-start.2 = (bf16[16,3,3,128]{3,0,2,1:T(8,128)(2,1)S(1)}, bf16[16,3,3,128]{3,0,2,1:T(8,128)(2,1)}, u32[]{:S(2)}) copy-start(bf16[16,3,3,128]{3,0,2,1:T(8,128)(2,1)} %param.10) | copy-start | bytes 110596
  3.9 12.9 %copy-start.4 = (s32[1,2048]{1,0:T(1,128)S(1)}, s32[1,2048]{1,0:T(1,128)}, u32[]{:S(2)}) copy-start(s32[1,2048]{1,0:T(1,128)} %param.9) | copy-start | bytes 24580
  4.0 13.0 %copy-start.3 = (s32[1,2048]{1,0:T(1,128)S(1)}, s32[1,2048]{1,0:T(1,128)}, u32[]{:S(2)}) copy-start(s32[1,2048]{1,0:T(1,128)} %param.8) | copy-start | bytes 24580
  5.0 27.3 %all-to-all-start = ((bf16[8,2,11264]{2,1,0:T(2,128)(2,1)}), bf16[8,2,11264]{2,1,0:T(2,128)(2,1)S(1)}, u32[]{:S(2)}, u32[]{:S(2)}) async-start(bf16[8,2,11264]{2,1,0:T(2,128)(2,1)} %reshape.278), calls=%async_computation | async-start | bytes 720896 | tf_op jit(solution)/shard_map/all_to_all | solution.py:135
  33.2 9.0 %collective-permute-start.1 = (bf16[128,264]{0,1:T(8,128)(2,1)S(1)}, bf16[128,264]{0,1:T(8,128)(2,1)S(1)}, u32[]{:S(2)}, u32[]{:S(2)}) collective-permute-start(bf16[128,264]{0,1:T(8,128)(2,1)S(1)} %bitcast.127), channel_id=1, source_target_pairs={{8,0},{16,8},{24,16},{32,24},{40,32},{48,40},{56,48},{64,56},{72,6... | collective-permute-start | bytes 202760 | tf_op jit(solution)/shard_map/ppermute | solution.py:10
  35.5 7.1 %collective-permute-start = (bf16[129,2,264]{2,1,0:T(2,128)(2,1)S(1)}, bf16[129,2,264]{2,1,0:T(2,128)(2,1)S(1)}, u32[]{:S(2)}, u32[]{:S(2)}) collective-permute-start(bf16[129,2,264]{2,1,0:T(2,128)(2,1)S(1)} %pad_maximum_fusion.1), channel_id=1, source_target_pairs={{0,8},{8,16},{16,24},{24,32},{32,40},{40,48},{48,56},{56,64},{64,7... | collective-permute-start | bytes 408680 | tf_op jit(solution)/shard_map/ppermute | solution.py:10
  37.9 10.3 %collective-permute-start.2 = (bf16[1,8,13952]{2,1,0:T(8,128)(2,1)S(1)}, bf16[1,8,13952]{2,1,0:T(8,128)(2,1)S(1)}, u32[]{:S(2)}, u32[]{:S(2)}) collective-permute-start(bf16[1,8,13952]{2,1,0:T(8,128)(2,1)S(1)} %get-tuple-element.14), channel_id=1, source_target_pairs={{0,8},{8,0},{16,24},{24,16},{32,40},{40,32},{48,56},{56,48},{64,72... | collective-permute-start | bytes 669704 | tf_op jit(solution)/shard_map/ppermute | solution.py:88
  48.3 14.3 %collective-permute-start.3 = (bf16[2,8,13952]{2,1,0:T(8,128)(2,1)S(1)}, bf16[2,8,13952]{2,1,0:T(8,128)(2,1)S(1)}, u32[]{:S(2)}, u32[]{:S(2)}) collective-permute-start(bf16[2,8,13952]{2,1,0:T(8,128)(2,1)S(1)} %maximum_select_fusion.2), channel_id=1, source_target_pairs={{0,16},{8,24},{16,0},{24,8},{32,48},{40,56},{48,32},{56,40},{64,80... | collective-permute-start | bytes 1339400 | tf_op jit(solution)/shard_map/ppermute | solution.py:88
  62.9 0.7 copy-start.5
  65.0 0.8 copy-start
  66.0 0.7 copy-start.6
  66.6 0.9 %slice-start = ((bf16[128,2,260]{0,1,2:T(2,128)(2,1)}), bf16[128,2,256]{0,1,2:T(2,128)(2,1)S(1)}, s32[]{:S(2)}) async-start(bf16[128,2,260]{0,1,2:T(2,128)(2,1)} %copy-done), calls=%async_computation.2 | async-start | bytes 262144 | tf_op jit(solution)/shard_map/slice | solution.py:182
